TPU v7x, 512 devices: a whole 4x8x8 slice. The times are simulated.
512 devices in a mesh: tiles: 512 (over y, x, z, core).
Axes of the slice: x: 4, y: 8, z: 8, core: 2. Of those that a mesh axis runs over, the one named last changes fastest.
Arguments:
- fields: bfloat16 [512, 96, 256], P('tiles'), may hold values from -6 to 6
- conv_a: bfloat16 [9, 96, 96], replicated, may hold values from -0.21875 to 0.21875
- bias_a: float32 [96], replicated, may hold values from -3 to 3
- conv_b: bfloat16 [9, 96, 96], replicated, may hold values from -0.21875 to 0.21875
- cotangent: bfloat16 [512, 96, 256], P('tiles'), may hold values from -6 to 6
- neighbour_tile: int32 [512, 4], P('tiles'), may hold values from 0 to 511, as said below
- edge_code: int32 [512, 4], P('tiles'), may hold values from 0 to 7, as said below
- corner_tile: int32 [512, 4], P('tiles'), may hold values from 0 to 511, as said below
- corner_code: int32 [512, 4], P('tiles'), may hold values from 0 to 3, as said below
- corner_missing: int32 [512, 4], P('tiles'), may hold values 0 or 1
Outputs:
- output: bfloat16 [512, 96, 256], P('tiles')
- grad_fields: bfloat16 [512, 96, 256], P('tiles')
- grad_a: float32 [9, 96, 96], replicated
- grad_b: float32 [9, 96, 96], replicated
- grad_bias: float32 [96], replicated
Inputs may be any that keep to these rules, and one draw needn't show every extreme that they name: `neighbour_tile`: the atlas is a torus of rows of 8 tiles. The tiles of side k of tile p and of corner c are p plus one of -8, 1, 8, -1 (sides) and of 1 - 8, 9, 7, -1 - 8 (corners), modulo 512, a different offset for each side and each corner of a tile. `edge_code`: adjacency is mutual: if side k of tile p meets side j of tile q, then side j of q meets side k of p, with the same reversal. `corner_tile`: offsets as stated for neighbour_tile. `corner_code`: if corner c of tile p meets corner m of tile q, then corner m of q meets corner c of p.
All inputs are finite; a program needn't handle non-finite values. No bound on the sum of `corner_missing` on one device may be relied on, other than what follows from the above.
Results may differ from a plain program's by a relative error of at most 0.0075.
Values may be sent and summed in bfloat16 or wider, within the bound.
No kernel may reach another device: no remote copies, remote signals or barrier semaphores. Data moves between devices by JAX's collectives and lax.ppermute only.
A program may use at most 64 MiB of HBM per device.

v0:
```python
import jax
import jax.numpy as jnp
from jax import lax
from jax.sharding import PartitionSpec as P

SIDE = 16
TILE_ROW = 8


inv_root_two = 0.7071067811865476
inv_root_tau = 0.3989422804014327


def passed_along(block, axis, distance):
    devices = range(lax.axis_size(axis))
    route = [((i - distance) % len(devices), i) for i in devices]
    return lax.ppermute(block, axis, route)


def gelu_slope(values):
    return (
        0.5 * (1.0 + lax.erf(values * inv_root_two))
        + values * jnp.exp(-0.5 * values * values) * inv_root_tau
    )


def strip_sides(tile_field):
    return jnp.stack(
        [tile_field[:, 0, :], tile_field[:, :, -1], tile_field[:, -1, :], tile_field[:, :, 0]],
        axis=0,
    )


def rim_sides(padded):
    return jnp.stack(
        [padded[:, 0, 1:-1], padded[:, 1:-1, -1], padded[:, -1, 1:-1], padded[:, 1:-1, 0]], axis=0
    )


def corner_cells(tile_field):
    return jnp.stack(
        [tile_field[:, 0, 0], tile_field[:, 0, -1], tile_field[:, -1, -1], tile_field[:, -1, 0]],
        axis=0,
    )


def offset_class(linked, offsets):
    device_count = lax.axis_size("tiles")
    own_index = lax.axis_index("tiles")
    relative = (linked - own_index) % device_count
    targets = jnp.array([shift_by % device_count for shift_by in offsets], dtype=jnp.int32)
    matches = (relative[:, None] == targets[None, :]).astype(jnp.int32)
    classes = jnp.sum(matches * jnp.arange(4, dtype=jnp.int32)[None, :], axis=1)
    return (matches, classes)


def exchange_rims(strips, corners, tile_links):
    neighbour_ids, edge_codes, corner_ids, corner_codes = tile_links
    row_length = TILE_ROW
    edge_offsets = [-row_length, 1, row_length, -1]
    diag_offsets = [1 - row_length, 1 + row_length, row_length - 1, -1 - row_length]
    edge_match, edge_class = offset_class(neighbour_ids, edge_offsets)
    diag_match, diag_class = offset_class(corner_ids, diag_offsets)
    reverse = (edge_codes >= 4)[:, None, None]
    their_side = edge_codes % 4
    received = []
    for direction in range(4):
        received.append(passed_along(strips, "tiles", -edge_offsets[direction]))
    stacked = jnp.concatenate(received, axis=0)
    picked = stacked[edge_class * 4 + their_side]
    picked = jnp.where(reverse, picked[:, :, ::-1], picked)
    corner_recv = []
    for direction in range(4):
        corner_recv.append(passed_along(corners, "tiles", -diag_offsets[direction]))
    corner_stack = jnp.concatenate(corner_recv, axis=0)
    corner_got = corner_stack[diag_class * 4 + corner_codes]
    return (picked, corner_got)


def halo_build(tile_field, tile_links, missing):
    picked, corner_got = exchange_rims(
        strip_sides(tile_field), corner_cells(tile_field), tile_links
    )
    corner_got = jnp.where((missing == 1)[:, None], jnp.zeros_like(corner_got), corner_got)
    padded = jnp.pad(tile_field, ((0, 0), (1, 1), (1, 1)))
    padded = padded.at[:, 0, 1:-1].set(picked[0])
    padded = padded.at[:, 1:-1, -1].set(picked[1])
    padded = padded.at[:, -1, 1:-1].set(picked[2])
    padded = padded.at[:, 1:-1, 0].set(picked[3])
    padded = padded.at[:, 0, 0].set(corner_got[0])
    padded = padded.at[:, 0, -1].set(corner_got[1])
    padded = padded.at[:, -1, -1].set(corner_got[2])
    padded = padded.at[:, -1, 0].set(corner_got[3])
    return padded


def adjoint_halo(back_rim, tile_links, missing):
    rim_corner = corner_cells(back_rim)
    rim_corner = jnp.where((missing == 1)[:, None], jnp.zeros_like(rim_corner), rim_corner)
    picked, corner_got = exchange_rims(rim_sides(back_rim), rim_corner, tile_links)
    summed = back_rim[:, 1:-1, 1:-1].astype(jnp.float32)
    summed = summed.at[:, 0, :].add(picked[0].astype(jnp.float32))
    summed = summed.at[:, :, -1].add(picked[1].astype(jnp.float32))
    summed = summed.at[:, -1, :].add(picked[2].astype(jnp.float32))
    summed = summed.at[:, :, 0].add(picked[3].astype(jnp.float32))
    summed = summed.at[:, 0, 0].add(corner_got[0].astype(jnp.float32))
    summed = summed.at[:, 0, -1].add(corner_got[1].astype(jnp.float32))
    summed = summed.at[:, -1, -1].add(corner_got[2].astype(jnp.float32))
    summed = summed.at[:, -1, 0].add(corner_got[3].astype(jnp.float32))
    return summed


def conv_cells(padded, weights):
    channels = padded.shape[0]
    cell_width = padded.shape[1] - 2
    result = jnp.zeros((weights.shape[1], cell_width * cell_width), jnp.float32)
    for tap_index in range(9):
        row_off, col_off = divmod(tap_index, 3)
        window = padded[:, row_off : row_off + cell_width, col_off : col_off + cell_width].reshape(
            channels, cell_width * cell_width
        )
        result = result + jnp.dot(weights[tap_index], window, preferred_element_type=jnp.float32)
    return result


def spread_back(grad_rows, weights, cell_width):
    grad_grid = grad_rows.reshape(grad_rows.shape[0], cell_width, cell_width)
    wide_grid = jnp.pad(grad_grid, ((0, 0), (2, 2), (2, 2)))
    ext_width = cell_width + 2
    result = jnp.zeros((weights.shape[2], ext_width * ext_width), jnp.float32)
    for tap_index in range(9):
        row_off, col_off = divmod(tap_index, 3)
        window = wide_grid[
            :, 2 - row_off : 2 - row_off + ext_width, 2 - col_off : 2 - col_off + ext_width
        ].reshape(grad_rows.shape[0], ext_width * ext_width)
        result = result + lax.dot_general(
            weights[tap_index], window, (((0,), (0,)), ((), ())), preferred_element_type=jnp.float32
        )
    return result.reshape(weights.shape[2], ext_width, ext_width)


def weight_terms(padded, grad_rows, cell_width):
    channels = padded.shape[0]
    term_list = []
    for tap_index in range(9):
        row_off, col_off = divmod(tap_index, 3)
        window = padded[:, row_off : row_off + cell_width, col_off : col_off + cell_width].reshape(
            channels, cell_width * cell_width
        )
        term_list.append(
            lax.dot_general(
                grad_rows, window, (((1,), (1,)), ((), ())), preferred_element_type=jnp.float32
            )
        )
    return jnp.stack(term_list, axis=0)


def body(
    fields,
    conv_a,
    bias_a,
    conv_b,
    cotangent,
    neighbour_tile,
    edge_code,
    corner_tile,
    corner_code,
    corner_missing,
):
    channels = fields.shape[1]
    cell_width = SIDE
    tile_links = (neighbour_tile[0], edge_code[0], corner_tile[0], corner_code[0])
    missing = corner_missing[0]
    padded_x = halo_build(fields[0].reshape(channels, cell_width, cell_width), tile_links, missing)
    pre_act = conv_cells(padded_x, conv_a) + bias_a[:, None]
    activation = jax.nn.gelu(pre_act, approximate=False).astype(jnp.bfloat16)
    pre_saved = pre_act.astype(jnp.bfloat16)
    padded_act = halo_build(
        activation.reshape(channels, cell_width, cell_width), tile_links, missing
    )
    output = (fields[0].astype(jnp.float32) + conv_cells(padded_act, conv_b)).astype(jnp.bfloat16)
    upstream = cotangent[0]
    back_act = spread_back(upstream, conv_b, cell_width).astype(jnp.bfloat16)
    terms_b = weight_terms(padded_act, upstream, cell_width)
    grad_act = adjoint_halo(back_act, tile_links, missing)
    grad_pre = (
        grad_act.reshape(channels, cell_width * cell_width)
        * gelu_slope(pre_saved.astype(jnp.float32))
    ).astype(jnp.bfloat16)
    back_x = spread_back(grad_pre, conv_a, cell_width).astype(jnp.bfloat16)
    terms_a = weight_terms(padded_x, grad_pre, cell_width)
    terms_bias = jnp.sum(grad_pre, axis=1, dtype=jnp.float32)
    summed_a, summed_b, summed_bias = lax.psum((terms_a, terms_b, terms_bias), "tiles")
    pulled_x = adjoint_halo(back_x, tile_links, missing).reshape(channels, cell_width * cell_width)
    grad_fields = (upstream.astype(jnp.float32) + pulled_x).astype(jnp.bfloat16)
    grad_scale = (lax.axis_size("tiles") * cell_width * cell_width) ** (-0.5)
    return (
        output[None],
        grad_fields[None],
        summed_a * grad_scale,
        summed_b * grad_scale,
        summed_bias * grad_scale,
    )


def solution(mesh):
    return jax.shard_map(
        body,
        mesh=mesh,
        in_specs=(
            P("tiles", None, None),
            P(),
            P(),
            P(),
            P("tiles", None, None),
            P("tiles", None),
            P("tiles", None),
            P("tiles", None),
            P("tiles", None),
            P("tiles", None),
        ),
        out_specs=(P("tiles", None, None), P("tiles", None, None), P(), P(), P()),
        check_vma=False,
    )
```

profile of v0, /device:TPU:1, one launch (start us, length us, event | category | flops | bytes accessed | tf_op | source)
XLA Modules:
  0.0 617.6 jit_solution(15387508278514202673)
XLA Ops:
  7.2 0.9 copy.151
  8.2 12.0 %collective-permute-start.7 = (bf16[4,96]{1,0:T(4,128)(2,1)S(1)}, bf16[4,96]{1,0:T(4,128)(2,1)S(1)}, u32[]{:S(2)}, u32[]{:S(2)}) collective-permute-start(bf16[4,96]{1,0:T(4,128)(2,1)S(1)} %pad_maximum_fusion.12), channel_id=1, source_target_pairs={{503,0},{504,1},{505,2},{506,3},{507,4},{508,5},{509,6},{510,7},{5... | collective-permute-start | bytes 2312 | tf_op jit(solution)/shard_map/ppermute | solution.py:17
  20.2 7.0 %collective-permute-start.6 = (bf16[4,96]{1,0:T(4,128)(2,1)S(1)}, bf16[4,96]{1,0:T(4,128)(2,1)S(1)}, u32[]{:S(2)}, u32[]{:S(2)}) collective-permute-start(bf16[4,96]{1,0:T(4,128)(2,1)S(1)} %pad_maximum_fusion.12), channel_id=1, source_target_pairs={{7,0},{8,1},{9,2},{10,3},{11,4},{12,5},{13,6},{14,7},{15,8},{16,9}... | collective-permute-start | bytes 2312 | tf_op jit(solution)/shard_map/ppermute | solution.py:17
  27.2 7.5 %collective-permute-start.5 = (bf16[4,96]{1,0:T(4,128)(2,1)S(1)}, bf16[4,96]{1,0:T(4,128)(2,1)S(1)}, u32[]{:S(2)}, u32[]{:S(2)}) collective-permute-start(bf16[4,96]{1,0:T(4,128)(2,1)S(1)} %pad_maximum_fusion.12), channel_id=1, source_target_pairs={{9,0},{10,1},{11,2},{12,3},{13,4},{14,5},{15,6},{16,7},{17,8},{18,... | collective-permute-start | bytes 2312 | tf_op jit(solution)/shard_map/ppermute | solution.py:17
  34.8 1.9 collective-permute-start.4
  36.8 1.9 collective-permute-start.3
  50.1 2.4 collective-permute-start.23
  52.6 11.2 %collective-permute-start.22 = (bf16[4,96]{1,0:T(4,128)(2,1)S(1)}, bf16[4,96]{1,0:T(4,128)(2,1)S(1)}, u32[]{:S(2)}, u32[]{:S(2)}) collective-permute-start(bf16[4,96]{1,0:T(4,128)(2,1)S(1)} %get-tuple-element.501), channel_id=1, source_target_pairs={{7,0},{8,1},{9,2},{10,3},{11,4},{12,5},{13,6},{14,7},{15,8},{16,9}... | collective-permute-start | bytes 2312 | tf_op jit(solution)/shard_map/ppermute | solution.py:17
  63.8 6.6 %collective-permute-start.21 = (bf16[4,96]{1,0:T(4,128)(2,1)S(1)}, bf16[4,96]{1,0:T(4,128)(2,1)S(1)}, u32[]{:S(2)}, u32[]{:S(2)}) collective-permute-start(bf16[4,96]{1,0:T(4,128)(2,1)S(1)} %get-tuple-element.501), channel_id=1, source_target_pairs={{9,0},{10,1},{11,2},{12,3},{13,4},{14,5},{15,6},{16,7},{17,8},{18,... | collective-permute-start | bytes 2312 | tf_op jit(solution)/shard_map/ppermute | solution.py:17
  70.5 1.9 collective-permute-start.20
  72.4 10.8 %collective-permute-start.2 = (bf16[4,96,16]{1,2,0:T(8,128)(2,1)S(1)}, bf16[4,96,16]{1,2,0:T(8,128)(2,1)S(1)}, u32[]{:S(2)}, u32[]{:S(2)}) collective-permute-start(bf16[4,96,16]{1,2,0:T(8,128)(2,1)S(1)} %pad_maximum_fusion.4), channel_id=1, source_target_pairs={{8,0},{9,1},{10,2},{11,3},{12,4},{13,5},{14,6},{15,7},{16,8},{17,9... | collective-permute-start | bytes 36872 | tf_op jit(solution)/shard_map/ppermute | solution.py:17
  83.3 1.9 collective-permute-start.1
  85.2 1.9 collective-permute-start
  87.1 3.6 collective-permute-start.19
  91.4 11.8 %collective-permute-start.18 = (bf16[4,96,16]{1,2,0:T(8,128)(2,1)S(1)}, bf16[4,96,16]{1,2,0:T(8,128)(2,1)S(1)}, u32[]{:S(2)}, u32[]{:S(2)}) collective-permute-start(bf16[4,96,16]{1,2,0:T(8,128)(2,1)S(1)} %pad_maximum_fusion.6), channel_id=1, source_target_pairs={{8,0},{9,1},{10,2},{11,3},{12,4},{13,5},{14,6},{15,7},{16,8},{17,9... | collective-permute-start | bytes 36872 | tf_op jit(solution)/shard_map/ppermute | solution.py:17
  103.2 1.9 collective-permute-start.17
  105.1 1.9 collective-permute-start.16
  108.2 9.5 %collective-permute-done.16 = bf16[4,96,16]{1,2,0:T(8,128)(2,1)S(1)} collective-permute-done((bf16[4,96,16]{1,2,0:T(8,128)(2,1)S(1)}, bf16[4,96,16]{1,2,0:T(8,128)(2,1)S(1)}, u32[]{:S(2)}, u32[]{:S(2)}) %collective-permute-start.16) | collective-permute-done | bytes 12320 | tf_op jit(solution)/shard_map/ppermute | solution.py:17
  118.5 1.4 scatter.54
  120.2 1.9 broadcast_select_fusion.9
  122.1 1.2 scatter.61
  123.7 2.0 broadcast_select_fusion.7
  125.6 1.3 scatter-add.61
  130.9 1.9 collective-permute-start.15
  132.8 13.3 %collective-permute-start.14 = (bf16[4,96]{1,0:T(4,128)(2,1)S(1)}, bf16[4,96]{1,0:T(4,128)(2,1)S(1)}, u32[]{:S(2)}, u32[]{:S(2)}) collective-permute-start(bf16[4,96]{1,0:T(4,128)(2,1)S(1)} %pad_maximum_fusion.13), channel_id=1, source_target_pairs={{7,0},{8,1},{9,2},{10,3},{11,4},{12,5},{13,6},{14,7},{15,8},{16,9}... | collective-permute-start | bytes 2312 | tf_op jit(solution)/shard_map/ppermute | solution.py:17
  146.1 1.9 collective-permute-start.13
  148.0 3.9 collective-permute-start.12
  154.9 99.5 %psum.23 = f32[96]{0:T(128)S(1)} all-reduce(f32[96]{0:T(128)S(1)} %get-tuple-element.406), channel_id=1, replica_groups=mesh['tiles'=512] {'tiles'}, use_global_device_ids=true, to_apply=%region_13.14 | all-reduce | flops 96 | bytes 768 | tf_op jit(solution)/shard_map/psum | solution.py:193
  255.0 2.5 collective-permute-start.11
  259.4 2.8 collective-permute-start.31
  262.2 9.9 %collective-permute-start.30 = (bf16[4,96]{1,0:T(4,128)(2,1)S(1)}, bf16[4,96]{1,0:T(4,128)(2,1)S(1)}, u32[]{:S(2)}, u32[]{:S(2)}) collective-permute-start(bf16[4,96]{1,0:T(4,128)(2,1)S(1)} %get-tuple-element.495), channel_id=1, source_target_pairs={{7,0},{8,1},{9,2},{10,3},{11,4},{12,5},{13,6},{14,7},{15,8},{16,9}... | collective-permute-start | bytes 2312 | tf_op jit(solution)/shard_map/ppermute | solution.py:17
  272.2 2.9 collective-permute-start.29
  275.0 5.4 collective-permute-start.28
  280.5 6.8 %collective-permute-start.10 = (bf16[4,96,16]{1,2,0:T(8,128)(2,1)S(1)}, bf16[4,96,16]{1,2,0:T(8,128)(2,1)S(1)}, u32[]{:S(2)}, u32[]{:S(2)}) collective-permute-start(bf16[4,96,16]{1,2,0:T(8,128)(2,1)S(1)} %pad_maximum_fusion.5), channel_id=1, source_target_pairs={{8,0},{9,1},{10,2},{11,3},{12,4},{13,5},{14,6},{15,7},{16,8},{17,9... | collective-permute-start | bytes 36872 | tf_op jit(solution)/shard_map/ppermute | solution.py:17
  287.3 1.9 collective-permute-start.9
  289.3 2.8 collective-permute-start.8
  292.1 3.5 collective-permute-start.27
  296.2 11.3 %collective-permute-start.26 = (bf16[4,96,16]{1,2,0:T(8,128)(2,1)S(1)}, bf16[4,96,16]{1,2,0:T(8,128)(2,1)S(1)}, u32[]{:S(2)}, u32[]{:S(2)}) collective-permute-start(bf16[4,96,16]{1,2,0:T(8,128)(2,1)S(1)} %pad_maximum_fusion.7), channel_id=1, source_target_pairs={{8,0},{9,1},{10,2},{11,3},{12,4},{13,5},{14,6},{15,7},{16,8},{17,9... | collective-permute-start | bytes 36872 | tf_op jit(solution)/shard_map/ppermute | solution.py:17
  307.5 3.8 collective-permute-start.25
  311.3 3.1 collective-permute-start.24
  315.0 8.9 %collective-permute-done.24 = bf16[4,96,16]{1,2,0:T(8,128)(2,1)S(1)} collective-permute-done((bf16[4,96,16]{1,2,0:T(8,128)(2,1)S(1)}, bf16[4,96,16]{1,2,0:T(8,128)(2,1)S(1)}, u32[]{:S(2)}, u32[]{:S(2)}) %collective-permute-start.24) | collective-permute-done | bytes 12320 | tf_op jit(solution)/shard_map/ppermute | solution.py:17
  324.7 1.4 scatter.66
  326.4 1.9 broadcast_select_fusion.8
  328.3 1.2 scatter.75
  330.3 2.0 broadcast_select_fusion.6
  332.2 1.3 scatter-add.75
  339.0 269.1 %all-reduce.7.cloned.1.call-done = (f32[9,96,96]{2,1,0:T(8,128)}, f32[9,96,96]{2,1,0:T(8,128)}) async-done(((f32[9,96,96]{2,1,0:T(8,128)}, f32[9,96,96]{2,1,0:T(8,128)}), (f32[9,96,96]{2,1,0:T(8,128)}, f32[9,96,96]{2,1,0:T(8,128)})) %all-reduce.7.cloned.1.call-update) | async-done | bytes 663568 | tf_op jit(solution)/shard_map/psum | solution.py:193
  608.1 1.9 broadcast_multiply_fusion.1
  (274 shorter events, 32.2 us)
Async XLA Ops:
  7.2 600.9 %all-reduce.7.cloned.1.call-start = ((), (), s32[]{:S(2)}) async-start(), calls=%async_computation | async-start | bytes 1769472 | tf_op jit(solution)/shard_map/psum | solution.py:193
  8.2 41.3 %collective-permute-start.7 = (bf16[4,96]{1,0:T(4,128)(2,1)S(1)}, bf16[4,96]{1,0:T(4,128)(2,1)S(1)}, u32[]{:S(2)}, u32[]{:S(2)}) collective-permute-start(bf16[4,96]{1,0:T(4,128)(2,1)S(1)} %pad_maximum_fusion.12), channel_id=1, source_target_pairs={{503,0},{504,1},{505,2},{506,3},{507,4},{508,5},{509,6},{510,7},{5... | collective-permute-start | bytes 2312 | tf_op jit(solution)/shard_map/ppermute | solution.py:17
  20.2 29.2 %collective-permute-start.6 = (bf16[4,96]{1,0:T(4,128)(2,1)S(1)}, bf16[4,96]{1,0:T(4,128)(2,1)S(1)}, u32[]{:S(2)}, u32[]{:S(2)}) collective-permute-start(bf16[4,96]{1,0:T(4,128)(2,1)S(1)} %pad_maximum_fusion.12), channel_id=1, source_target_pairs={{7,0},{8,1},{9,2},{10,3},{11,4},{12,5},{13,6},{14,7},{15,8},{16,9}... | collective-permute-start | bytes 2312 | tf_op jit(solution)/shard_map/ppermute | solution.py:17
  27.2 22.2 %collective-permute-start.5 = (bf16[4,96]{1,0:T(4,128)(2,1)S(1)}, bf16[4,96]{1,0:T(4,128)(2,1)S(1)}, u32[]{:S(2)}, u32[]{:S(2)}) collective-permute-start(bf16[4,96]{1,0:T(4,128)(2,1)S(1)} %pad_maximum_fusion.12), channel_id=1, source_target_pairs={{9,0},{10,1},{11,2},{12,3},{13,4},{14,5},{15,6},{16,7},{17,8},{18,... | collective-permute-start | bytes 2312 | tf_op jit(solution)/shard_map/ppermute | solution.py:17
  34.8 14.7 %collective-permute-start.4 = (bf16[4,96]{1,0:T(4,128)(2,1)S(1)}, bf16[4,96]{1,0:T(4,128)(2,1)S(1)}, u32[]{:S(2)}, u32[]{:S(2)}) collective-permute-start(bf16[4,96]{1,0:T(4,128)(2,1)S(1)} %pad_maximum_fusion.12), channel_id=1, source_target_pairs={{505,0},{506,1},{507,2},{508,3},{509,4},{510,5},{511,6},{0,7},{1,8... | collective-permute-start | bytes 2312 | tf_op jit(solution)/shard_map/ppermute | solution.py:17
  36.7 2.0 copy-start
  36.8 54.6 %collective-permute-start.3 = (bf16[4,96,16]{1,2,0:T(8,128)(2,1)S(1)}, bf16[4,96,16]{1,2,0:T(8,128)(2,1)S(1)}, u32[]{:S(2)}, u32[]{:S(2)}) collective-permute-start(bf16[4,96,16]{1,2,0:T(8,128)(2,1)S(1)} %pad_maximum_fusion.4), channel_id=1, source_target_pairs={{511,0},{0,1},{1,2},{2,3},{3,4},{4,5},{5,6},{6,7},{7,8},{8,9},{9,1... | collective-permute-start | bytes 36872 | tf_op jit(solution)/shard_map/ppermute | solution.py:17
  39.3 0.9 copy-start.1
  42.4 0.7 copy-start.11
  44.3 0.7 copy-start.10
  45.0 0.8 copy-start.9
  45.7 0.7 copy-start.12
  46.5 0.7 copy-start.13
  47.1 0.7 copy-start.8
  48.7 0.7 copy-start.15
  50.1 22.3 %collective-permute-start.23 = (bf16[4,96]{1,0:T(4,128)(2,1)S(1)}, bf16[4,96]{1,0:T(4,128)(2,1)S(1)}, u32[]{:S(2)}, u32[]{:S(2)}) collective-permute-start(bf16[4,96]{1,0:T(4,128)(2,1)S(1)} %get-tuple-element.501), channel_id=1, source_target_pairs={{503,0},{504,1},{505,2},{506,3},{507,4},{508,5},{509,6},{510,7},{5... | collective-permute-start | bytes 2312 | tf_op jit(solution)/shard_map/ppermute | solution.py:17
  52.6 30.7 %collective-permute-start.22 = (bf16[4,96]{1,0:T(4,128)(2,1)S(1)}, bf16[4,96]{1,0:T(4,128)(2,1)S(1)}, u32[]{:S(2)}, u32[]{:S(2)}) collective-permute-start(bf16[4,96]{1,0:T(4,128)(2,1)S(1)} %get-tuple-element.501), channel_id=1, source_target_pairs={{7,0},{8,1},{9,2},{10,3},{11,4},{12,5},{13,6},{14,7},{15,8},{16,9}... | collective-permute-start | bytes 2312 | tf_op jit(solution)/shard_map/ppermute | solution.py:17
  63.8 21.4 %collective-permute-start.21 = (bf16[4,96]{1,0:T(4,128)(2,1)S(1)}, bf16[4,96]{1,0:T(4,128)(2,1)S(1)}, u32[]{:S(2)}, u32[]{:S(2)}) collective-permute-start(bf16[4,96]{1,0:T(4,128)(2,1)S(1)} %get-tuple-element.501), channel_id=1, source_target_pairs={{9,0},{10,1},{11,2},{12,3},{13,4},{14,5},{15,6},{16,7},{17,8},{18,... | collective-permute-start | bytes 2312 | tf_op jit(solution)/shard_map/ppermute | solution.py:17
  70.5 16.7 %collective-permute-start.20 = (bf16[4,96]{1,0:T(4,128)(2,1)S(1)}, bf16[4,96]{1,0:T(4,128)(2,1)S(1)}, u32[]{:S(2)}, u32[]{:S(2)}) collective-permute-start(bf16[4,96]{1,0:T(4,128)(2,1)S(1)} %get-tuple-element.501), channel_id=1, source_target_pairs={{505,0},{506,1},{507,2},{508,3},{509,4},{510,5},{511,6},{0,7},{1,8... | collective-permute-start | bytes 2312 | tf_op jit(solution)/shard_map/ppermute | solution.py:17
  72.4 30.7 %collective-permute-start.2 = (bf16[4,96,16]{1,2,0:T(8,128)(2,1)S(1)}, bf16[4,96,16]{1,2,0:T(8,128)(2,1)S(1)}, u32[]{:S(2)}, u32[]{:S(2)}) collective-permute-start(bf16[4,96,16]{1,2,0:T(8,128)(2,1)S(1)} %pad_maximum_fusion.4), channel_id=1, source_target_pairs={{8,0},{9,1},{10,2},{11,3},{12,4},{13,5},{14,6},{15,7},{16,8},{17,9... | collective-permute-start | bytes 36872 | tf_op jit(solution)/shard_map/ppermute | solution.py:17
  83.3 21.8 %collective-permute-start.1 = (bf16[4,96,16]{1,2,0:T(8,128)(2,1)S(1)}, bf16[4,96,16]{1,2,0:T(8,128)(2,1)S(1)}, u32[]{:S(2)}, u32[]{:S(2)}) collective-permute-start(bf16[4,96,16]{1,2,0:T(8,128)(2,1)S(1)} %pad_maximum_fusion.4), channel_id=1, source_target_pairs={{1,0},{2,1},{3,2},{4,3},{5,4},{6,5},{7,6},{8,7},{9,8},{10,9},{11,1... | collective-permute-start | bytes 36872 | tf_op jit(solution)/shard_map/ppermute | solution.py:17
  85.2 21.8 %collective-permute-start = (bf16[4,96,16]{1,2,0:T(8,128)(2,1)S(1)}, bf16[4,96,16]{1,2,0:T(8,128)(2,1)S(1)}, u32[]{:S(2)}, u32[]{:S(2)}) collective-permute-start(bf16[4,96,16]{1,2,0:T(8,128)(2,1)S(1)} %pad_maximum_fusion.4), channel_id=1, source_target_pairs={{504,0},{505,1},{506,2},{507,3},{508,4},{509,5},{510,6},{511,7},{0... | collective-permute-start | bytes 36872 | tf_op jit(solution)/shard_map/ppermute | solution.py:17
  87.1 20.5 %collective-permute-start.19 = (bf16[4,96,16]{1,2,0:T(8,128)(2,1)S(1)}, bf16[4,96,16]{1,2,0:T(8,128)(2,1)S(1)}, u32[]{:S(2)}, u32[]{:S(2)}) collective-permute-start(bf16[4,96,16]{1,2,0:T(8,128)(2,1)S(1)} %pad_maximum_fusion.6), channel_id=1, source_target_pairs={{511,0},{0,1},{1,2},{2,3},{3,4},{4,5},{5,6},{6,7},{7,8},{8,9},{9,1... | collective-permute-start | bytes 36872 | tf_op jit(solution)/shard_map/ppermute | solution.py:17
  91.4 16.3 %collective-permute-start.18 = (bf16[4,96,16]{1,2,0:T(8,128)(2,1)S(1)}, bf16[4,96,16]{1,2,0:T(8,128)(2,1)S(1)}, u32[]{:S(2)}, u32[]{:S(2)}) collective-permute-start(bf16[4,96,16]{1,2,0:T(8,128)(2,1)S(1)} %pad_maximum_fusion.6), channel_id=1, source_target_pairs={{8,0},{9,1},{10,2},{11,3},{12,4},{13,5},{14,6},{15,7},{16,8},{17,9... | collective-permute-start | bytes 36872 | tf_op jit(solution)/shard_map/ppermute | solution.py:17
  103.2 5.1 collective-permute-start.17
  105.1 12.6 %collective-permute-start.16 = (bf16[4,96,16]{1,2,0:T(8,128)(2,1)S(1)}, bf16[4,96,16]{1,2,0:T(8,128)(2,1)S(1)}, u32[]{:S(2)}, u32[]{:S(2)}) collective-permute-start(bf16[4,96,16]{1,2,0:T(8,128)(2,1)S(1)} %pad_maximum_fusion.6), channel_id=1, source_target_pairs={{504,0},{505,1},{506,2},{507,3},{508,4},{509,5},{510,6},{511,7},{0... | collective-permute-start | bytes 36872 | tf_op jit(solution)/shard_map/ppermute | solution.py:17
  127.3 0.9 copy-start.2
  129.5 0.7 copy-start.16
  130.9 127.9 %collective-permute-start.15 = (bf16[4,96]{1,0:T(4,128)(2,1)S(1)}, bf16[4,96]{1,0:T(4,128)(2,1)S(1)}, u32[]{:S(2)}, u32[]{:S(2)}) collective-permute-start(bf16[4,96]{1,0:T(4,128)(2,1)S(1)} %pad_maximum_fusion.13), channel_id=1, source_target_pairs={{503,0},{504,1},{505,2},{506,3},{507,4},{508,5},{509,6},{510,7},{5... | collective-permute-start | bytes 2312 | tf_op jit(solution)/shard_map/ppermute | solution.py:17
  132.8 125.9 %collective-permute-start.14 = (bf16[4,96]{1,0:T(4,128)(2,1)S(1)}, bf16[4,96]{1,0:T(4,128)(2,1)S(1)}, u32[]{:S(2)}, u32[]{:S(2)}) collective-permute-start(bf16[4,96]{1,0:T(4,128)(2,1)S(1)} %pad_maximum_fusion.13), channel_id=1, source_target_pairs={{7,0},{8,1},{9,2},{10,3},{11,4},{12,5},{13,6},{14,7},{15,8},{16,9}... | collective-permute-start | bytes 2312 | tf_op jit(solution)/shard_map/ppermute | solution.py:17
  146.1 112.7 %collective-permute-start.13 = (bf16[4,96]{1,0:T(4,128)(2,1)S(1)}, bf16[4,96]{1,0:T(4,128)(2,1)S(1)}, u32[]{:S(2)}, u32[]{:S(2)}) collective-permute-start(bf16[4,96]{1,0:T(4,128)(2,1)S(1)} %pad_maximum_fusion.13), channel_id=1, source_target_pairs={{9,0},{10,1},{11,2},{12,3},{13,4},{14,5},{15,6},{16,7},{17,8},{18,... | collective-permute-start | bytes 2312 | tf_op jit(solution)/shard_map/ppermute | solution.py:17
  148.0 110.8 %collective-permute-start.12 = (bf16[4,96]{1,0:T(4,128)(2,1)S(1)}, bf16[4,96]{1,0:T(4,128)(2,1)S(1)}, u32[]{:S(2)}, u32[]{:S(2)}) collective-permute-start(bf16[4,96]{1,0:T(4,128)(2,1)S(1)} %pad_maximum_fusion.13), channel_id=1, source_target_pairs={{505,0},{506,1},{507,2},{508,3},{509,4},{510,5},{511,6},{0,7},{1,8... | collective-permute-start | bytes 2312 | tf_op jit(solution)/shard_map/ppermute | solution.py:17
  255.0 41.2 %collective-permute-start.11 = (bf16[4,96,16]{1,2,0:T(8,128)(2,1)S(1)}, bf16[4,96,16]{1,2,0:T(8,128)(2,1)S(1)}, u32[]{:S(2)}, u32[]{:S(2)}) collective-permute-start(bf16[4,96,16]{1,2,0:T(8,128)(2,1)S(1)} %pad_maximum_fusion.5), channel_id=1, source_target_pairs={{511,0},{0,1},{1,2},{2,3},{3,4},{4,5},{5,6},{6,7},{7,8},{8,9},{9,1... | collective-permute-start | bytes 36872 | tf_op jit(solution)/shard_map/ppermute | solution.py:17
  258.6 65.4 %copy-start.3 = (f32[9,96,96]{2,1,0:T(8,128)}, f32[9,96,96]{2,1,0:T(8,128)S(1)}, u32[]{:S(2)}) copy-start(f32[9,96,96]{2,1,0:T(8,128)S(1)} %fusion.18) | copy-start | bytes 995332
  259.4 21.1 %collective-permute-start.31 = (bf16[4,96]{1,0:T(4,128)(2,1)S(1)}, bf16[4,96]{1,0:T(4,128)(2,1)S(1)}, u32[]{:S(2)}, u32[]{:S(2)}) collective-permute-start(bf16[4,96]{1,0:T(4,128)(2,1)S(1)} %get-tuple-element.495), channel_id=1, source_target_pairs={{503,0},{504,1},{505,2},{506,3},{507,4},{508,5},{509,6},{510,7},{5... | collective-permute-start | bytes 2312 | tf_op jit(solution)/shard_map/ppermute | solution.py:17
  262.2 25.1 %collective-permute-start.30 = (bf16[4,96]{1,0:T(4,128)(2,1)S(1)}, bf16[4,96]{1,0:T(4,128)(2,1)S(1)}, u32[]{:S(2)}, u32[]{:S(2)}) collective-permute-start(bf16[4,96]{1,0:T(4,128)(2,1)S(1)} %get-tuple-element.495), channel_id=1, source_target_pairs={{7,0},{8,1},{9,2},{10,3},{11,4},{12,5},{13,6},{14,7},{15,8},{16,9}... | collective-permute-start | bytes 2312 | tf_op jit(solution)/shard_map/ppermute | solution.py:17
  272.2 17.1 %collective-permute-start.29 = (bf16[4,96]{1,0:T(4,128)(2,1)S(1)}, bf16[4,96]{1,0:T(4,128)(2,1)S(1)}, u32[]{:S(2)}, u32[]{:S(2)}) collective-permute-start(bf16[4,96]{1,0:T(4,128)(2,1)S(1)} %get-tuple-element.495), channel_id=1, source_target_pairs={{9,0},{10,1},{11,2},{12,3},{13,4},{14,5},{15,6},{16,7},{17,8},{18,... | collective-permute-start | bytes 2312 | tf_op jit(solution)/shard_map/ppermute | solution.py:17
  275.0 17.0 %collective-permute-start.28 = (bf16[4,96]{1,0:T(4,128)(2,1)S(1)}, bf16[4,96]{1,0:T(4,128)(2,1)S(1)}, u32[]{:S(2)}, u32[]{:S(2)}) collective-permute-start(bf16[4,96]{1,0:T(4,128)(2,1)S(1)} %get-tuple-element.495), channel_id=1, source_target_pairs={{505,0},{506,1},{507,2},{508,3},{509,4},{510,5},{511,6},{0,7},{1,8... | collective-permute-start | bytes 2312 | tf_op jit(solution)/shard_map/ppermute | solution.py:17
  280.5 27.0 %collective-permute-start.10 = (bf16[4,96,16]{1,2,0:T(8,128)(2,1)S(1)}, bf16[4,96,16]{1,2,0:T(8,128)(2,1)S(1)}, u32[]{:S(2)}, u32[]{:S(2)}) collective-permute-start(bf16[4,96,16]{1,2,0:T(8,128)(2,1)S(1)} %pad_maximum_fusion.5), channel_id=1, source_target_pairs={{8,0},{9,1},{10,2},{11,3},{12,4},{13,5},{14,6},{15,7},{16,8},{17,9... | collective-permute-start | bytes 36872 | tf_op jit(solution)/shard_map/ppermute | solution.py:17
  287.3 24.0 %collective-permute-start.9 = (bf16[4,96,16]{1,2,0:T(8,128)(2,1)S(1)}, bf16[4,96,16]{1,2,0:T(8,128)(2,1)S(1)}, u32[]{:S(2)}, u32[]{:S(2)}) collective-permute-start(bf16[4,96,16]{1,2,0:T(8,128)(2,1)S(1)} %pad_maximum_fusion.5), channel_id=1, source_target_pairs={{1,0},{2,1},{3,2},{4,3},{5,4},{6,5},{7,6},{8,7},{9,8},{10,9},{11,1... | collective-permute-start | bytes 36872 | tf_op jit(solution)/shard_map/ppermute | solution.py:17
  289.3 25.1 %collective-permute-start.8 = (bf16[4,96,16]{1,2,0:T(8,128)(2,1)S(1)}, bf16[4,96,16]{1,2,0:T(8,128)(2,1)S(1)}, u32[]{:S(2)}, u32[]{:S(2)}) collective-permute-start(bf16[4,96,16]{1,2,0:T(8,128)(2,1)S(1)} %pad_maximum_fusion.5), channel_id=1, source_target_pairs={{504,0},{505,1},{506,2},{507,3},{508,4},{509,5},{510,6},{511,7},{0... | collective-permute-start | bytes 36872 | tf_op jit(solution)/shard_map/ppermute | solution.py:17
  292.1 22.9 %collective-permute-start.27 = (bf16[4,96,16]{1,2,0:T(8,128)(2,1)S(1)}, bf16[4,96,16]{1,2,0:T(8,128)(2,1)S(1)}, u32[]{:S(2)}, u32[]{:S(2)}) collective-permute-start(bf16[4,96,16]{1,2,0:T(8,128)(2,1)S(1)} %pad_maximum_fusion.7), channel_id=1, source_target_pairs={{511,0},{0,1},{1,2},{2,3},{3,4},{4,5},{5,6},{6,7},{7,8},{8,9},{9,1... | collective-permute-start | bytes 36872 | tf_op jit(solution)/shard_map/ppermute | solution.py:17
  296.2 18.8 %collective-permute-start.26 = (bf16[4,96,16]{1,2,0:T(8,128)(2,1)S(1)}, bf16[4,96,16]{1,2,0:T(8,128)(2,1)S(1)}, u32[]{:S(2)}, u32[]{:S(2)}) collective-permute-start(bf16[4,96,16]{1,2,0:T(8,128)(2,1)S(1)} %pad_maximum_fusion.7), channel_id=1, source_target_pairs={{8,0},{9,1},{10,2},{11,3},{12,4},{13,5},{14,6},{15,7},{16,8},{17,9... | collective-permute-start | bytes 36872 | tf_op jit(solution)/shard_map/ppermute | solution.py:17
  307.5 7.5 %collective-permute-start.25 = (bf16[4,96,16]{1,2,0:T(8,128)(2,1)S(1)}, bf16[4,96,16]{1,2,0:T(8,128)(2,1)S(1)}, u32[]{:S(2)}, u32[]{:S(2)}) collective-permute-start(bf16[4,96,16]{1,2,0:T(8,128)(2,1)S(1)} %pad_maximum_fusion.7), channel_id=1, source_target_pairs={{1,0},{2,1},{3,2},{4,3},{5,4},{6,5},{7,6},{8,7},{9,8},{10,9},{11,1... | collective-permute-start | bytes 36872 | tf_op jit(solution)/shard_map/ppermute | solution.py:17
  311.3 12.6 %collective-permute-start.24 = (bf16[4,96,16]{1,2,0:T(8,128)(2,1)S(1)}, bf16[4,96,16]{1,2,0:T(8,128)(2,1)S(1)}, u32[]{:S(2)}, u32[]{:S(2)}) collective-permute-start(bf16[4,96,16]{1,2,0:T(8,128)(2,1)S(1)} %pad_maximum_fusion.7), channel_id=1, source_target_pairs={{504,0},{505,1},{506,2},{507,3},{508,4},{509,5},{510,6},{511,7},{0... | collective-permute-start | bytes 36872 | tf_op jit(solution)/shard_map/ppermute | solution.py:17
  336.6 0.8 copy-start.4
  337.4 0.8 copy-start.6
  608.1 1.9 copy-start.5
  (2 other events, 1.3 us)
Sparse Core Ops, SparseCore 0:
  337.5 270.5 all-reduce.6
where the time goes:
time: 619 us; the launch traced here: 618 us
  waiting for transfers between devices  288 us (47%)
  starting transfers between devices  164 us (26%)
  blocking collectives  99.5 us (16%)
  local copies, waits for them, and re-layouts  26.6 us (4%)
  between operations  15.5 us (3%)
  other arithmetic  13.3 us (2%)
  matrix products  10.1 us (2%)
    psum x1, waiting for transfers between devices, body(): lax.psum((terms_a, terms_b, terms_bias), 'tiles')  269 us
    ppermute x32, starting transfers between devices, passed_along(): return lax.ppermute(block, axis, route)  164 us
    psum x1, blocking collectives, body(): lax.psum((terms_a, terms_b, terms_bias), 'tiles')  99.5 us
    ppermute x32, waiting for transfers between devices, passed_along(): return lax.ppermute(block, axis, route)  19 us
  transfers between devices with their start and end apart: 33, of which 4 were waited for; matrix products, arithmetic and copies ran while one was open for 3% of the time, Pallas kernels for 0%

commit v1 on v0

--- a/solution.py
+++ b/solution.py
@@ -54,60 +54,70 @@
     return (matches, classes)
 
 
-def exchange_rims(strips, corners, tile_links):
+def exchange_groups(strip_groups, corner_groups, tile_links):
     neighbour_ids, edge_codes, corner_ids, corner_codes = tile_links
     row_length = TILE_ROW
     edge_offsets = [-row_length, 1, row_length, -1]
     diag_offsets = [1 - row_length, 1 + row_length, row_length - 1, -1 - row_length]
-    edge_match, edge_class = offset_class(neighbour_ids, edge_offsets)
-    diag_match, diag_class = offset_class(corner_ids, diag_offsets)
+    _, edge_class = offset_class(neighbour_ids, edge_offsets)
+    _, diag_class = offset_class(corner_ids, diag_offsets)
+    groups = len(strip_groups)
+    strips = jnp.concatenate(strip_groups, axis=0)
+    corners = jnp.concatenate(corner_groups, axis=0)
+    received = [passed_along(strips, "tiles", -edge_offsets[d]) for d in range(4)]
+    stacked = jnp.concatenate(received, axis=0)
+    corner_recv = [passed_along(corners, "tiles", -diag_offsets[d]) for d in range(4)]
+    corner_stack = jnp.concatenate(corner_recv, axis=0)
     reverse = (edge_codes >= 4)[:, None, None]
     their_side = edge_codes % 4
-    received = []
-    for direction in range(4):
-        received.append(passed_along(strips, "tiles", -edge_offsets[direction]))
-    stacked = jnp.concatenate(received, axis=0)
-    picked = stacked[edge_class * 4 + their_side]
-    picked = jnp.where(reverse, picked[:, :, ::-1], picked)
-    corner_recv = []
-    for direction in range(4):
-        corner_recv.append(passed_along(corners, "tiles", -diag_offsets[direction]))
-    corner_stack = jnp.concatenate(corner_recv, axis=0)
-    corner_got = corner_stack[diag_class * 4 + corner_codes]
-    return (picked, corner_got)
-
-
-def halo_build(tile_field, tile_links, missing):
-    picked, corner_got = exchange_rims(
-        strip_sides(tile_field), corner_cells(tile_field), tile_links
-    )
+    out = []
+    for g in range(groups):
+        picked = stacked[edge_class * (4 * groups) + 4 * g + their_side]
+        picked = jnp.where(reverse, picked[:, :, ::-1], picked)
+        corner_got = corner_stack[diag_class * (4 * groups) + 4 * g + corner_codes]
+        out.append((picked, corner_got))
+    return out
+
+
+def assemble_padded(tile_field, picked, corner_got, missing):
     corner_got = jnp.where((missing == 1)[:, None], jnp.zeros_like(corner_got), corner_got)
-    padded = jnp.pad(tile_field, ((0, 0), (1, 1), (1, 1)))
-    padded = padded.at[:, 0, 1:-1].set(picked[0])
-    padded = padded.at[:, 1:-1, -1].set(picked[1])
-    padded = padded.at[:, -1, 1:-1].set(picked[2])
-    padded = padded.at[:, 1:-1, 0].set(picked[3])
-    padded = padded.at[:, 0, 0].set(corner_got[0])
-    padded = padded.at[:, 0, -1].set(corner_got[1])
-    padded = padded.at[:, -1, -1].set(corner_got[2])
-    padded = padded.at[:, -1, 0].set(corner_got[3])
-    return padded
-
-
-def adjoint_halo(back_rim, tile_links, missing):
+    top = jnp.concatenate(
+        [corner_got[0][:, None], picked[0], corner_got[1][:, None]], axis=1
+    )
+    bottom = jnp.concatenate(
+        [corner_got[3][:, None], picked[2], corner_got[2][:, None]], axis=1
+    )
+    middle = jnp.concatenate(
+        [picked[3][:, :, None], tile_field, picked[1][:, :, None]], axis=2
+    )
+    return jnp.concatenate([top[:, None, :], middle, bottom[:, None, :]], axis=1)
+
+
+def rim_payload(back_rim, missing):
     rim_corner = corner_cells(back_rim)
     rim_corner = jnp.where((missing == 1)[:, None], jnp.zeros_like(rim_corner), rim_corner)
-    picked, corner_got = exchange_rims(rim_sides(back_rim), rim_corner, tile_links)
+    return rim_sides(back_rim), rim_corner
+
+
+def adjoint_sum(back_rim, picked, corner_got):
     summed = back_rim[:, 1:-1, 1:-1].astype(jnp.float32)
-    summed = summed.at[:, 0, :].add(picked[0].astype(jnp.float32))
-    summed = summed.at[:, :, -1].add(picked[1].astype(jnp.float32))
-    summed = summed.at[:, -1, :].add(picked[2].astype(jnp.float32))
-    summed = summed.at[:, :, 0].add(picked[3].astype(jnp.float32))
-    summed = summed.at[:, 0, 0].add(corner_got[0].astype(jnp.float32))
-    summed = summed.at[:, 0, -1].add(corner_got[1].astype(jnp.float32))
-    summed = summed.at[:, -1, -1].add(corner_got[2].astype(jnp.float32))
-    summed = summed.at[:, -1, 0].add(corner_got[3].astype(jnp.float32))
-    return summed
+    p = picked.astype(jnp.float32)
+    c = corner_got.astype(jnp.float32)
+    side = SIDE
+    summed = summed + jnp.pad(p[0][:, None, :], ((0, 0), (0, side - 1), (0, 0)))
+    summed = summed + jnp.pad(p[2][:, None, :], ((0, 0), (side - 1, 0), (0, 0)))
+    summed = summed + jnp.pad(p[3][:, :, None], ((0, 0), (0, 0), (0, side - 1)))
+    summed = summed + jnp.pad(p[1][:, :, None], ((0, 0), (0, 0), (side - 1, 0)))
+    corner_grid = jnp.stack(
+        [
+            jnp.stack([c[0], c[1]], axis=-1),
+            jnp.stack([c[3], c[2]], axis=-1),
+        ],
+        axis=-2,
+    )
+    full = jnp.zeros_like(summed)
+    full = full.at[:, 0::side - 1, 0::side - 1].set(corner_grid)
+    return summed + full
 
 
 def conv_cells(padded, weights):
@@ -171,18 +181,20 @@
     cell_width = SIDE
     tile_links = (neighbour_tile[0], edge_code[0], corner_tile[0], corner_code[0])
     missing = corner_missing[0]
-    padded_x = halo_build(fields[0].reshape(channels, cell_width, cell_width), tile_links, missing)
+    field_grid = fields[0].reshape(channels, cell_width, cell_width)
+    upstream = cotangent[0]
+    back_act = spread_back(upstream, conv_b, cell_width).astype(jnp.bfloat16)
+    act_rims, act_rim_corners = rim_payload(back_act, missing)
+    (x_picked, x_corners), (ba_picked, ba_corners) = exchange_groups(
+        [strip_sides(field_grid), act_rims],
+        [corner_cells(field_grid), act_rim_corners],
+        tile_links,
+    )
+    padded_x = assemble_padded(field_grid, x_picked, x_corners, missing)
     pre_act = conv_cells(padded_x, conv_a) + bias_a[:, None]
     activation = jax.nn.gelu(pre_act, approximate=False).astype(jnp.bfloat16)
     pre_saved = pre_act.astype(jnp.bfloat16)
-    padded_act = halo_build(
-        activation.reshape(channels, cell_width, cell_width), tile_links, missing
-    )
-    output = (fields[0].astype(jnp.float32) + conv_cells(padded_act, conv_b)).astype(jnp.bfloat16)
-    upstream = cotangent[0]
-    back_act = spread_back(upstream, conv_b, cell_width).astype(jnp.bfloat16)
-    terms_b = weight_terms(padded_act, upstream, cell_width)
-    grad_act = adjoint_halo(back_act, tile_links, missing)
+    grad_act = adjoint_sum(back_act, ba_picked, ba_corners)
     grad_pre = (
         grad_act.reshape(channels, cell_width * cell_width)
         * gelu_slope(pre_saved.astype(jnp.float32))
@@ -190,8 +202,25 @@
     back_x = spread_back(grad_pre, conv_a, cell_width).astype(jnp.bfloat16)
     terms_a = weight_terms(padded_x, grad_pre, cell_width)
     terms_bias = jnp.sum(grad_pre, axis=1, dtype=jnp.float32)
-    summed_a, summed_b, summed_bias = lax.psum((terms_a, terms_b, terms_bias), "tiles")
-    pulled_x = adjoint_halo(back_x, tile_links, missing).reshape(channels, cell_width * cell_width)
+    act_grid = activation.reshape(channels, cell_width, cell_width)
+    x_rims, x_rim_corners = rim_payload(back_x, missing)
+    (a_picked, a_corners), (bx_picked, bx_corners) = exchange_groups(
+        [strip_sides(act_grid), x_rims],
+        [corner_cells(act_grid), x_rim_corners],
+        tile_links,
+    )
+    padded_act = assemble_padded(act_grid, a_picked, a_corners, missing)
+    output = (fields[0].astype(jnp.float32) + conv_cells(padded_act, conv_b)).astype(jnp.bfloat16)
+    terms_b = weight_terms(padded_act, upstream, cell_width)
+    tap_size = terms_a.size
+    flat = jnp.concatenate([terms_a.reshape(-1), terms_b.reshape(-1), terms_bias])
+    summed = lax.psum(flat, "tiles")
+    summed_a = summed[:tap_size].reshape(terms_a.shape)
+    summed_b = summed[tap_size : 2 * tap_size].reshape(terms_b.shape)
+    summed_bias = summed[2 * tap_size :]
+    pulled_x = adjoint_sum(back_x, bx_picked, bx_corners).reshape(
+        channels, cell_width * cell_width
+    )
     grad_fields = (upstream.astype(jnp.float32) + pulled_x).astype(jnp.bfloat16)
     grad_scale = (lax.axis_size("tiles") * cell_width * cell_width) ** (-0.5)
     return (

time: 619 us -> 418 us (0.68)
  blocking collectives: 99.5 us -> 0 us
  starting transfers between devices: 164 us -> 82.1 us
  other arithmetic: 13.3 us -> 5.41 us
  local copies, waits for them, and re-layouts: 26.6 us -> 19 us
    psum x1 -> x0, blocking collectives: 99.5 us -> none  [body(): lax.psum((terms_a, terms_b, terms_bias), 'tiles')]
    ppermute x32 -> x16, starting transfers between devices: 164 us -> 82.1 us  [passed_along(): return lax.ppermute(block, axis, route)]
    another operation x14 -> x6, other arithmetic: 9.24 us -> 0.05 us  [adjoint_sum(): jnp.stack([jnp.stack([c[0], c[1]], axis=-1), jnp.stack([c[3], c[2]], axis...]
    ppermute x32 -> x16, waiting for transfers between devices: 19 us -> 19.6 us  [passed_along(): return lax.ppermute(block, axis, route)]
  transfers between devices with their start and end apart: 33 -> 17, of which waited for: 4 -> 4; matrix products, arithmetic and copies ran while one was open for 3% -> 2% of each run, Pallas kernels for 0% -> 0%
where the time goes in v1:
time: 418 us
  waiting for transfers between devices  286 us (68%)
  starting transfers between devices  82.1 us (20%)
  local copies, waits for them, and re-layouts  19 us (5%)
  between operations  15.2 us (4%)
  matrix products  10.4 us (2%)
  other arithmetic  5.41 us (1%)
    psum x1, waiting for transfers between devices, body(): summed = lax.psum(flat, 'tiles')  266 us
    ppermute x16, starting transfers between devices, passed_along(): return lax.ppermute(block, axis, route)  82.1 us
    ppermute x16, waiting for transfers between devices, passed_along(): return lax.ppermute(block, axis, route)  19.6 us
  transfers between devices with their start and end apart: 17, of which 4 were waited for; matrix products, arithmetic and copies ran while one was open for 2% of the time, Pallas kernels for 0%

profile of v1, /device:TPU:1, one launch (start us, length us, event | category | flops | bytes accessed | tf_op | source)
XLA Modules:
  0.0 417.7 jit_solution(3553146024857435849)
XLA Ops:
  7.2 0.7 compare_bitcast_fusion.1
  7.9 0.9 copy.97
  9.4 0.9 copy-done.1
  12.5 12.0 %collective-permute-start.3 = (bf16[8,96]{1,0:T(8,128)(2,1)S(1)}, bf16[8,96]{1,0:T(8,128)(2,1)S(1)}, u32[]{:S(2)}, u32[]{:S(2)}) collective-permute-start(bf16[8,96]{1,0:T(8,128)(2,1)S(1)} %concatenate.83), channel_id=1, source_target_pairs={{503,0},{504,1},{505,2},{506,3},{507,4},{508,5},{509,6},{510,7},{5... | collective-permute-start | bytes 4616 | tf_op jit(solution)/shard_map/ppermute | solution.py:17
  24.5 7.0 %collective-permute-start.2 = (bf16[8,96]{1,0:T(8,128)(2,1)S(1)}, bf16[8,96]{1,0:T(8,128)(2,1)S(1)}, u32[]{:S(2)}, u32[]{:S(2)}) collective-permute-start(bf16[8,96]{1,0:T(8,128)(2,1)S(1)} %concatenate.83), channel_id=1, source_target_pairs={{7,0},{8,1},{9,2},{10,3},{11,4},{12,5},{13,6},{14,7},{15,8},{16,9}... | collective-permute-start | bytes 4616 | tf_op jit(solution)/shard_map/ppermute | solution.py:17
  31.6 7.5 %collective-permute-start.1 = (bf16[8,96]{1,0:T(8,128)(2,1)S(1)}, bf16[8,96]{1,0:T(8,128)(2,1)S(1)}, u32[]{:S(2)}, u32[]{:S(2)}) collective-permute-start(bf16[8,96]{1,0:T(8,128)(2,1)S(1)} %concatenate.83), channel_id=1, source_target_pairs={{9,0},{10,1},{11,2},{12,3},{13,4},{14,5},{15,6},{16,7},{17,8},{18,... | collective-permute-start | bytes 4616 | tf_op jit(solution)/shard_map/ppermute | solution.py:17
  39.1 1.9 collective-permute-start
  41.2 1.9 collective-permute-start.7
  43.2 0.6 copy-done.6
  43.8 0.6 copy-done.4
  44.5 0.6 copy-done.10
  45.4 0.6 copy-done.9
  46.9 4.3 %collective-permute-done = bf16[8,96]{1,0:T(8,128)(2,1)S(1)} collective-permute-done((bf16[8,96]{1,0:T(8,128)(2,1)S(1)}, bf16[8,96]{1,0:T(8,128)(2,1)S(1)}, u32[]{:S(2)}, u32[]{:S(2)}) %collective-permute-start) | collective-permute-done | bytes 1568 | tf_op jit(solution)/shard_map/ppermute | solution.py:17
  51.3 7.7 %collective-permute-start.6 = (bf16[8,96,16]{1,2,0:T(8,128)(2,1)S(1)}, bf16[8,96,16]{1,2,0:T(8,128)(2,1)S(1)}, u32[]{:S(2)}, u32[]{:S(2)}) collective-permute-start(bf16[8,96,16]{1,2,0:T(8,128)(2,1)S(1)} %constant_dynamic-update-slice_fusion.4), channel_id=1, source_target_pairs={{8,0},{9,1},{10,2},{11,3},{12,4},{13,5},{14,6},{15,7},{16,8},{17,9... | collective-permute-start | bytes 73736 | tf_op jit(solution)/shard_map/ppermute | solution.py:17
  59.0 1.9 collective-permute-start.5
  60.9 1.9 collective-permute-start.4
  62.9 0.6 gather_fusion.3
  63.5 0.6 gather_fusion
  64.2 0.7 scatter_fusion
  64.9 9.1 %collective-permute-done.4 = bf16[8,96,16]{1,2,0:T(8,128)(2,1)S(1)} collective-permute-done((bf16[8,96,16]{1,2,0:T(8,128)(2,1)S(1)}, bf16[8,96,16]{1,2,0:T(8,128)(2,1)S(1)}, u32[]{:S(2)}, u32[]{:S(2)}) %collective-permute-start.4) | collective-permute-done | bytes 24608 | tf_op jit(solution)/shard_map/ppermute | solution.py:17
  74.1 0.6 gather_fusion.2
  74.7 0.6 gather_fusion.1
  76.0 0.9 copy-done.2
  78.2 0.6 copy-done.8
  78.8 0.5 convert_reduce_fusion
  82.5 1.9 collective-permute-start.11
  84.4 11.4 %collective-permute-start.10 = (bf16[8,96]{1,0:T(8,128)(2,1)S(1)}, bf16[8,96]{1,0:T(8,128)(2,1)S(1)}, u32[]{:S(2)}, u32[]{:S(2)}) collective-permute-start(bf16[8,96]{1,0:T(8,128)(2,1)S(1)} %concatenate.95), channel_id=1, source_target_pairs={{7,0},{8,1},{9,2},{10,3},{11,4},{12,5},{13,6},{14,7},{15,8},{16,9}... | collective-permute-start | bytes 4616 | tf_op jit(solution)/shard_map/ppermute | solution.py:17
  95.8 2.2 collective-permute-start.9
  98.1 5.4 %collective-permute-start.8 = (bf16[8,96]{1,0:T(8,128)(2,1)S(1)}, bf16[8,96]{1,0:T(8,128)(2,1)S(1)}, u32[]{:S(2)}, u32[]{:S(2)}) collective-permute-start(bf16[8,96]{1,0:T(8,128)(2,1)S(1)} %concatenate.95), channel_id=1, source_target_pairs={{505,0},{506,1},{507,2},{508,3},{509,4},{510,5},{511,6},{0,7},{1,8... | collective-permute-start | bytes 4616 | tf_op jit(solution)/shard_map/ppermute | solution.py:17
  105.1 5.9 %collective-permute-start.15 = (bf16[8,96,16]{1,2,0:T(8,128)(2,1)S(1)}, bf16[8,96,16]{1,2,0:T(8,128)(2,1)S(1)}, u32[]{:S(2)}, u32[]{:S(2)}) collective-permute-start(bf16[8,96,16]{1,2,0:T(8,128)(2,1)S(1)} %constant_dynamic-update-slice_fusion.20), channel_id=1, source_target_pairs={{511,0},{0,1},{1,2},{2,3},{3,4},{4,5},{5,6},{6,7},{7,8},{8,9},{9,1... | collective-permute-start | bytes 73736 | tf_op jit(solution)/shard_map/ppermute | solution.py:17
  111.1 5.6 %collective-permute-start.14 = (bf16[8,96,16]{1,2,0:T(8,128)(2,1)S(1)}, bf16[8,96,16]{1,2,0:T(8,128)(2,1)S(1)}, u32[]{:S(2)}, u32[]{:S(2)}) collective-permute-start(bf16[8,96,16]{1,2,0:T(8,128)(2,1)S(1)} %constant_dynamic-update-slice_fusion.20), channel_id=1, source_target_pairs={{8,0},{9,1},{10,2},{11,3},{12,4},{13,5},{14,6},{15,7},{16,8},{17,9... | collective-permute-start | bytes 73736 | tf_op jit(solution)/shard_map/ppermute | solution.py:17
  116.7 2.7 collective-permute-start.13
  119.4 4.9 %collective-permute-start.12 = (bf16[8,96,16]{1,2,0:T(8,128)(2,1)S(1)}, bf16[8,96,16]{1,2,0:T(8,128)(2,1)S(1)}, u32[]{:S(2)}, u32[]{:S(2)}) collective-permute-start(bf16[8,96,16]{1,2,0:T(8,128)(2,1)S(1)} %constant_dynamic-update-slice_fusion.20), channel_id=1, source_target_pairs={{504,0},{505,1},{506,2},{507,3},{508,4},{509,5},{510,6},{511,7},{0... | collective-permute-start | bytes 73736 | tf_op jit(solution)/shard_map/ppermute | solution.py:17
  124.3 0.6 gather_fusion.7
  124.9 0.6 gather_fusion.4
  125.6 0.7 scatter_fusion.1
  126.3 6.1 %collective-permute-done.12 = bf16[8,96,16]{1,2,0:T(8,128)(2,1)S(1)} collective-permute-done((bf16[8,96,16]{1,2,0:T(8,128)(2,1)S(1)}, bf16[8,96,16]{1,2,0:T(8,128)(2,1)S(1)}, u32[]{:S(2)}, u32[]{:S(2)}) %collective-permute-start.12) | collective-permute-done | bytes 24608 | tf_op jit(solution)/shard_map/ppermute | solution.py:17
  132.5 0.6 gather_fusion.6
  133.1 0.6 gather_fusion.5
  134.2 0.7 copy-done
  135.2 0.7 copy.125
  138.9 0.9 pad_maximum_fusion
  140.0 0.8 fusion.14
  140.7 265.9 %all-reduce.12.cloned.1.call-done = f32[165984]{0:T(1024)} async-done(((f32[165984]{0:T(1024)}), f32[165984]{0:T(1024)}) %all-reduce.12.cloned.1.call-update) | async-done | bytes 663952 | tf_op jit(solution)/shard_map/psum | solution.py:217
  406.6 1.1 slice_multiply_fusion
  407.8 0.9 mul.198
  408.7 0.9 mul.196
  409.6 1.2 slice_multiply_fusion.2
  (220 shorter events, 14.7 us)
Async XLA Ops:
  7.2 399.5 %all-reduce.12.cloned.1.call-start = ((), (), s32[]{:S(2)}) async-start(), calls=%async_computation | async-start | bytes 1335296 | tf_op jit(solution)/shard_map/psum | solution.py:217
  7.9 0.9 copy-start.3
  9.3 0.9 copy-start.1
  12.5 50.4 %collective-permute-start.3 = (bf16[8,96]{1,0:T(8,128)(2,1)S(1)}, bf16[8,96]{1,0:T(8,128)(2,1)S(1)}, u32[]{:S(2)}, u32[]{:S(2)}) collective-permute-start(bf16[8,96]{1,0:T(8,128)(2,1)S(1)} %concatenate.83), channel_id=1, source_target_pairs={{503,0},{504,1},{505,2},{506,3},{507,4},{508,5},{509,6},{510,7},{5... | collective-permute-start | bytes 4616 | tf_op jit(solution)/shard_map/ppermute | solution.py:17
  24.5 36.4 %collective-permute-start.2 = (bf16[8,96]{1,0:T(8,128)(2,1)S(1)}, bf16[8,96]{1,0:T(8,128)(2,1)S(1)}, u32[]{:S(2)}, u32[]{:S(2)}) collective-permute-start(bf16[8,96]{1,0:T(8,128)(2,1)S(1)} %concatenate.83), channel_id=1, source_target_pairs={{7,0},{8,1},{9,2},{10,3},{11,4},{12,5},{13,6},{14,7},{15,8},{16,9}... | collective-permute-start | bytes 4616 | tf_op jit(solution)/shard_map/ppermute | solution.py:17
  31.6 27.4 %collective-permute-start.1 = (bf16[8,96]{1,0:T(8,128)(2,1)S(1)}, bf16[8,96]{1,0:T(8,128)(2,1)S(1)}, u32[]{:S(2)}, u32[]{:S(2)}) collective-permute-start(bf16[8,96]{1,0:T(8,128)(2,1)S(1)} %concatenate.83), channel_id=1, source_target_pairs={{9,0},{10,1},{11,2},{12,3},{13,4},{14,5},{15,6},{16,7},{17,8},{18,... | collective-permute-start | bytes 4616 | tf_op jit(solution)/shard_map/ppermute | solution.py:17
  39.1 12.1 %collective-permute-start = (bf16[8,96]{1,0:T(8,128)(2,1)S(1)}, bf16[8,96]{1,0:T(8,128)(2,1)S(1)}, u32[]{:S(2)}, u32[]{:S(2)}) collective-permute-start(bf16[8,96]{1,0:T(8,128)(2,1)S(1)} %concatenate.83), channel_id=1, source_target_pairs={{505,0},{506,1},{507,2},{508,3},{509,4},{510,5},{511,6},{0,7},{1,8... | collective-permute-start | bytes 4616 | tf_op jit(solution)/shard_map/ppermute | solution.py:17
  41.2 32.9 %collective-permute-start.7 = (bf16[8,96,16]{1,2,0:T(8,128)(2,1)S(1)}, bf16[8,96,16]{1,2,0:T(8,128)(2,1)S(1)}, u32[]{:S(2)}, u32[]{:S(2)}) collective-permute-start(bf16[8,96,16]{1,2,0:T(8,128)(2,1)S(1)} %constant_dynamic-update-slice_fusion.4), channel_id=1, source_target_pairs={{511,0},{0,1},{1,2},{2,3},{3,4},{4,5},{5,6},{6,7},{7,8},{8,9},{9,1... | collective-permute-start | bytes 73736 | tf_op jit(solution)/shard_map/ppermute | solution.py:17
  43.2 0.7 copy-start.6
  43.8 0.7 copy-start.4
  43.8 0.7 copy-start.5
  44.5 0.7 copy-start.10
  45.4 0.7 copy-start.9
  46.1 0.7 copy-start.7
  51.3 22.8 %collective-permute-start.6 = (bf16[8,96,16]{1,2,0:T(8,128)(2,1)S(1)}, bf16[8,96,16]{1,2,0:T(8,128)(2,1)S(1)}, u32[]{:S(2)}, u32[]{:S(2)}) collective-permute-start(bf16[8,96,16]{1,2,0:T(8,128)(2,1)S(1)} %constant_dynamic-update-slice_fusion.4), channel_id=1, source_target_pairs={{8,0},{9,1},{10,2},{11,3},{12,4},{13,5},{14,6},{15,7},{16,8},{17,9... | collective-permute-start | bytes 73736 | tf_op jit(solution)/shard_map/ppermute | solution.py:17
  59.0 15.1 %collective-permute-start.5 = (bf16[8,96,16]{1,2,0:T(8,128)(2,1)S(1)}, bf16[8,96,16]{1,2,0:T(8,128)(2,1)S(1)}, u32[]{:S(2)}, u32[]{:S(2)}) collective-permute-start(bf16[8,96,16]{1,2,0:T(8,128)(2,1)S(1)} %constant_dynamic-update-slice_fusion.4), channel_id=1, source_target_pairs={{1,0},{2,1},{3,2},{4,3},{5,4},{6,5},{7,6},{8,7},{9,8},{10,9},{11,1... | collective-permute-start | bytes 73736 | tf_op jit(solution)/shard_map/ppermute | solution.py:17
  60.9 13.1 %collective-permute-start.4 = (bf16[8,96,16]{1,2,0:T(8,128)(2,1)S(1)}, bf16[8,96,16]{1,2,0:T(8,128)(2,1)S(1)}, u32[]{:S(2)}, u32[]{:S(2)}) collective-permute-start(bf16[8,96,16]{1,2,0:T(8,128)(2,1)S(1)} %constant_dynamic-update-slice_fusion.4), channel_id=1, source_target_pairs={{504,0},{505,1},{506,2},{507,3},{508,4},{509,5},{510,6},{511,7},{0... | collective-permute-start | bytes 73736 | tf_op jit(solution)/shard_map/ppermute | solution.py:17
  75.9 0.9 copy-start.2
  78.1 0.7 copy-start.8
  82.5 41.8 %collective-permute-start.11 = (bf16[8,96]{1,0:T(8,128)(2,1)S(1)}, bf16[8,96]{1,0:T(8,128)(2,1)S(1)}, u32[]{:S(2)}, u32[]{:S(2)}) collective-permute-start(bf16[8,96]{1,0:T(8,128)(2,1)S(1)} %concatenate.95), channel_id=1, source_target_pairs={{503,0},{504,1},{505,2},{506,3},{507,4},{508,5},{509,6},{510,7},{5... | collective-permute-start | bytes 4616 | tf_op jit(solution)/shard_map/ppermute | solution.py:17
  84.4 35.0 %collective-permute-start.10 = (bf16[8,96]{1,0:T(8,128)(2,1)S(1)}, bf16[8,96]{1,0:T(8,128)(2,1)S(1)}, u32[]{:S(2)}, u32[]{:S(2)}) collective-permute-start(bf16[8,96]{1,0:T(8,128)(2,1)S(1)} %concatenate.95), channel_id=1, source_target_pairs={{7,0},{8,1},{9,2},{10,3},{11,4},{12,5},{13,6},{14,7},{15,8},{16,9}... | collective-permute-start | bytes 4616 | tf_op jit(solution)/shard_map/ppermute | solution.py:17
  95.8 20.9 %collective-permute-start.9 = (bf16[8,96]{1,0:T(8,128)(2,1)S(1)}, bf16[8,96]{1,0:T(8,128)(2,1)S(1)}, u32[]{:S(2)}, u32[]{:S(2)}) collective-permute-start(bf16[8,96]{1,0:T(8,128)(2,1)S(1)} %concatenate.95), channel_id=1, source_target_pairs={{9,0},{10,1},{11,2},{12,3},{13,4},{14,5},{15,6},{16,7},{17,8},{18,... | collective-permute-start | bytes 4616 | tf_op jit(solution)/shard_map/ppermute | solution.py:17
  98.1 13.0 %collective-permute-start.8 = (bf16[8,96]{1,0:T(8,128)(2,1)S(1)}, bf16[8,96]{1,0:T(8,128)(2,1)S(1)}, u32[]{:S(2)}, u32[]{:S(2)}) collective-permute-start(bf16[8,96]{1,0:T(8,128)(2,1)S(1)} %concatenate.95), channel_id=1, source_target_pairs={{505,0},{506,1},{507,2},{508,3},{509,4},{510,5},{511,6},{0,7},{1,8... | collective-permute-start | bytes 4616 | tf_op jit(solution)/shard_map/ppermute | solution.py:17
  105.1 27.3 %collective-permute-start.15 = (bf16[8,96,16]{1,2,0:T(8,128)(2,1)S(1)}, bf16[8,96,16]{1,2,0:T(8,128)(2,1)S(1)}, u32[]{:S(2)}, u32[]{:S(2)}) collective-permute-start(bf16[8,96,16]{1,2,0:T(8,128)(2,1)S(1)} %constant_dynamic-update-slice_fusion.20), channel_id=1, source_target_pairs={{511,0},{0,1},{1,2},{2,3},{3,4},{4,5},{5,6},{6,7},{7,8},{8,9},{9,1... | collective-permute-start | bytes 73736 | tf_op jit(solution)/shard_map/ppermute | solution.py:17
  111.1 21.4 %collective-permute-start.14 = (bf16[8,96,16]{1,2,0:T(8,128)(2,1)S(1)}, bf16[8,96,16]{1,2,0:T(8,128)(2,1)S(1)}, u32[]{:S(2)}, u32[]{:S(2)}) collective-permute-start(bf16[8,96,16]{1,2,0:T(8,128)(2,1)S(1)} %constant_dynamic-update-slice_fusion.20), channel_id=1, source_target_pairs={{8,0},{9,1},{10,2},{11,3},{12,4},{13,5},{14,6},{15,7},{16,8},{17,9... | collective-permute-start | bytes 73736 | tf_op jit(solution)/shard_map/ppermute | solution.py:17
  116.7 15.7 %collective-permute-start.13 = (bf16[8,96,16]{1,2,0:T(8,128)(2,1)S(1)}, bf16[8,96,16]{1,2,0:T(8,128)(2,1)S(1)}, u32[]{:S(2)}, u32[]{:S(2)}) collective-permute-start(bf16[8,96,16]{1,2,0:T(8,128)(2,1)S(1)} %constant_dynamic-update-slice_fusion.20), channel_id=1, source_target_pairs={{1,0},{2,1},{3,2},{4,3},{5,4},{6,5},{7,6},{8,7},{9,8},{10,9},{11,1... | collective-permute-start | bytes 73736 | tf_op jit(solution)/shard_map/ppermute | solution.py:17
  119.4 13.0 %collective-permute-start.12 = (bf16[8,96,16]{1,2,0:T(8,128)(2,1)S(1)}, bf16[8,96,16]{1,2,0:T(8,128)(2,1)S(1)}, u32[]{:S(2)}, u32[]{:S(2)}) collective-permute-start(bf16[8,96,16]{1,2,0:T(8,128)(2,1)S(1)} %constant_dynamic-update-slice_fusion.20), channel_id=1, source_target_pairs={{504,0},{505,1},{506,2},{507,3},{508,4},{509,5},{510,6},{511,7},{0... | collective-permute-start | bytes 73736 | tf_op jit(solution)/shard_map/ppermute | solution.py:17
  134.0 0.8 copy-start
Sparse Core Ops, SparseCore 0:
  139.9 266.6 all-reduce.11

commit v2 on v1

--- a/solution.py
+++ b/solution.py
@@ -5,6 +5,7 @@
 
 SIDE = 16
 TILE_ROW = 8
+HALVING_ROUNDS = 3
 
 
 inv_root_two = 0.7071067811865476
@@ -15,6 +16,36 @@
     devices = range(lax.axis_size(axis))
     route = [((i - distance) % len(devices), i) for i in devices]
     return lax.ppermute(block, axis, route)
+
+
+def xor_partner(block, distance):
+    devices = lax.axis_size("tiles")
+    return lax.ppermute(block, "tiles", [(i, i ^ distance) for i in range(devices)])
+
+
+def tree_all_reduce(flat, halving_rounds):
+    devices = lax.axis_size("tiles")
+    bits = devices.bit_length() - 1
+    own = lax.axis_index("tiles")
+    halving_rounds = min(halving_rounds, bits)
+    quantum = 128 << halving_rounds
+    length = flat.shape[0]
+    padded = -(-length // quantum) * quantum
+    cur = jnp.pad(flat, (0, padded - length))
+    for k in range(halving_rounds):
+        half = cur.shape[0] // 2
+        upper = ((own >> k) & 1) == 1
+        low, high = cur[:half], cur[half:]
+        keep = jnp.where(upper, high, low)
+        send = jnp.where(upper, low, high)
+        cur = keep + xor_partner(send, 1 << k)
+    for k in range(halving_rounds, bits):
+        cur = cur + xor_partner(cur, 1 << k)
+    for k in reversed(range(halving_rounds)):
+        upper = ((own >> k) & 1) == 1
+        got = xor_partner(cur, 1 << k)
+        cur = jnp.where(upper, jnp.concatenate([got, cur]), jnp.concatenate([cur, got]))
+    return cur[:length]
 
 
 def gelu_slope(values):
@@ -214,7 +245,7 @@
     terms_b = weight_terms(padded_act, upstream, cell_width)
     tap_size = terms_a.size
     flat = jnp.concatenate([terms_a.reshape(-1), terms_b.reshape(-1), terms_bias])
-    summed = lax.psum(flat, "tiles")
+    summed = tree_all_reduce(flat, HALVING_ROUNDS)
     summed_a = summed[:tap_size].reshape(terms_a.shape)
     summed_b = summed[tap_size : 2 * tap_size].reshape(terms_b.shape)
     summed_bias = summed[2 * tap_size :]

time: 418 us -> 225 us (0.54)
  waiting for transfers between devices: 286 us -> 64.6 us
  starting transfers between devices: 82.1 us -> 124 us
  between operations: 15.2 us -> 1.93 us
    psum x1 -> x0, waiting for transfers between devices: 266 us -> none  [body(): summed = lax.psum(flat, 'tiles')]
    ppermute x0 -> x12, waiting for transfers between devices: none -> 44.2 us  [xor_partner(): lax.ppermute(block, 'tiles', [(i, i ^ distance) for i in range(devices)])]
    ppermute x0 -> x12, starting transfers between devices: none -> 42.4 us  [xor_partner(): lax.ppermute(block, 'tiles', [(i, i ^ distance) for i in range(devices)])]
  transfers between devices with their start and end apart: 17 -> 28, of which waited for: 4 -> 15; matrix products, arithmetic and copies ran while one was open for 2% -> 4% of each run, Pallas kernels for 0% -> 0%
where the time goes in v2:
time: 225 us; the launch traced here: 224 us
  starting transfers between devices  124 us (55%)
  waiting for transfers between devices  64.6 us (29%)
  local copies, waits for them, and re-layouts  19.1 us (8%)
  matrix products  10.4 us (5%)
  other arithmetic  3.2 us (1%)
    ppermute x16, starting transfers between devices, passed_along(): return lax.ppermute(block, axis, route)  82.1 us
    ppermute x12, waiting for transfers between devices, xor_partner(): lax.ppermute(block, 'tiles', [(i, i ^ distance) for i in range(devices)])  44.2 us
    ppermute x12, starting transfers between devices, xor_partner(): lax.ppermute(block, 'tiles', [(i, i ^ distance) for i in range(devices)])  42.4 us
    ppermute x16, waiting for transfers between devices, passed_along(): return lax.ppermute(block, axis, route)  20.4 us
    unnamed x51, local copies, waits for them, and re-layouts  8.21 us
  transfers between devices with their start and end apart: 28, of which 15 were waited for; matrix products, arithmetic and copies ran while one was open for 4% of the time, Pallas kernels for 0%

profile of v2, /device:TPU:1, one launch (start us, length us, event | category | flops | bytes accessed | tf_op | source)
XLA Modules:
  0.0 223.8 jit_solution(17152172969414602639)
XLA Ops:
  1.3 0.9 copy.97
  2.8 0.9 copy-done.1
  5.9 12.0 %collective-permute-start.3 = (bf16[8,96]{1,0:T(8,128)(2,1)S(1)}, bf16[8,96]{1,0:T(8,128)(2,1)S(1)}, u32[]{:S(2)}, u32[]{:S(2)}) collective-permute-start(bf16[8,96]{1,0:T(8,128)(2,1)S(1)} %concatenate.104), channel_id=1, source_target_pairs={{503,0},{504,1},{505,2},{506,3},{507,4},{508,5},{509,6},{510,7},{5... | collective-permute-start | bytes 4616 | tf_op jit(solution)/shard_map/ppermute | solution.py:18
  18.0 7.0 %collective-permute-start.2 = (bf16[8,96]{1,0:T(8,128)(2,1)S(1)}, bf16[8,96]{1,0:T(8,128)(2,1)S(1)}, u32[]{:S(2)}, u32[]{:S(2)}) collective-permute-start(bf16[8,96]{1,0:T(8,128)(2,1)S(1)} %concatenate.104), channel_id=1, source_target_pairs={{7,0},{8,1},{9,2},{10,3},{11,4},{12,5},{13,6},{14,7},{15,8},{16,9}... | collective-permute-start | bytes 4616 | tf_op jit(solution)/shard_map/ppermute | solution.py:18
  25.0 7.5 %collective-permute-start.1 = (bf16[8,96]{1,0:T(8,128)(2,1)S(1)}, bf16[8,96]{1,0:T(8,128)(2,1)S(1)}, u32[]{:S(2)}, u32[]{:S(2)}) collective-permute-start(bf16[8,96]{1,0:T(8,128)(2,1)S(1)} %concatenate.104), channel_id=1, source_target_pairs={{9,0},{10,1},{11,2},{12,3},{13,4},{14,5},{15,6},{16,7},{17,8},{18,... | collective-permute-start | bytes 4616 | tf_op jit(solution)/shard_map/ppermute | solution.py:18
  32.6 1.9 collective-permute-start
  34.6 1.9 collective-permute-start.7
  40.4 4.3 %collective-permute-done = bf16[8,96]{1,0:T(8,128)(2,1)S(1)} collective-permute-done((bf16[8,96]{1,0:T(8,128)(2,1)S(1)}, bf16[8,96]{1,0:T(8,128)(2,1)S(1)}, u32[]{:S(2)}, u32[]{:S(2)}) %collective-permute-start) | collective-permute-done | bytes 1568 | tf_op jit(solution)/shard_map/ppermute | solution.py:18
  44.7 7.7 %collective-permute-start.6 = (bf16[8,96,16]{1,2,0:T(8,128)(2,1)S(1)}, bf16[8,96,16]{1,2,0:T(8,128)(2,1)S(1)}, u32[]{:S(2)}, u32[]{:S(2)}) collective-permute-start(bf16[8,96,16]{1,2,0:T(8,128)(2,1)S(1)} %constant_dynamic-update-slice_fusion.4), channel_id=1, source_target_pairs={{8,0},{9,1},{10,2},{11,3},{12,4},{13,5},{14,6},{15,7},{16,8},{17,9... | collective-permute-start | bytes 73736 | tf_op jit(solution)/shard_map/ppermute | solution.py:18
  52.4 1.9 collective-permute-start.5
  54.4 1.9 collective-permute-start.4
  58.4 9.1 %collective-permute-done.4 = bf16[8,96,16]{1,2,0:T(8,128)(2,1)S(1)} collective-permute-done((bf16[8,96,16]{1,2,0:T(8,128)(2,1)S(1)}, bf16[8,96,16]{1,2,0:T(8,128)(2,1)S(1)}, u32[]{:S(2)}, u32[]{:S(2)}) %collective-permute-start.4) | collective-permute-done | bytes 24608 | tf_op jit(solution)/shard_map/ppermute | solution.py:18
  69.4 0.9 copy-done.2
  75.9 1.9 collective-permute-start.11
  77.8 11.4 %collective-permute-start.10 = (bf16[8,96]{1,0:T(8,128)(2,1)S(1)}, bf16[8,96]{1,0:T(8,128)(2,1)S(1)}, u32[]{:S(2)}, u32[]{:S(2)}) collective-permute-start(bf16[8,96]{1,0:T(8,128)(2,1)S(1)} %concatenate.116), channel_id=1, source_target_pairs={{7,0},{8,1},{9,2},{10,3},{11,4},{12,5},{13,6},{14,7},{15,8},{16,9}... | collective-permute-start | bytes 4616 | tf_op jit(solution)/shard_map/ppermute | solution.py:18
  89.3 2.2 %collective-permute-start.9 = (bf16[8,96]{1,0:T(8,128)(2,1)S(1)}, bf16[8,96]{1,0:T(8,128)(2,1)S(1)}, u32[]{:S(2)}, u32[]{:S(2)}) collective-permute-start(bf16[8,96]{1,0:T(8,128)(2,1)S(1)} %concatenate.116), channel_id=1, source_target_pairs={{9,0},{10,1},{11,2},{12,3},{13,4},{14,5},{15,6},{16,7},{17,8},{18,... | collective-permute-start | bytes 4616 | tf_op jit(solution)/shard_map/ppermute | solution.py:18
  91.5 5.4 %collective-permute-start.8 = (bf16[8,96]{1,0:T(8,128)(2,1)S(1)}, bf16[8,96]{1,0:T(8,128)(2,1)S(1)}, u32[]{:S(2)}, u32[]{:S(2)}) collective-permute-start(bf16[8,96]{1,0:T(8,128)(2,1)S(1)} %concatenate.116), channel_id=1, source_target_pairs={{505,0},{506,1},{507,2},{508,3},{509,4},{510,5},{511,6},{0,7},{1,8... | collective-permute-start | bytes 4616 | tf_op jit(solution)/shard_map/ppermute | solution.py:18
  98.6 5.9 %collective-permute-start.15 = (bf16[8,96,16]{1,2,0:T(8,128)(2,1)S(1)}, bf16[8,96,16]{1,2,0:T(8,128)(2,1)S(1)}, u32[]{:S(2)}, u32[]{:S(2)}) collective-permute-start(bf16[8,96,16]{1,2,0:T(8,128)(2,1)S(1)} %constant_dynamic-update-slice_fusion.20), channel_id=1, source_target_pairs={{511,0},{0,1},{1,2},{2,3},{3,4},{4,5},{5,6},{6,7},{7,8},{8,9},{9,1... | collective-permute-start | bytes 73736 | tf_op jit(solution)/shard_map/ppermute | solution.py:18
  104.5 5.6 %collective-permute-start.14 = (bf16[8,96,16]{1,2,0:T(8,128)(2,1)S(1)}, bf16[8,96,16]{1,2,0:T(8,128)(2,1)S(1)}, u32[]{:S(2)}, u32[]{:S(2)}) collective-permute-start(bf16[8,96,16]{1,2,0:T(8,128)(2,1)S(1)} %constant_dynamic-update-slice_fusion.20), channel_id=1, source_target_pairs={{8,0},{9,1},{10,2},{11,3},{12,4},{13,5},{14,6},{15,7},{16,8},{17,9... | collective-permute-start | bytes 73736 | tf_op jit(solution)/shard_map/ppermute | solution.py:18
  110.1 2.7 %collective-permute-start.13 = (bf16[8,96,16]{1,2,0:T(8,128)(2,1)S(1)}, bf16[8,96,16]{1,2,0:T(8,128)(2,1)S(1)}, u32[]{:S(2)}, u32[]{:S(2)}) collective-permute-start(bf16[8,96,16]{1,2,0:T(8,128)(2,1)S(1)} %constant_dynamic-update-slice_fusion.20), channel_id=1, source_target_pairs={{1,0},{2,1},{3,2},{4,3},{5,4},{6,5},{7,6},{8,7},{9,8},{10,9},{11,1... | collective-permute-start | bytes 73736 | tf_op jit(solution)/shard_map/ppermute | solution.py:18
  112.8 4.9 %collective-permute-start.12 = (bf16[8,96,16]{1,2,0:T(8,128)(2,1)S(1)}, bf16[8,96,16]{1,2,0:T(8,128)(2,1)S(1)}, u32[]{:S(2)}, u32[]{:S(2)}) collective-permute-start(bf16[8,96,16]{1,2,0:T(8,128)(2,1)S(1)} %constant_dynamic-update-slice_fusion.20), channel_id=1, source_target_pairs={{504,0},{505,1},{506,2},{507,3},{508,4},{509,5},{510,6},{511,7},{0... | collective-permute-start | bytes 73736 | tf_op jit(solution)/shard_map/ppermute | solution.py:18
  119.0 6.9 %collective-permute-done.12 = bf16[8,96,16]{1,2,0:T(8,128)(2,1)S(1)} collective-permute-done((bf16[8,96,16]{1,2,0:T(8,128)(2,1)S(1)}, bf16[8,96,16]{1,2,0:T(8,128)(2,1)S(1)}, u32[]{:S(2)}, u32[]{:S(2)}) %collective-permute-start.12) | collective-permute-done | bytes 24608 | tf_op jit(solution)/shard_map/ppermute | solution.py:18
  127.5 0.7 copy-done
  130.4 3.2 %collective-permute-start.16 = (f32[83456]{0:T(1024)S(1)}, f32[83456]{0:T(1024)S(1)}, u32[]{:S(2)}, u32[]{:S(2)}) collective-permute-start(f32[83456]{0:T(1024)S(1)} %broadcast_select_fusion), channel_id=1, source_target_pairs={{0,1},{1,0},{2,3},{3,2},{4,5},{5,4},{6,7},{7,6},{8,9},{9,8},{10,11... | collective-permute-start | bytes 1001480 | tf_op jit(solution)/shard_map/ppermute | solution.py:23
  135.0 2.7 %collective-permute-start.17 = (f32[41728]{0:T(1024)S(1)}, f32[41728]{0:T(1024)S(1)}, u32[]{:S(2)}, u32[]{:S(2)}) collective-permute-start(f32[41728]{0:T(1024)S(1)} %slice_select_fusion), channel_id=1, source_target_pairs={{0,2},{1,3},{2,0},{3,1},{4,6},{5,7},{6,4},{7,5},{8,10},{9,11},{10,... | collective-permute-start | bytes 500744 | tf_op jit(solution)/shard_map/ppermute | solution.py:23
  137.8 4.5 %collective-permute-done.17 = f32[41728]{0:T(1024)S(1)} collective-permute-done((f32[41728]{0:T(1024)S(1)}, f32[41728]{0:T(1024)S(1)}, u32[]{:S(2)}, u32[]{:S(2)}) %collective-permute-start.17) | collective-permute-done | bytes 166944 | tf_op jit(solution)/shard_map/ppermute | solution.py:23
  142.4 3.7 %collective-permute-start.18 = (f32[20864]{0:T(1024)S(1)}, f32[20864]{0:T(1024)S(1)}, u32[]{:S(2)}, u32[]{:S(2)}) collective-permute-start(f32[20864]{0:T(1024)S(1)} %slice_select_fusion.1), channel_id=1, source_target_pairs={{0,4},{1,5},{2,6},{3,7},{4,0},{5,1},{6,2},{7,3},{8,12},{9,13},{10,... | collective-permute-start | bytes 250376 | tf_op jit(solution)/shard_map/ppermute | solution.py:23
  146.3 3.6 %collective-permute-done.18 = f32[20864]{0:T(1024)S(1)} collective-permute-done((f32[20864]{0:T(1024)S(1)}, f32[20864]{0:T(1024)S(1)}, u32[]{:S(2)}, u32[]{:S(2)}) %collective-permute-start.18) | collective-permute-done | bytes 83488 | tf_op jit(solution)/shard_map/ppermute | solution.py:23
  149.9 2.7 %collective-permute-start.19 = (f32[20864]{0:T(1024)S(1)}, f32[20864]{0:T(1024)S(1)}, u32[]{:S(2)}, u32[]{:S(2)}) collective-permute-start(f32[20864]{0:T(1024)S(1)} %select_add_fusion.2), channel_id=1, source_target_pairs={{0,8},{1,9},{2,10},{3,11},{4,12},{5,13},{6,14},{7,15},{8,0},{9,1},... | collective-permute-start | bytes 250376 | tf_op jit(solution)/shard_map/ppermute | solution.py:23
  152.8 6.3 %collective-permute-done.19 = f32[20864]{0:T(1024)S(1)} collective-permute-done((f32[20864]{0:T(1024)S(1)}, f32[20864]{0:T(1024)S(1)}, u32[]{:S(2)}, u32[]{:S(2)}) %collective-permute-start.19) | collective-permute-done | bytes 83488 | tf_op jit(solution)/shard_map/ppermute | solution.py:23
  159.1 1.9 collective-permute-start.20
  161.2 3.1 %collective-permute-done.20 = f32[20864]{0:T(1024)S(1)} collective-permute-done((f32[20864]{0:T(1024)S(1)}, f32[20864]{0:T(1024)S(1)}, u32[]{:S(2)}, u32[]{:S(2)}) %collective-permute-start.20) | collective-permute-done | bytes 83488 | tf_op jit(solution)/shard_map/ppermute | solution.py:23
  164.3 1.9 collective-permute-start.21
  166.4 4.7 %collective-permute-done.21 = f32[20864]{0:T(1024)S(1)} collective-permute-done((f32[20864]{0:T(1024)S(1)}, f32[20864]{0:T(1024)S(1)}, u32[]{:S(2)}, u32[]{:S(2)}) %collective-permute-start.21) | collective-permute-done | bytes 83488 | tf_op jit(solution)/shard_map/ppermute | solution.py:23
  171.1 1.9 collective-permute-start.22
  173.2 3.5 %collective-permute-done.22 = f32[20864]{0:T(1024)S(1)} collective-permute-done((f32[20864]{0:T(1024)S(1)}, f32[20864]{0:T(1024)S(1)}, u32[]{:S(2)}, u32[]{:S(2)}) %collective-permute-start.22) | collective-permute-done | bytes 83488 | tf_op jit(solution)/shard_map/ppermute | solution.py:23
  176.6 1.9 collective-permute-start.23
  178.6 4.6 %collective-permute-done.23 = f32[20864]{0:T(1024)S(1)} collective-permute-done((f32[20864]{0:T(1024)S(1)}, f32[20864]{0:T(1024)S(1)}, u32[]{:S(2)}, u32[]{:S(2)}) %collective-permute-start.23) | collective-permute-done | bytes 83488 | tf_op jit(solution)/shard_map/ppermute | solution.py:23
  183.2 4.4 %collective-permute-start.24 = (f32[20864]{0:T(1024)S(1)}, f32[20864]{0:T(1024)S(1)}, u32[]{:S(2)}, u32[]{:S(2)}) collective-permute-start(f32[20864]{0:T(1024)S(1)} %add.548), channel_id=1, source_target_pairs={{0,256},{1,257},{2,258},{3,259},{4,260},{5,261},{6,262},{7,263},{8... | collective-permute-start | bytes 250376 | tf_op jit(solution)/shard_map/ppermute | solution.py:23
  187.8 5.5 %collective-permute-done.24 = f32[20864]{0:T(1024)S(1)} collective-permute-done((f32[20864]{0:T(1024)S(1)}, f32[20864]{0:T(1024)S(1)}, u32[]{:S(2)}, u32[]{:S(2)}) %collective-permute-start.24) | collective-permute-done | bytes 83488 | tf_op jit(solution)/shard_map/ppermute | solution.py:23
  193.2 2.5 %collective-permute-start.25 = (f32[20864]{0:T(1024)S(1)}, f32[20864]{0:T(1024)S(1)}, u32[]{:S(2)}, u32[]{:S(2)}) collective-permute-start(f32[20864]{0:T(1024)S(1)} %add.549), channel_id=1, source_target_pairs={{0,4},{1,5},{2,6},{3,7},{4,0},{5,1},{6,2},{7,3},{8,12},{9,13},{10,... | collective-permute-start | bytes 250376 | tf_op jit(solution)/shard_map/ppermute | solution.py:23
  196.5 3.8 %collective-permute-done.25 = f32[20864]{0:T(1024)S(1)} collective-permute-done((f32[20864]{0:T(1024)S(1)}, f32[20864]{0:T(1024)S(1)}, u32[]{:S(2)}, u32[]{:S(2)}) %collective-permute-start.25) | collective-permute-done | bytes 83488 | tf_op jit(solution)/shard_map/ppermute | solution.py:23
  200.3 2.0 collective-permute-start.26
  202.4 4.0 %collective-permute-done.26 = f32[41728]{0:T(1024)S(1)} collective-permute-done((f32[41728]{0:T(1024)S(1)}, f32[41728]{0:T(1024)S(1)}, u32[]{:S(2)}, u32[]{:S(2)}) %collective-permute-start.26) | collective-permute-done | bytes 166944 | tf_op jit(solution)/shard_map/ppermute | solution.py:23
  206.5 13.5 %collective-permute-start.27 = (f32[83456]{0:T(1024)S(1)}, f32[83456]{0:T(1024)S(1)}, u32[]{:S(2)}, u32[]{:S(2)}) collective-permute-start(f32[83456]{0:T(1024)S(1)} %maximum_select_fusion.1), channel_id=1, source_target_pairs={{0,1},{1,0},{2,3},{3,2},{4,5},{5,4},{6,7},{7,6},{8,9},{9,8},{10,11... | collective-permute-start | bytes 1001480 | tf_op jit(solution)/shard_map/ppermute | solution.py:23
  220.2 0.8 fusion.14
  221.9 0.9 mul.198
  222.8 0.9 mul.196
  (255 shorter events, 27.5 us)
Async XLA Ops:
  1.3 0.9 copy-start.3
  2.8 0.9 copy-start.1
  5.9 50.4 %collective-permute-start.3 = (bf16[8,96]{1,0:T(8,128)(2,1)S(1)}, bf16[8,96]{1,0:T(8,128)(2,1)S(1)}, u32[]{:S(2)}, u32[]{:S(2)}) collective-permute-start(bf16[8,96]{1,0:T(8,128)(2,1)S(1)} %concatenate.104), channel_id=1, source_target_pairs={{503,0},{504,1},{505,2},{506,3},{507,4},{508,5},{509,6},{510,7},{5... | collective-permute-start | bytes 4616 | tf_op jit(solution)/shard_map/ppermute | solution.py:18
  18.0 36.4 %collective-permute-start.2 = (bf16[8,96]{1,0:T(8,128)(2,1)S(1)}, bf16[8,96]{1,0:T(8,128)(2,1)S(1)}, u32[]{:S(2)}, u32[]{:S(2)}) collective-permute-start(bf16[8,96]{1,0:T(8,128)(2,1)S(1)} %concatenate.104), channel_id=1, source_target_pairs={{7,0},{8,1},{9,2},{10,3},{11,4},{12,5},{13,6},{14,7},{15,8},{16,9}... | collective-permute-start | bytes 4616 | tf_op jit(solution)/shard_map/ppermute | solution.py:18
  25.0 27.4 %collective-permute-start.1 = (bf16[8,96]{1,0:T(8,128)(2,1)S(1)}, bf16[8,96]{1,0:T(8,128)(2,1)S(1)}, u32[]{:S(2)}, u32[]{:S(2)}) collective-permute-start(bf16[8,96]{1,0:T(8,128)(2,1)S(1)} %concatenate.104), channel_id=1, source_target_pairs={{9,0},{10,1},{11,2},{12,3},{13,4},{14,5},{15,6},{16,7},{17,8},{18,... | collective-permute-start | bytes 4616 | tf_op jit(solution)/shard_map/ppermute | solution.py:18
  32.6 12.1 %collective-permute-start = (bf16[8,96]{1,0:T(8,128)(2,1)S(1)}, bf16[8,96]{1,0:T(8,128)(2,1)S(1)}, u32[]{:S(2)}, u32[]{:S(2)}) collective-permute-start(bf16[8,96]{1,0:T(8,128)(2,1)S(1)} %concatenate.104), channel_id=1, source_target_pairs={{505,0},{506,1},{507,2},{508,3},{509,4},{510,5},{511,6},{0,7},{1,8... | collective-permute-start | bytes 4616 | tf_op jit(solution)/shard_map/ppermute | solution.py:18
  34.6 32.9 %collective-permute-start.7 = (bf16[8,96,16]{1,2,0:T(8,128)(2,1)S(1)}, bf16[8,96,16]{1,2,0:T(8,128)(2,1)S(1)}, u32[]{:S(2)}, u32[]{:S(2)}) collective-permute-start(bf16[8,96,16]{1,2,0:T(8,128)(2,1)S(1)} %constant_dynamic-update-slice_fusion.4), channel_id=1, source_target_pairs={{511,0},{0,1},{1,2},{2,3},{3,4},{4,5},{5,6},{6,7},{7,8},{8,9},{9,1... | collective-permute-start | bytes 73736 | tf_op jit(solution)/shard_map/ppermute | solution.py:18
  36.6 0.7 copy-start.6
  37.3 0.7 copy-start.4
  37.3 0.7 copy-start.5
  37.9 0.7 copy-start.10
  38.8 0.7 copy-start.9
  39.5 0.7 copy-start.7
  44.7 22.8 %collective-permute-start.6 = (bf16[8,96,16]{1,2,0:T(8,128)(2,1)S(1)}, bf16[8,96,16]{1,2,0:T(8,128)(2,1)S(1)}, u32[]{:S(2)}, u32[]{:S(2)}) collective-permute-start(bf16[8,96,16]{1,2,0:T(8,128)(2,1)S(1)} %constant_dynamic-update-slice_fusion.4), channel_id=1, source_target_pairs={{8,0},{9,1},{10,2},{11,3},{12,4},{13,5},{14,6},{15,7},{16,8},{17,9... | collective-permute-start | bytes 73736 | tf_op jit(solution)/shard_map/ppermute | solution.py:18
  52.4 15.1 %collective-permute-start.5 = (bf16[8,96,16]{1,2,0:T(8,128)(2,1)S(1)}, bf16[8,96,16]{1,2,0:T(8,128)(2,1)S(1)}, u32[]{:S(2)}, u32[]{:S(2)}) collective-permute-start(bf16[8,96,16]{1,2,0:T(8,128)(2,1)S(1)} %constant_dynamic-update-slice_fusion.4), channel_id=1, source_target_pairs={{1,0},{2,1},{3,2},{4,3},{5,4},{6,5},{7,6},{8,7},{9,8},{10,9},{11,1... | collective-permute-start | bytes 73736 | tf_op jit(solution)/shard_map/ppermute | solution.py:18
  54.4 13.1 %collective-permute-start.4 = (bf16[8,96,16]{1,2,0:T(8,128)(2,1)S(1)}, bf16[8,96,16]{1,2,0:T(8,128)(2,1)S(1)}, u32[]{:S(2)}, u32[]{:S(2)}) collective-permute-start(bf16[8,96,16]{1,2,0:T(8,128)(2,1)S(1)} %constant_dynamic-update-slice_fusion.4), channel_id=1, source_target_pairs={{504,0},{505,1},{506,2},{507,3},{508,4},{509,5},{510,6},{511,7},{0... | collective-permute-start | bytes 73736 | tf_op jit(solution)/shard_map/ppermute | solution.py:18
  69.3 0.9 copy-start.2
  71.6 0.7 copy-start.8
  75.9 41.8 %collective-permute-start.11 = (bf16[8,96]{1,0:T(8,128)(2,1)S(1)}, bf16[8,96]{1,0:T(8,128)(2,1)S(1)}, u32[]{:S(2)}, u32[]{:S(2)}) collective-permute-start(bf16[8,96]{1,0:T(8,128)(2,1)S(1)} %concatenate.116), channel_id=1, source_target_pairs={{503,0},{504,1},{505,2},{506,3},{507,4},{508,5},{509,6},{510,7},{5... | collective-permute-start | bytes 4616 | tf_op jit(solution)/shard_map/ppermute | solution.py:18
  77.8 35.0 %collective-permute-start.10 = (bf16[8,96]{1,0:T(8,128)(2,1)S(1)}, bf16[8,96]{1,0:T(8,128)(2,1)S(1)}, u32[]{:S(2)}, u32[]{:S(2)}) collective-permute-start(bf16[8,96]{1,0:T(8,128)(2,1)S(1)} %concatenate.116), channel_id=1, source_target_pairs={{7,0},{8,1},{9,2},{10,3},{11,4},{12,5},{13,6},{14,7},{15,8},{16,9}... | collective-permute-start | bytes 4616 | tf_op jit(solution)/shard_map/ppermute | solution.py:18
  89.3 20.8 %collective-permute-start.9 = (bf16[8,96]{1,0:T(8,128)(2,1)S(1)}, bf16[8,96]{1,0:T(8,128)(2,1)S(1)}, u32[]{:S(2)}, u32[]{:S(2)}) collective-permute-start(bf16[8,96]{1,0:T(8,128)(2,1)S(1)} %concatenate.116), channel_id=1, source_target_pairs={{9,0},{10,1},{11,2},{12,3},{13,4},{14,5},{15,6},{16,7},{17,8},{18,... | collective-permute-start | bytes 4616 | tf_op jit(solution)/shard_map/ppermute | solution.py:18
  91.5 13.0 %collective-permute-start.8 = (bf16[8,96]{1,0:T(8,128)(2,1)S(1)}, bf16[8,96]{1,0:T(8,128)(2,1)S(1)}, u32[]{:S(2)}, u32[]{:S(2)}) collective-permute-start(bf16[8,96]{1,0:T(8,128)(2,1)S(1)} %concatenate.116), channel_id=1, source_target_pairs={{505,0},{506,1},{507,2},{508,3},{509,4},{510,5},{511,6},{0,7},{1,8... | collective-permute-start | bytes 4616 | tf_op jit(solution)/shard_map/ppermute | solution.py:18
  98.6 27.3 %collective-permute-start.15 = (bf16[8,96,16]{1,2,0:T(8,128)(2,1)S(1)}, bf16[8,96,16]{1,2,0:T(8,128)(2,1)S(1)}, u32[]{:S(2)}, u32[]{:S(2)}) collective-permute-start(bf16[8,96,16]{1,2,0:T(8,128)(2,1)S(1)} %constant_dynamic-update-slice_fusion.20), channel_id=1, source_target_pairs={{511,0},{0,1},{1,2},{2,3},{3,4},{4,5},{5,6},{6,7},{7,8},{8,9},{9,1... | collective-permute-start | bytes 73736 | tf_op jit(solution)/shard_map/ppermute | solution.py:18
  104.5 21.4 %collective-permute-start.14 = (bf16[8,96,16]{1,2,0:T(8,128)(2,1)S(1)}, bf16[8,96,16]{1,2,0:T(8,128)(2,1)S(1)}, u32[]{:S(2)}, u32[]{:S(2)}) collective-permute-start(bf16[8,96,16]{1,2,0:T(8,128)(2,1)S(1)} %constant_dynamic-update-slice_fusion.20), channel_id=1, source_target_pairs={{8,0},{9,1},{10,2},{11,3},{12,4},{13,5},{14,6},{15,7},{16,8},{17,9... | collective-permute-start | bytes 73736 | tf_op jit(solution)/shard_map/ppermute | solution.py:18
  110.1 15.7 %collective-permute-start.13 = (bf16[8,96,16]{1,2,0:T(8,128)(2,1)S(1)}, bf16[8,96,16]{1,2,0:T(8,128)(2,1)S(1)}, u32[]{:S(2)}, u32[]{:S(2)}) collective-permute-start(bf16[8,96,16]{1,2,0:T(8,128)(2,1)S(1)} %constant_dynamic-update-slice_fusion.20), channel_id=1, source_target_pairs={{1,0},{2,1},{3,2},{4,3},{5,4},{6,5},{7,6},{8,7},{9,8},{10,9},{11,1... | collective-permute-start | bytes 73736 | tf_op jit(solution)/shard_map/ppermute | solution.py:18
  112.8 13.0 %collective-permute-start.12 = (bf16[8,96,16]{1,2,0:T(8,128)(2,1)S(1)}, bf16[8,96,16]{1,2,0:T(8,128)(2,1)S(1)}, u32[]{:S(2)}, u32[]{:S(2)}) collective-permute-start(bf16[8,96,16]{1,2,0:T(8,128)(2,1)S(1)} %constant_dynamic-update-slice_fusion.20), channel_id=1, source_target_pairs={{504,0},{505,1},{506,2},{507,3},{508,4},{509,5},{510,6},{511,7},{0... | collective-permute-start | bytes 73736 | tf_op jit(solution)/shard_map/ppermute | solution.py:18
  127.5 0.8 copy-start
  130.4 4.4 %collective-permute-start.16 = (f32[83456]{0:T(1024)S(1)}, f32[83456]{0:T(1024)S(1)}, u32[]{:S(2)}, u32[]{:S(2)}) collective-permute-start(f32[83456]{0:T(1024)S(1)} %broadcast_select_fusion), channel_id=1, source_target_pairs={{0,1},{1,0},{2,3},{3,2},{4,5},{5,4},{6,7},{7,6},{8,9},{9,8},{10,11... | collective-permute-start | bytes 1001480 | tf_op jit(solution)/shard_map/ppermute | solution.py:23
  135.0 7.4 %collective-permute-start.17 = (f32[41728]{0:T(1024)S(1)}, f32[41728]{0:T(1024)S(1)}, u32[]{:S(2)}, u32[]{:S(2)}) collective-permute-start(f32[41728]{0:T(1024)S(1)} %slice_select_fusion), channel_id=1, source_target_pairs={{0,2},{1,3},{2,0},{3,1},{4,6},{5,7},{6,4},{7,5},{8,10},{9,11},{10,... | collective-permute-start | bytes 500744 | tf_op jit(solution)/shard_map/ppermute | solution.py:23
  142.4 7.5 %collective-permute-start.18 = (f32[20864]{0:T(1024)S(1)}, f32[20864]{0:T(1024)S(1)}, u32[]{:S(2)}, u32[]{:S(2)}) collective-permute-start(f32[20864]{0:T(1024)S(1)} %slice_select_fusion.1), channel_id=1, source_target_pairs={{0,4},{1,5},{2,6},{3,7},{4,0},{5,1},{6,2},{7,3},{8,12},{9,13},{10,... | collective-permute-start | bytes 250376 | tf_op jit(solution)/shard_map/ppermute | solution.py:23
  149.9 9.1 %collective-permute-start.19 = (f32[20864]{0:T(1024)S(1)}, f32[20864]{0:T(1024)S(1)}, u32[]{:S(2)}, u32[]{:S(2)}) collective-permute-start(f32[20864]{0:T(1024)S(1)} %select_add_fusion.2), channel_id=1, source_target_pairs={{0,8},{1,9},{2,10},{3,11},{4,12},{5,13},{6,14},{7,15},{8,0},{9,1},... | collective-permute-start | bytes 250376 | tf_op jit(solution)/shard_map/ppermute | solution.py:23
  159.1 5.2 %collective-permute-start.20 = (f32[20864]{0:T(1024)S(1)}, f32[20864]{0:T(1024)S(1)}, u32[]{:S(2)}, u32[]{:S(2)}) collective-permute-start(f32[20864]{0:T(1024)S(1)} %add.544), channel_id=1, source_target_pairs={{0,16},{1,17},{2,18},{3,19},{4,20},{5,21},{6,22},{7,23},{8,24},{9,... | collective-permute-start | bytes 250376 | tf_op jit(solution)/shard_map/ppermute | solution.py:23
  164.3 6.7 %collective-permute-start.21 = (f32[20864]{0:T(1024)S(1)}, f32[20864]{0:T(1024)S(1)}, u32[]{:S(2)}, u32[]{:S(2)}) collective-permute-start(f32[20864]{0:T(1024)S(1)} %add.545), channel_id=1, source_target_pairs={{0,32},{1,33},{2,34},{3,35},{4,36},{5,37},{6,38},{7,39},{8,40},{9,... | collective-permute-start | bytes 250376 | tf_op jit(solution)/shard_map/ppermute | solution.py:23
  171.1 5.5 %collective-permute-start.22 = (f32[20864]{0:T(1024)S(1)}, f32[20864]{0:T(1024)S(1)}, u32[]{:S(2)}, u32[]{:S(2)}) collective-permute-start(f32[20864]{0:T(1024)S(1)} %add.546), channel_id=1, source_target_pairs={{0,64},{1,65},{2,66},{3,67},{4,68},{5,69},{6,70},{7,71},{8,72},{9,... | collective-permute-start | bytes 250376 | tf_op jit(solution)/shard_map/ppermute | solution.py:23
  176.6 6.6 %collective-permute-start.23 = (f32[20864]{0:T(1024)S(1)}, f32[20864]{0:T(1024)S(1)}, u32[]{:S(2)}, u32[]{:S(2)}) collective-permute-start(f32[20864]{0:T(1024)S(1)} %add.547), channel_id=1, source_target_pairs={{0,128},{1,129},{2,130},{3,131},{4,132},{5,133},{6,134},{7,135},{8... | collective-permute-start | bytes 250376 | tf_op jit(solution)/shard_map/ppermute | solution.py:23
  183.2 10.0 %collective-permute-start.24 = (f32[20864]{0:T(1024)S(1)}, f32[20864]{0:T(1024)S(1)}, u32[]{:S(2)}, u32[]{:S(2)}) collective-permute-start(f32[20864]{0:T(1024)S(1)} %add.548), channel_id=1, source_target_pairs={{0,256},{1,257},{2,258},{3,259},{4,260},{5,261},{6,262},{7,263},{8... | collective-permute-start | bytes 250376 | tf_op jit(solution)/shard_map/ppermute | solution.py:23
  193.2 7.0 %collective-permute-start.25 = (f32[20864]{0:T(1024)S(1)}, f32[20864]{0:T(1024)S(1)}, u32[]{:S(2)}, u32[]{:S(2)}) collective-permute-start(f32[20864]{0:T(1024)S(1)} %add.549), channel_id=1, source_target_pairs={{0,4},{1,5},{2,6},{3,7},{4,0},{5,1},{6,2},{7,3},{8,12},{9,13},{10,... | collective-permute-start | bytes 250376 | tf_op jit(solution)/shard_map/ppermute | solution.py:23
  200.3 6.1 %collective-permute-start.26 = (f32[41728]{0:T(1024)S(1)}, f32[41728]{0:T(1024)S(1)}, u32[]{:S(2)}, u32[]{:S(2)}) collective-permute-start(f32[41728]{0:T(1024)S(1)} %maximum_select_fusion.2), channel_id=1, source_target_pairs={{0,2},{1,3},{2,0},{3,1},{4,6},{5,7},{6,4},{7,5},{8,10},{9,11},{10,... | collective-permute-start | bytes 500744 | tf_op jit(solution)/shard_map/ppermute | solution.py:23
  206.5 14.8 %collective-permute-start.27 = (f32[83456]{0:T(1024)S(1)}, f32[83456]{0:T(1024)S(1)}, u32[]{:S(2)}, u32[]{:S(2)}) collective-permute-start(f32[83456]{0:T(1024)S(1)} %maximum_select_fusion.1), channel_id=1, source_target_pairs={{0,1},{1,0},{2,3},{3,2},{4,5},{5,4},{6,7},{7,6},{8,9},{9,8},{10,11... | collective-permute-start | bytes 1001480 | tf_op jit(solution)/shard_map/ppermute | solution.py:23

commit v3 on v2

--- a/solution.py
+++ b/solution.py
@@ -85,6 +85,12 @@
     return (matches, classes)
 
 
+def corner_row(corners, width):
+    block = jnp.transpose(corners, (1, 0))
+    block = jnp.pad(block, ((0, 0), (0, width - block.shape[1])))
+    return block[None]
+
+
 def exchange_groups(strip_groups, corner_groups, tile_links):
     neighbour_ids, edge_codes, corner_ids, corner_codes = tile_links
     row_length = TILE_ROW
@@ -93,19 +99,36 @@
     _, edge_class = offset_class(neighbour_ids, edge_offsets)
     _, diag_class = offset_class(corner_ids, diag_offsets)
     groups = len(strip_groups)
+    n_strips = 4 * groups
     strips = jnp.concatenate(strip_groups, axis=0)
     corners = jnp.concatenate(corner_groups, axis=0)
-    received = [passed_along(strips, "tiles", -edge_offsets[d]) for d in range(4)]
-    stacked = jnp.concatenate(received, axis=0)
-    corner_recv = [passed_along(corners, "tiles", -diag_offsets[d]) for d in range(4)]
-    corner_stack = jnp.concatenate(corner_recv, axis=0)
+    width = strips.shape[2]
+    payload_a = jnp.concatenate([strips, corner_row(corners, width)], axis=0)
+    from_next = passed_along(payload_a, "tiles", -1)
+    from_prev = passed_along(payload_a, "tiles", 1)
+    corners_next = jnp.transpose(from_next[n_strips, :, :n_strips], (1, 0))
+    corners_prev = jnp.transpose(from_prev[n_strips, :, :n_strips], (1, 0))
+    relay = jnp.concatenate([corners_next, corners_prev], axis=0)
+    payload_b = jnp.concatenate([strips, corner_row(relay, width)], axis=0)
+    from_up = passed_along(payload_b, "tiles", row_length)
+    from_down = passed_along(payload_b, "tiles", -row_length)
+    stacked = jnp.concatenate(
+        [from_up[:n_strips], from_next[:n_strips], from_down[:n_strips], from_prev[:n_strips]],
+        axis=0,
+    )
+    up_relay = jnp.transpose(from_up[n_strips, :, : 2 * n_strips], (1, 0))
+    down_relay = jnp.transpose(from_down[n_strips, :, : 2 * n_strips], (1, 0))
+    corner_stack = jnp.concatenate(
+        [up_relay[:n_strips], down_relay[:n_strips], down_relay[n_strips:], up_relay[n_strips:]],
+        axis=0,
+    )
     reverse = (edge_codes >= 4)[:, None, None]
     their_side = edge_codes % 4
     out = []
     for g in range(groups):
-        picked = stacked[edge_class * (4 * groups) + 4 * g + their_side]
+        picked = stacked[edge_class * n_strips + 4 * g + their_side]
         picked = jnp.where(reverse, picked[:, :, ::-1], picked)
-        corner_got = corner_stack[diag_class * (4 * groups) + 4 * g + corner_codes]
+        corner_got = corner_stack[diag_class * n_strips + 4 * g + corner_codes]
         out.append((picked, corner_got))
     return out
 

time: 225 us -> 189 us (0.84)
  starting transfers between devices: 124 us -> 93.6 us
  waiting for transfers between devices: 64.6 us -> 59.2 us
    ppermute x16 -> x8, starting transfers between devices: 82.1 us -> 50.7 us  [passed_along(): return lax.ppermute(block, axis, route)]
    ppermute x16 -> x8, waiting for transfers between devices: 20.4 us -> 11.9 us  [passed_along(): return lax.ppermute(block, axis, route)]
    ppermute x12, waiting for transfers between devices: 44.2 us -> 47.3 us  [xor_partner(): lax.ppermute(block, 'tiles', [(i, i ^ distance) for i in range(devices)])]
    unnamed x51 -> x53, local copies, waits for them, and re-layouts: 8.21 us -> 8.69 us
  transfers between devices with their start and end apart: 28 -> 20, of which waited for: 15 -> 14; matrix products, arithmetic and copies ran while one was open for 4% -> 3% of each run, Pallas kernels for 0% -> 0%
where the time goes in v3:
time: 189 us; the launch traced here: 188 us
  starting transfers between devices  93.6 us (50%)
  waiting for transfers between devices  59.2 us (31%)
  local copies, waits for them, and re-layouts  20.4 us (11%)
  matrix products  10.5 us (6%)
  other arithmetic  2.64 us (1%)
  between operations  2.03 us (1%)
    ppermute x8, starting transfers between devices, passed_along(): return lax.ppermute(block, axis, route)  50.7 us
    ppermute x12, waiting for transfers between devices, xor_partner(): lax.ppermute(block, 'tiles', [(i, i ^ distance) for i in range(devices)])  47.3 us
    ppermute x12, starting transfers between devices, xor_partner(): lax.ppermute(block, 'tiles', [(i, i ^ distance) for i in range(devices)])  42.9 us
    ppermute x8, waiting for transfers between devices, passed_along(): return lax.ppermute(block, axis, route)  11.9 us
    unnamed x53, local copies, waits for them, and re-layouts  8.69 us
    dot_general x18, matrix products, spread_back(): lax.dot_general(weights[tap_index], window, (((0,), (0,)), ((), ())), pre...  3.9 us
  transfers between devices with their start and end apart: 20, of which 14 were waited for; matrix products, arithmetic and copies ran while one was open for 3% of the time, Pallas kernels for 0%

profile of v3, /device:TPU:1, one launch (start us, length us, event | category | flops | bytes accessed | tf_op | source)
XLA Modules:
  0.0 188.3 jit_solution(7143029643115672263)
XLA Ops:
  0.6 0.9 copy.88
  2.2 0.9 copy-done.1
  6.1 5.4 %collective-permute-start.1 = (bf16[9,96,16]{1,2,0:T(8,128)(2,1)S(1)}, bf16[9,96,16]{1,2,0:T(8,128)(2,1)S(1)}, u32[]{:S(2)}, u32[]{:S(2)}) collective-permute-start(bf16[9,96,16]{1,2,0:T(8,128)(2,1)S(1)} %constant_dynamic-update-slice_fusion), channel_id=1, source_target_pairs={{511,0},{0,1},{1,2},{2,3},{3,4},{4,5},{5,6},{6,7},{7,8},{8,9},{9,1... | collective-permute-start | bytes 82952 | tf_op jit(solution)/shard_map/ppermute | solution.py:18
  11.5 5.3 %collective-permute-start = (bf16[9,96,16]{1,2,0:T(8,128)(2,1)S(1)}, bf16[9,96,16]{1,2,0:T(8,128)(2,1)S(1)}, u32[]{:S(2)}, u32[]{:S(2)}) collective-permute-start(bf16[9,96,16]{1,2,0:T(8,128)(2,1)S(1)} %constant_dynamic-update-slice_fusion), channel_id=1, source_target_pairs={{1,0},{2,1},{3,2},{4,3},{5,4},{6,5},{7,6},{8,7},{9,8},{10,9},{11,1... | collective-permute-start | bytes 82952 | tf_op jit(solution)/shard_map/ppermute | solution.py:18
  16.8 0.6 copy-done.10
  17.5 0.6 copy-done.8
  18.2 0.6 copy-done.15
  19.1 0.6 copy-done.14
  20.5 6.4 %collective-permute-start.2 = (bf16[9,96,16]{1,2,0:T(8,128)(2,1)S(1)}, bf16[9,96,16]{1,2,0:T(8,128)(2,1)S(1)}, u32[]{:S(2)}, u32[]{:S(2)}) collective-permute-start(bf16[9,96,16]{1,2,0:T(8,128)(2,1)S(1)} %constant_dynamic-update-slice_fusion.9), channel_id=1, source_target_pairs={{504,0},{505,1},{506,2},{507,3},{508,4},{509,5},{510,6},{511,7},{0... | collective-permute-start | bytes 82952 | tf_op jit(solution)/shard_map/ppermute | solution.py:18
  27.1 7.0 %collective-permute-start.3 = (bf16[9,96,16]{1,2,0:T(8,128)(2,1)S(1)}, bf16[9,96,16]{1,2,0:T(8,128)(2,1)S(1)}, u32[]{:S(2)}, u32[]{:S(2)}) collective-permute-start(bf16[9,96,16]{1,2,0:T(8,128)(2,1)S(1)} %constant_dynamic-update-slice_fusion.9), channel_id=1, source_target_pairs={{8,0},{9,1},{10,2},{11,3},{12,4},{13,5},{14,6},{15,7},{16,8},{17,9... | collective-permute-start | bytes 82952 | tf_op jit(solution)/shard_map/ppermute | solution.py:18
  34.1 1.5 collective-permute-done.3
  37.0 0.7 slice-done
  39.1 0.7 scatter_fusion
  40.4 0.9 copy-done.2
  43.2 0.6 copy-done.13
  47.7 5.3 %collective-permute-start.5 = (bf16[9,96,16]{1,2,0:T(8,128)(2,1)S(1)}, bf16[9,96,16]{1,2,0:T(8,128)(2,1)S(1)}, u32[]{:S(2)}, u32[]{:S(2)}) collective-permute-start(bf16[9,96,16]{1,2,0:T(8,128)(2,1)S(1)} %constant_dynamic-update-slice_fusion.18), channel_id=1, source_target_pairs={{511,0},{0,1},{1,2},{2,3},{3,4},{4,5},{5,6},{6,7},{7,8},{8,9},{9,1... | collective-permute-start | bytes 82952 | tf_op jit(solution)/shard_map/ppermute | solution.py:18
  53.0 7.3 %collective-permute-start.4 = (bf16[9,96,16]{1,2,0:T(8,128)(2,1)S(1)}, bf16[9,96,16]{1,2,0:T(8,128)(2,1)S(1)}, u32[]{:S(2)}, u32[]{:S(2)}) collective-permute-start(bf16[9,96,16]{1,2,0:T(8,128)(2,1)S(1)} %constant_dynamic-update-slice_fusion.18), channel_id=1, source_target_pairs={{1,0},{2,1},{3,2},{4,3},{5,4},{6,5},{7,6},{8,7},{9,8},{10,9},{11,1... | collective-permute-start | bytes 82952 | tf_op jit(solution)/shard_map/ppermute | solution.py:18
  61.4 12.1 %collective-permute-start.7 = (bf16[9,96,16]{1,2,0:T(8,128)(2,1)S(1)}, bf16[9,96,16]{1,2,0:T(8,128)(2,1)S(1)}, u32[]{:S(2)}, u32[]{:S(2)}) collective-permute-start(bf16[9,96,16]{1,2,0:T(8,128)(2,1)S(1)} %constant_dynamic-update-slice_fusion.27), channel_id=1, source_target_pairs={{8,0},{9,1},{10,2},{11,3},{12,4},{13,5},{14,6},{15,7},{16,8},{17,9... | collective-permute-start | bytes 82952 | tf_op jit(solution)/shard_map/ppermute | solution.py:18
  73.5 1.9 %collective-permute-start.6 = (bf16[9,96,16]{1,2,0:T(8,128)(2,1)S(1)}, bf16[9,96,16]{1,2,0:T(8,128)(2,1)S(1)}, u32[]{:S(2)}, u32[]{:S(2)}) collective-permute-start(bf16[9,96,16]{1,2,0:T(8,128)(2,1)S(1)} %constant_dynamic-update-slice_fusion.27), channel_id=1, source_target_pairs={{504,0},{505,1},{506,2},{507,3},{508,4},{509,5},{510,6},{511,7},{0... | collective-permute-start | bytes 82952 | tf_op jit(solution)/shard_map/ppermute | solution.py:18
  75.9 10.4 %collective-permute-done.6 = bf16[9,96,16]{1,2,0:T(8,128)(2,1)S(1)} collective-permute-done((bf16[9,96,16]{1,2,0:T(8,128)(2,1)S(1)}, bf16[9,96,16]{1,2,0:T(8,128)(2,1)S(1)}, u32[]{:S(2)}, u32[]{:S(2)}) %collective-permute-start.6) | collective-permute-done | bytes 27680 | tf_op jit(solution)/shard_map/ppermute | solution.py:18
  91.2 6.8 %collective-permute-start.8 = (f32[83456]{0:T(1024)S(1)}, f32[83456]{0:T(1024)S(1)}, u32[]{:S(2)}, u32[]{:S(2)}) collective-permute-start(f32[83456]{0:T(1024)S(1)} %broadcast_select_fusion), channel_id=1, source_target_pairs={{0,1},{1,0},{2,3},{3,2},{4,5},{5,4},{6,7},{7,6},{8,9},{9,8},{10,11... | collective-permute-start | bytes 1001480 | tf_op jit(solution)/shard_map/ppermute | solution.py:23
  98.3 0.9 collective-permute-done.8
  99.3 1.9 %collective-permute-start.9 = (f32[41728]{0:T(1024)S(1)}, f32[41728]{0:T(1024)S(1)}, u32[]{:S(2)}, u32[]{:S(2)}) collective-permute-start(f32[41728]{0:T(1024)S(1)} %slice_select_fusion), channel_id=1, source_target_pairs={{0,2},{1,3},{2,0},{3,1},{4,6},{5,7},{6,4},{7,5},{8,10},{9,11},{10,... | collective-permute-start | bytes 500744 | tf_op jit(solution)/shard_map/ppermute | solution.py:23
  101.4 5.3 %collective-permute-done.9 = f32[41728]{0:T(1024)S(1)} collective-permute-done((f32[41728]{0:T(1024)S(1)}, f32[41728]{0:T(1024)S(1)}, u32[]{:S(2)}, u32[]{:S(2)}) %collective-permute-start.9) | collective-permute-done | bytes 166944 | tf_op jit(solution)/shard_map/ppermute | solution.py:23
  106.7 4.0 %collective-permute-start.10 = (f32[20864]{0:T(1024)S(1)}, f32[20864]{0:T(1024)S(1)}, u32[]{:S(2)}, u32[]{:S(2)}) collective-permute-start(f32[20864]{0:T(1024)S(1)} %slice_select_fusion.1), channel_id=1, source_target_pairs={{0,4},{1,5},{2,6},{3,7},{4,0},{5,1},{6,2},{7,3},{8,12},{9,13},{10,... | collective-permute-start | bytes 250376 | tf_op jit(solution)/shard_map/ppermute | solution.py:23
  110.9 4.3 %collective-permute-done.10 = f32[20864]{0:T(1024)S(1)} collective-permute-done((f32[20864]{0:T(1024)S(1)}, f32[20864]{0:T(1024)S(1)}, u32[]{:S(2)}, u32[]{:S(2)}) %collective-permute-start.10) | collective-permute-done | bytes 83488 | tf_op jit(solution)/shard_map/ppermute | solution.py:23
  115.2 1.9 %collective-permute-start.11 = (f32[20864]{0:T(1024)S(1)}, f32[20864]{0:T(1024)S(1)}, u32[]{:S(2)}, u32[]{:S(2)}) collective-permute-start(f32[20864]{0:T(1024)S(1)} %select_add_fusion.2), channel_id=1, source_target_pairs={{0,8},{1,9},{2,10},{3,11},{4,12},{5,13},{6,14},{7,15},{8,0},{9,1},... | collective-permute-start | bytes 250376 | tf_op jit(solution)/shard_map/ppermute | solution.py:23
  117.7 6.9 %collective-permute-done.11 = f32[20864]{0:T(1024)S(1)} collective-permute-done((f32[20864]{0:T(1024)S(1)}, f32[20864]{0:T(1024)S(1)}, u32[]{:S(2)}, u32[]{:S(2)}) %collective-permute-start.11) | collective-permute-done | bytes 83488 | tf_op jit(solution)/shard_map/ppermute | solution.py:23
  124.7 1.9 %collective-permute-start.12 = (f32[20864]{0:T(1024)S(1)}, f32[20864]{0:T(1024)S(1)}, u32[]{:S(2)}, u32[]{:S(2)}) collective-permute-start(f32[20864]{0:T(1024)S(1)} %add.548), channel_id=1, source_target_pairs={{0,16},{1,17},{2,18},{3,19},{4,20},{5,21},{6,22},{7,23},{8,24},{9,... | collective-permute-start | bytes 250376 | tf_op jit(solution)/shard_map/ppermute | solution.py:23
  126.6 3.3 %collective-permute-done.12 = f32[20864]{0:T(1024)S(1)} collective-permute-done((f32[20864]{0:T(1024)S(1)}, f32[20864]{0:T(1024)S(1)}, u32[]{:S(2)}, u32[]{:S(2)}) %collective-permute-start.12) | collective-permute-done | bytes 83488 | tf_op jit(solution)/shard_map/ppermute | solution.py:23
  129.9 1.9 %collective-permute-start.13 = (f32[20864]{0:T(1024)S(1)}, f32[20864]{0:T(1024)S(1)}, u32[]{:S(2)}, u32[]{:S(2)}) collective-permute-start(f32[20864]{0:T(1024)S(1)} %add.549), channel_id=1, source_target_pairs={{0,32},{1,33},{2,34},{3,35},{4,36},{5,37},{6,38},{7,39},{8,40},{9,... | collective-permute-start | bytes 250376 | tf_op jit(solution)/shard_map/ppermute | solution.py:23
  131.9 4.8 %collective-permute-done.13 = f32[20864]{0:T(1024)S(1)} collective-permute-done((f32[20864]{0:T(1024)S(1)}, f32[20864]{0:T(1024)S(1)}, u32[]{:S(2)}, u32[]{:S(2)}) %collective-permute-start.13) | collective-permute-done | bytes 83488 | tf_op jit(solution)/shard_map/ppermute | solution.py:23
  136.7 1.9 %collective-permute-start.14 = (f32[20864]{0:T(1024)S(1)}, f32[20864]{0:T(1024)S(1)}, u32[]{:S(2)}, u32[]{:S(2)}) collective-permute-start(f32[20864]{0:T(1024)S(1)} %add.550), channel_id=1, source_target_pairs={{0,64},{1,65},{2,66},{3,67},{4,68},{5,69},{6,70},{7,71},{8,72},{9,... | collective-permute-start | bytes 250376 | tf_op jit(solution)/shard_map/ppermute | solution.py:23
  138.6 3.3 %collective-permute-done.14 = f32[20864]{0:T(1024)S(1)} collective-permute-done((f32[20864]{0:T(1024)S(1)}, f32[20864]{0:T(1024)S(1)}, u32[]{:S(2)}, u32[]{:S(2)}) %collective-permute-start.14) | collective-permute-done | bytes 83488 | tf_op jit(solution)/shard_map/ppermute | solution.py:23
  141.9 1.9 %collective-permute-start.15 = (f32[20864]{0:T(1024)S(1)}, f32[20864]{0:T(1024)S(1)}, u32[]{:S(2)}, u32[]{:S(2)}) collective-permute-start(f32[20864]{0:T(1024)S(1)} %add.551), channel_id=1, source_target_pairs={{0,128},{1,129},{2,130},{3,131},{4,132},{5,133},{6,134},{7,135},{8... | collective-permute-start | bytes 250376 | tf_op jit(solution)/shard_map/ppermute | solution.py:23
  143.9 0.7 scatter_fusion.1
  144.6 4.1 %collective-permute-done.15 = f32[20864]{0:T(1024)S(1)} collective-permute-done((f32[20864]{0:T(1024)S(1)}, f32[20864]{0:T(1024)S(1)}, u32[]{:S(2)}, u32[]{:S(2)}) %collective-permute-start.15) | collective-permute-done | bytes 83488 | tf_op jit(solution)/shard_map/ppermute | solution.py:23
  148.7 4.4 %collective-permute-start.16 = (f32[20864]{0:T(1024)S(1)}, f32[20864]{0:T(1024)S(1)}, u32[]{:S(2)}, u32[]{:S(2)}) collective-permute-start(f32[20864]{0:T(1024)S(1)} %add.552), channel_id=1, source_target_pairs={{0,256},{1,257},{2,258},{3,259},{4,260},{5,261},{6,262},{7,263},{8... | collective-permute-start | bytes 250376 | tf_op jit(solution)/shard_map/ppermute | solution.py:23
  153.3 5.4 %collective-permute-done.16 = f32[20864]{0:T(1024)S(1)} collective-permute-done((f32[20864]{0:T(1024)S(1)}, f32[20864]{0:T(1024)S(1)}, u32[]{:S(2)}, u32[]{:S(2)}) %collective-permute-start.16) | collective-permute-done | bytes 83488 | tf_op jit(solution)/shard_map/ppermute | solution.py:23
  158.7 1.9 %collective-permute-start.17 = (f32[20864]{0:T(1024)S(1)}, f32[20864]{0:T(1024)S(1)}, u32[]{:S(2)}, u32[]{:S(2)}) collective-permute-start(f32[20864]{0:T(1024)S(1)} %add.553), channel_id=1, source_target_pairs={{0,4},{1,5},{2,6},{3,7},{4,0},{5,1},{6,2},{7,3},{8,12},{9,13},{10,... | collective-permute-start | bytes 250376 | tf_op jit(solution)/shard_map/ppermute | solution.py:23
  160.7 0.7 copy.119
  161.4 4.7 %collective-permute-done.17 = f32[20864]{0:T(1024)S(1)} collective-permute-done((f32[20864]{0:T(1024)S(1)}, f32[20864]{0:T(1024)S(1)}, u32[]{:S(2)}, u32[]{:S(2)}) %collective-permute-start.17) | collective-permute-done | bytes 83488 | tf_op jit(solution)/shard_map/ppermute | solution.py:23
  166.1 1.9 %collective-permute-start.18 = (f32[41728]{0:T(1024)S(1)}, f32[41728]{0:T(1024)S(1)}, u32[]{:S(2)}, u32[]{:S(2)}) collective-permute-start(f32[41728]{0:T(1024)S(1)} %maximum_select_fusion.2), channel_id=1, source_target_pairs={{0,2},{1,3},{2,0},{3,1},{4,6},{5,7},{6,4},{7,5},{8,10},{9,11},{10,... | collective-permute-start | bytes 500744 | tf_op jit(solution)/shard_map/ppermute | solution.py:23
  168.2 4.0 %collective-permute-done.18 = f32[41728]{0:T(1024)S(1)} collective-permute-done((f32[41728]{0:T(1024)S(1)}, f32[41728]{0:T(1024)S(1)}, u32[]{:S(2)}, u32[]{:S(2)}) %collective-permute-start.18) | collective-permute-done | bytes 166944 | tf_op jit(solution)/shard_map/ppermute | solution.py:23
  172.2 12.3 %collective-permute-start.19 = (f32[83456]{0:T(1024)S(1)}, f32[83456]{0:T(1024)S(1)}, u32[]{:S(2)}, u32[]{:S(2)}) collective-permute-start(f32[83456]{0:T(1024)S(1)} %maximum_select_fusion.1), channel_id=1, source_target_pairs={{0,1},{1,0},{2,3},{3,2},{4,5},{5,4},{6,7},{7,6},{8,9},{9,8},{10,11... | collective-permute-start | bytes 1001480 | tf_op jit(solution)/shard_map/ppermute | solution.py:23
  184.7 0.8 fusion.14
  186.4 0.9 mul.198
  187.4 0.9 mul.196
  (265 shorter events, 22.3 us)
Async XLA Ops:
  0.6 1.0 copy-start
  2.2 0.9 copy-start.1
  5.2 0.7 copy-start.12
  6.1 14.4 %collective-permute-start.1 = (bf16[9,96,16]{1,2,0:T(8,128)(2,1)S(1)}, bf16[9,96,16]{1,2,0:T(8,128)(2,1)S(1)}, u32[]{:S(2)}, u32[]{:S(2)}) collective-permute-start(bf16[9,96,16]{1,2,0:T(8,128)(2,1)S(1)} %constant_dynamic-update-slice_fusion), channel_id=1, source_target_pairs={{511,0},{0,1},{1,2},{2,3},{3,4},{4,5},{5,6},{6,7},{7,8},{8,9},{9,1... | collective-permute-start | bytes 82952 | tf_op jit(solution)/shard_map/ppermute | solution.py:18
  11.5 9.0 %collective-permute-start = (bf16[9,96,16]{1,2,0:T(8,128)(2,1)S(1)}, bf16[9,96,16]{1,2,0:T(8,128)(2,1)S(1)}, u32[]{:S(2)}, u32[]{:S(2)}) collective-permute-start(bf16[9,96,16]{1,2,0:T(8,128)(2,1)S(1)} %constant_dynamic-update-slice_fusion), channel_id=1, source_target_pairs={{1,0},{2,1},{3,2},{4,3},{5,4},{6,5},{7,6},{8,7},{9,8},{10,9},{11,1... | collective-permute-start | bytes 82952 | tf_op jit(solution)/shard_map/ppermute | solution.py:18
  16.8 0.7 copy-start.10
  17.5 0.7 copy-start.8
  17.5 0.7 copy-start.9
  18.2 0.7 copy-start.15
  19.1 0.7 copy-start.14
  19.7 0.7 copy-start.11
  20.5 13.6 %copy-start.4 = (bf16[9,96,16]{1,2,0:T(8,128)(2,1)}, bf16[9,96,16]{1,2,0:T(8,128)(2,1)S(1)}, u32[]{:S(2)}) copy-start(bf16[9,96,16]{1,2,0:T(8,128)(2,1)S(1)} %collective-permute-done.1) | copy-start | bytes 82948
  20.5 13.6 %copy-start.5 = (bf16[9,96,16]{1,2,0:T(8,128)(2,1)}, bf16[9,96,16]{1,2,0:T(8,128)(2,1)S(1)}, u32[]{:S(2)}) copy-start(bf16[9,96,16]{1,2,0:T(8,128)(2,1)S(1)} %collective-permute-done) | copy-start | bytes 82948
  20.5 13.6 %collective-permute-start.2 = (bf16[9,96,16]{1,2,0:T(8,128)(2,1)S(1)}, bf16[9,96,16]{1,2,0:T(8,128)(2,1)S(1)}, u32[]{:S(2)}, u32[]{:S(2)}) collective-permute-start(bf16[9,96,16]{1,2,0:T(8,128)(2,1)S(1)} %constant_dynamic-update-slice_fusion.9), channel_id=1, source_target_pairs={{504,0},{505,1},{506,2},{507,3},{508,4},{509,5},{510,6},{511,7},{0... | collective-permute-start | bytes 82952 | tf_op jit(solution)/shard_map/ppermute | solution.py:18
  27.1 8.6 %collective-permute-start.3 = (bf16[9,96,16]{1,2,0:T(8,128)(2,1)S(1)}, bf16[9,96,16]{1,2,0:T(8,128)(2,1)S(1)}, u32[]{:S(2)}, u32[]{:S(2)}) collective-permute-start(bf16[9,96,16]{1,2,0:T(8,128)(2,1)S(1)} %constant_dynamic-update-slice_fusion.9), channel_id=1, source_target_pairs={{8,0},{9,1},{10,2},{11,3},{12,4},{13,5},{14,6},{15,7},{16,8},{17,9... | collective-permute-start | bytes 82952 | tf_op jit(solution)/shard_map/ppermute | solution.py:18
  36.9 0.8 slice-start
  36.9 0.8 slice-start.1
  40.3 0.9 copy-start.2
  41.7 0.8 copy-start.3
  43.2 0.7 copy-start.13
  47.7 13.7 %collective-permute-start.5 = (bf16[9,96,16]{1,2,0:T(8,128)(2,1)S(1)}, bf16[9,96,16]{1,2,0:T(8,128)(2,1)S(1)}, u32[]{:S(2)}, u32[]{:S(2)}) collective-permute-start(bf16[9,96,16]{1,2,0:T(8,128)(2,1)S(1)} %constant_dynamic-update-slice_fusion.18), channel_id=1, source_target_pairs={{511,0},{0,1},{1,2},{2,3},{3,4},{4,5},{5,6},{6,7},{7,8},{8,9},{9,1... | collective-permute-start | bytes 82952 | tf_op jit(solution)/shard_map/ppermute | solution.py:18
  53.0 8.4 %collective-permute-start.4 = (bf16[9,96,16]{1,2,0:T(8,128)(2,1)S(1)}, bf16[9,96,16]{1,2,0:T(8,128)(2,1)S(1)}, u32[]{:S(2)}, u32[]{:S(2)}) collective-permute-start(bf16[9,96,16]{1,2,0:T(8,128)(2,1)S(1)} %constant_dynamic-update-slice_fusion.18), channel_id=1, source_target_pairs={{1,0},{2,1},{3,2},{4,3},{5,4},{6,5},{7,6},{8,7},{9,8},{10,9},{11,1... | collective-permute-start | bytes 82952 | tf_op jit(solution)/shard_map/ppermute | solution.py:18
  61.3 14.6 %copy-start.6 = (bf16[9,96,16]{1,2,0:T(8,128)(2,1)}, bf16[9,96,16]{1,2,0:T(8,128)(2,1)S(1)}, u32[]{:S(2)}) copy-start(bf16[9,96,16]{1,2,0:T(8,128)(2,1)S(1)} %collective-permute-done.5) | copy-start | bytes 82948
  61.4 14.5 %copy-start.7 = (bf16[9,96,16]{1,2,0:T(8,128)(2,1)}, bf16[9,96,16]{1,2,0:T(8,128)(2,1)S(1)}, u32[]{:S(2)}) copy-start(bf16[9,96,16]{1,2,0:T(8,128)(2,1)S(1)} %collective-permute-done.4) | copy-start | bytes 82948
  61.4 14.5 %collective-permute-start.7 = (bf16[9,96,16]{1,2,0:T(8,128)(2,1)S(1)}, bf16[9,96,16]{1,2,0:T(8,128)(2,1)S(1)}, u32[]{:S(2)}, u32[]{:S(2)}) collective-permute-start(bf16[9,96,16]{1,2,0:T(8,128)(2,1)S(1)} %constant_dynamic-update-slice_fusion.27), channel_id=1, source_target_pairs={{8,0},{9,1},{10,2},{11,3},{12,4},{13,5},{14,6},{15,7},{16,8},{17,9... | collective-permute-start | bytes 82952 | tf_op jit(solution)/shard_map/ppermute | solution.py:18
  73.5 12.8 %collective-permute-start.6 = (bf16[9,96,16]{1,2,0:T(8,128)(2,1)S(1)}, bf16[9,96,16]{1,2,0:T(8,128)(2,1)S(1)}, u32[]{:S(2)}, u32[]{:S(2)}) collective-permute-start(bf16[9,96,16]{1,2,0:T(8,128)(2,1)S(1)} %constant_dynamic-update-slice_fusion.27), channel_id=1, source_target_pairs={{504,0},{505,1},{506,2},{507,3},{508,4},{509,5},{510,6},{511,7},{0... | collective-permute-start | bytes 82952 | tf_op jit(solution)/shard_map/ppermute | solution.py:18
  75.9 10.4 %slice-start.2 = ((bf16[9,96,16]{1,2,0:T(8,128)(2,1)}), bf16[8,96,16]{1,2,0:T(8,128)(2,1)S(1)}, s32[]{:S(2)}) async-start(bf16[9,96,16]{1,2,0:T(8,128)(2,1)} %copy-done.6), calls=%async_computation.2 | async-start | bytes 65536 | tf_op jit(solution)/shard_map/slice | solution.py:116
  75.9 10.4 %slice-start.3 = ((bf16[9,96,16]{1,2,0:T(8,128)(2,1)}), bf16[8,96,16]{1,2,0:T(8,128)(2,1)S(1)}, s32[]{:S(2)}) async-start(bf16[9,96,16]{1,2,0:T(8,128)(2,1)} %copy-done.7), calls=%async_computation.3 | async-start | bytes 65536 | tf_op jit(solution)/shard_map/slice | solution.py:116
  91.2 8.1 %collective-permute-start.8 = (f32[83456]{0:T(1024)S(1)}, f32[83456]{0:T(1024)S(1)}, u32[]{:S(2)}, u32[]{:S(2)}) collective-permute-start(f32[83456]{0:T(1024)S(1)} %broadcast_select_fusion), channel_id=1, source_target_pairs={{0,1},{1,0},{2,3},{3,2},{4,5},{5,4},{6,7},{7,6},{8,9},{9,8},{10,11... | collective-permute-start | bytes 1001480 | tf_op jit(solution)/shard_map/ppermute | solution.py:23
  99.3 7.4 %collective-permute-start.9 = (f32[41728]{0:T(1024)S(1)}, f32[41728]{0:T(1024)S(1)}, u32[]{:S(2)}, u32[]{:S(2)}) collective-permute-start(f32[41728]{0:T(1024)S(1)} %slice_select_fusion), channel_id=1, source_target_pairs={{0,2},{1,3},{2,0},{3,1},{4,6},{5,7},{6,4},{7,5},{8,10},{9,11},{10,... | collective-permute-start | bytes 500744 | tf_op jit(solution)/shard_map/ppermute | solution.py:23
  106.7 8.4 %collective-permute-start.10 = (f32[20864]{0:T(1024)S(1)}, f32[20864]{0:T(1024)S(1)}, u32[]{:S(2)}, u32[]{:S(2)}) collective-permute-start(f32[20864]{0:T(1024)S(1)} %slice_select_fusion.1), channel_id=1, source_target_pairs={{0,4},{1,5},{2,6},{3,7},{4,0},{5,1},{6,2},{7,3},{8,12},{9,13},{10,... | collective-permute-start | bytes 250376 | tf_op jit(solution)/shard_map/ppermute | solution.py:23
  115.2 9.5 %collective-permute-start.11 = (f32[20864]{0:T(1024)S(1)}, f32[20864]{0:T(1024)S(1)}, u32[]{:S(2)}, u32[]{:S(2)}) collective-permute-start(f32[20864]{0:T(1024)S(1)} %select_add_fusion.2), channel_id=1, source_target_pairs={{0,8},{1,9},{2,10},{3,11},{4,12},{5,13},{6,14},{7,15},{8,0},{9,1},... | collective-permute-start | bytes 250376 | tf_op jit(solution)/shard_map/ppermute | solution.py:23
  124.7 5.2 %collective-permute-start.12 = (f32[20864]{0:T(1024)S(1)}, f32[20864]{0:T(1024)S(1)}, u32[]{:S(2)}, u32[]{:S(2)}) collective-permute-start(f32[20864]{0:T(1024)S(1)} %add.548), channel_id=1, source_target_pairs={{0,16},{1,17},{2,18},{3,19},{4,20},{5,21},{6,22},{7,23},{8,24},{9,... | collective-permute-start | bytes 250376 | tf_op jit(solution)/shard_map/ppermute | solution.py:23
  129.9 6.7 %collective-permute-start.13 = (f32[20864]{0:T(1024)S(1)}, f32[20864]{0:T(1024)S(1)}, u32[]{:S(2)}, u32[]{:S(2)}) collective-permute-start(f32[20864]{0:T(1024)S(1)} %add.549), channel_id=1, source_target_pairs={{0,32},{1,33},{2,34},{3,35},{4,36},{5,37},{6,38},{7,39},{8,40},{9,... | collective-permute-start | bytes 250376 | tf_op jit(solution)/shard_map/ppermute | solution.py:23
  136.7 5.2 %collective-permute-start.14 = (f32[20864]{0:T(1024)S(1)}, f32[20864]{0:T(1024)S(1)}, u32[]{:S(2)}, u32[]{:S(2)}) collective-permute-start(f32[20864]{0:T(1024)S(1)} %add.550), channel_id=1, source_target_pairs={{0,64},{1,65},{2,66},{3,67},{4,68},{5,69},{6,70},{7,71},{8,72},{9,... | collective-permute-start | bytes 250376 | tf_op jit(solution)/shard_map/ppermute | solution.py:23
  141.9 6.8 %collective-permute-start.15 = (f32[20864]{0:T(1024)S(1)}, f32[20864]{0:T(1024)S(1)}, u32[]{:S(2)}, u32[]{:S(2)}) collective-permute-start(f32[20864]{0:T(1024)S(1)} %add.551), channel_id=1, source_target_pairs={{0,128},{1,129},{2,130},{3,131},{4,132},{5,133},{6,134},{7,135},{8... | collective-permute-start | bytes 250376 | tf_op jit(solution)/shard_map/ppermute | solution.py:23
  148.7 10.0 %collective-permute-start.16 = (f32[20864]{0:T(1024)S(1)}, f32[20864]{0:T(1024)S(1)}, u32[]{:S(2)}, u32[]{:S(2)}) collective-permute-start(f32[20864]{0:T(1024)S(1)} %add.552), channel_id=1, source_target_pairs={{0,256},{1,257},{2,258},{3,259},{4,260},{5,261},{6,262},{7,263},{8... | collective-permute-start | bytes 250376 | tf_op jit(solution)/shard_map/ppermute | solution.py:23
  158.7 7.3 %collective-permute-start.17 = (f32[20864]{0:T(1024)S(1)}, f32[20864]{0:T(1024)S(1)}, u32[]{:S(2)}, u32[]{:S(2)}) collective-permute-start(f32[20864]{0:T(1024)S(1)} %add.553), channel_id=1, source_target_pairs={{0,4},{1,5},{2,6},{3,7},{4,0},{5,1},{6,2},{7,3},{8,12},{9,13},{10,... | collective-permute-start | bytes 250376 | tf_op jit(solution)/shard_map/ppermute | solution.py:23
  166.1 6.1 %collective-permute-start.18 = (f32[41728]{0:T(1024)S(1)}, f32[41728]{0:T(1024)S(1)}, u32[]{:S(2)}, u32[]{:S(2)}) collective-permute-start(f32[41728]{0:T(1024)S(1)} %maximum_select_fusion.2), channel_id=1, source_target_pairs={{0,2},{1,3},{2,0},{3,1},{4,6},{5,7},{6,4},{7,5},{8,10},{9,11},{10,... | collective-permute-start | bytes 500744 | tf_op jit(solution)/shard_map/ppermute | solution.py:23
  172.2 13.6 %collective-permute-start.19 = (f32[83456]{0:T(1024)S(1)}, f32[83456]{0:T(1024)S(1)}, u32[]{:S(2)}, u32[]{:S(2)}) collective-permute-start(f32[83456]{0:T(1024)S(1)} %maximum_select_fusion.1), channel_id=1, source_target_pairs={{0,1},{1,0},{2,3},{3,2},{4,5},{5,4},{6,7},{7,6},{8,9},{9,8},{10,11... | collective-permute-start | bytes 1001480 | tf_op jit(solution)/shard_map/ppermute | solution.py:23

commit v4 on v3

--- a/solution.py
+++ b/solution.py
@@ -266,12 +266,12 @@
     padded_act = assemble_padded(act_grid, a_picked, a_corners, missing)
     output = (fields[0].astype(jnp.float32) + conv_cells(padded_act, conv_b)).astype(jnp.bfloat16)
     terms_b = weight_terms(padded_act, upstream, cell_width)
-    tap_size = terms_a.size
-    flat = jnp.concatenate([terms_a.reshape(-1), terms_b.reshape(-1), terms_bias])
-    summed = tree_all_reduce(flat, HALVING_ROUNDS)
-    summed_a = summed[:tap_size].reshape(terms_a.shape)
-    summed_b = summed[tap_size : 2 * tap_size].reshape(terms_b.shape)
-    summed_bias = summed[2 * tap_size :]
+    summed_ab = tree_all_reduce(
+        jnp.concatenate([terms_a.reshape(-1), terms_bias]), HALVING_ROUNDS
+    )
+    summed_a = summed_ab[: terms_a.size].reshape(terms_a.shape)
+    summed_bias = summed_ab[terms_a.size :]
+    summed_b = tree_all_reduce(terms_b.reshape(-1), HALVING_ROUNDS).reshape(terms_b.shape)
     pulled_x = adjoint_sum(back_x, bx_picked, bx_corners).reshape(
         channels, cell_width * cell_width
     )

time: 189 us -> 196 us (1.037)
  starting transfers between devices: 93.6 us -> 142 us
  waiting for transfers between devices: 59.2 us -> 16 us
    ppermute x12 -> x24, starting transfers between devices: 42.9 us -> 91.3 us  [xor_partner(): lax.ppermute(block, 'tiles', [(i, i ^ distance) for i in range(devices)])]
    ppermute x12 -> x24, waiting for transfers between devices: 47.3 us -> 13.5 us  [xor_partner(): lax.ppermute(block, 'tiles', [(i, i ^ distance) for i in range(devices)])]
    ppermute x8, waiting for transfers between devices: 11.9 us -> 2.55 us  [passed_along(): return lax.ppermute(block, axis, route)]
  transfers between devices with their start and end apart: 20 -> 32, of which waited for: 14 -> 9; matrix products, arithmetic and copies ran while one was open for 3% -> 6% of each run, Pallas kernels for 0% -> 0%
where the time goes in v4:
time: 196 us; the launch traced here: 194 us
  starting transfers between devices  142 us (72%)
  local copies, waits for them, and re-layouts  21.1 us (11%)
  waiting for transfers between devices  16 us (8%)
  matrix products  10.5 us (5%)
  other arithmetic  2.66 us (1%)
  between operations  2.36 us (1%)
    ppermute x24, starting transfers between devices, xor_partner(): lax.ppermute(block, 'tiles', [(i, i ^ distance) for i in range(devices)])  91.3 us
    ppermute x8, starting transfers between devices, passed_along(): return lax.ppermute(block, axis, route)  50.4 us
    ppermute x24, waiting for transfers between devices, xor_partner(): lax.ppermute(block, 'tiles', [(i, i ^ distance) for i in range(devices)])  13.5 us
    unnamed x53, local copies, waits for them, and re-layouts  8.68 us
  transfers between devices with their start and end apart: 32, of which 9 were waited for; matrix products, arithmetic and copies ran while one was open for 6% of the time, Pallas kernels for 0%

profile of v4, /device:TPU:1, one launch (start us, length us, event | category | flops | bytes accessed | tf_op | source)
XLA Modules:
  0.0 194.3 jit_solution(12947627390959308225)
XLA Ops:
  0.6 0.9 copy.88
  2.2 0.9 copy-done.1
  6.1 5.4 %collective-permute-start.1 = (bf16[9,96,16]{1,2,0:T(8,128)(2,1)S(1)}, bf16[9,96,16]{1,2,0:T(8,128)(2,1)S(1)}, u32[]{:S(2)}, u32[]{:S(2)}) collective-permute-start(bf16[9,96,16]{1,2,0:T(8,128)(2,1)S(1)} %constant_dynamic-update-slice_fusion), channel_id=1, source_target_pairs={{511,0},{0,1},{1,2},{2,3},{3,4},{4,5},{5,6},{6,7},{7,8},{8,9},{9,1... | collective-permute-start | bytes 82952 | tf_op jit(solution)/shard_map/ppermute | solution.py:18
  11.5 5.3 %collective-permute-start = (bf16[9,96,16]{1,2,0:T(8,128)(2,1)S(1)}, bf16[9,96,16]{1,2,0:T(8,128)(2,1)S(1)}, u32[]{:S(2)}, u32[]{:S(2)}) collective-permute-start(bf16[9,96,16]{1,2,0:T(8,128)(2,1)S(1)} %constant_dynamic-update-slice_fusion), channel_id=1, source_target_pairs={{1,0},{2,1},{3,2},{4,3},{5,4},{6,5},{7,6},{8,7},{9,8},{10,9},{11,1... | collective-permute-start | bytes 82952 | tf_op jit(solution)/shard_map/ppermute | solution.py:18
  20.5 6.4 %collective-permute-start.2 = (bf16[9,96,16]{1,2,0:T(8,128)(2,1)S(1)}, bf16[9,96,16]{1,2,0:T(8,128)(2,1)S(1)}, u32[]{:S(2)}, u32[]{:S(2)}) collective-permute-start(bf16[9,96,16]{1,2,0:T(8,128)(2,1)S(1)} %constant_dynamic-update-slice_fusion.9), channel_id=1, source_target_pairs={{504,0},{505,1},{506,2},{507,3},{508,4},{509,5},{510,6},{511,7},{0... | collective-permute-start | bytes 82952 | tf_op jit(solution)/shard_map/ppermute | solution.py:18
  27.0 7.0 %collective-permute-start.3 = (bf16[9,96,16]{1,2,0:T(8,128)(2,1)S(1)}, bf16[9,96,16]{1,2,0:T(8,128)(2,1)S(1)}, u32[]{:S(2)}, u32[]{:S(2)}) collective-permute-start(bf16[9,96,16]{1,2,0:T(8,128)(2,1)S(1)} %constant_dynamic-update-slice_fusion.9), channel_id=1, source_target_pairs={{8,0},{9,1},{10,2},{11,3},{12,4},{13,5},{14,6},{15,7},{16,8},{17,9... | collective-permute-start | bytes 82952 | tf_op jit(solution)/shard_map/ppermute | solution.py:18
  34.1 1.5 collective-permute-done.3
  37.0 0.7 slice-done
  39.1 0.7 scatter_fusion
  40.4 0.9 copy-done.2
  47.7 5.3 %collective-permute-start.5 = (bf16[9,96,16]{1,2,0:T(8,128)(2,1)S(1)}, bf16[9,96,16]{1,2,0:T(8,128)(2,1)S(1)}, u32[]{:S(2)}, u32[]{:S(2)}) collective-permute-start(bf16[9,96,16]{1,2,0:T(8,128)(2,1)S(1)} %constant_dynamic-update-slice_fusion.18), channel_id=1, source_target_pairs={{511,0},{0,1},{1,2},{2,3},{3,4},{4,5},{5,6},{6,7},{7,8},{8,9},{9,1... | collective-permute-start | bytes 82952 | tf_op jit(solution)/shard_map/ppermute | solution.py:18
  53.0 7.3 %collective-permute-start.4 = (bf16[9,96,16]{1,2,0:T(8,128)(2,1)S(1)}, bf16[9,96,16]{1,2,0:T(8,128)(2,1)S(1)}, u32[]{:S(2)}, u32[]{:S(2)}) collective-permute-start(bf16[9,96,16]{1,2,0:T(8,128)(2,1)S(1)} %constant_dynamic-update-slice_fusion.18), channel_id=1, source_target_pairs={{1,0},{2,1},{3,2},{4,3},{5,4},{6,5},{7,6},{8,7},{9,8},{10,9},{11,1... | collective-permute-start | bytes 82952 | tf_op jit(solution)/shard_map/ppermute | solution.py:18
  61.8 1.9 collective-permute-start.6
  63.8 9.2 %collective-permute-start.8 = (f32[41984]{0:T(1024)S(1)}, f32[41984]{0:T(1024)S(1)}, u32[]{:S(2)}, u32[]{:S(2)}) collective-permute-start(f32[41984]{0:T(1024)S(1)} %slice_select_fusion.1), channel_id=1, source_target_pairs={{0,1},{1,0},{2,3},{3,2},{4,5},{5,4},{6,7},{7,6},{8,9},{9,8},{10,11... | collective-permute-start | bytes 503816 | tf_op jit(solution)/shard_map/ppermute | solution.py:23
  73.0 11.8 %collective-permute-start.7 = (bf16[9,96,16]{1,2,0:T(8,128)(2,1)S(1)}, bf16[9,96,16]{1,2,0:T(8,128)(2,1)S(1)}, u32[]{:S(2)}, u32[]{:S(2)}) collective-permute-start(bf16[9,96,16]{1,2,0:T(8,128)(2,1)S(1)} %constant_dynamic-update-slice_fusion.27), channel_id=1, source_target_pairs={{8,0},{9,1},{10,2},{11,3},{12,4},{13,5},{14,6},{15,7},{16,8},{17,9... | collective-permute-start | bytes 82952 | tf_op jit(solution)/shard_map/ppermute | solution.py:18
  84.8 1.0 collective-permute-done.7
  92.6 2.8 %collective-permute-start.20 = (f32[41472]{0:T(1024)S(1)}, f32[41472]{0:T(1024)S(1)}, u32[]{:S(2)}, u32[]{:S(2)}) collective-permute-start(f32[41472]{0:T(1024)S(1)} %slice_select_fusion), channel_id=1, source_target_pairs={{0,1},{1,0},{2,3},{3,2},{4,5},{5,4},{6,7},{7,6},{8,9},{9,8},{10,11... | collective-permute-start | bytes 497672 | tf_op jit(solution)/shard_map/ppermute | solution.py:23
  95.5 1.9 collective-permute-start.9
  97.4 4.0 %collective-permute-done.9 = f32[20992]{0:T(1024)S(1)} collective-permute-done((f32[20992]{0:T(1024)S(1)}, f32[20992]{0:T(1024)S(1)}, u32[]{:S(2)}, u32[]{:S(2)}) %collective-permute-start.9) | collective-permute-done | bytes 84000 | tf_op jit(solution)/shard_map/ppermute | solution.py:23
  101.5 1.9 collective-permute-start.10
  103.4 2.6 %collective-permute-start.21 = (f32[20736]{0:T(1024)S(1)}, f32[20736]{0:T(1024)S(1)}, u32[]{:S(2)}, u32[]{:S(2)}) collective-permute-start(f32[20736]{0:T(1024)S(1)} %slice_select_fusion.2), channel_id=1, source_target_pairs={{0,2},{1,3},{2,0},{3,1},{4,6},{5,7},{6,4},{7,5},{8,10},{9,11},{10,... | collective-permute-start | bytes 248840 | tf_op jit(solution)/shard_map/ppermute | solution.py:23
  106.0 1.6 collective-permute-done.10
  107.7 1.9 collective-permute-start.11
  109.6 3.3 %collective-permute-start.22 = (f32[10368]{0:T(1024)S(1)}, f32[10368]{0:T(1024)S(1)}, u32[]{:S(2)}, u32[]{:S(2)}) collective-permute-start(f32[10368]{0:T(1024)S(1)} %slice_select_fusion.4), channel_id=1, source_target_pairs={{0,4},{1,5},{2,6},{3,7},{4,0},{5,1},{6,2},{7,3},{8,12},{9,13},{10,... | collective-permute-start | bytes 124424 | tf_op jit(solution)/shard_map/ppermute | solution.py:23
  113.0 3.5 %collective-permute-done.11 = f32[10496]{0:T(1024)S(1)} collective-permute-done((f32[10496]{0:T(1024)S(1)}, f32[10496]{0:T(1024)S(1)}, u32[]{:S(2)}, u32[]{:S(2)}) %collective-permute-start.11) | collective-permute-done | bytes 42016 | tf_op jit(solution)/shard_map/ppermute | solution.py:23
  116.5 1.9 collective-permute-start.12
  118.4 4.3 %collective-permute-start.23 = (f32[10368]{0:T(1024)S(1)}, f32[10368]{0:T(1024)S(1)}, u32[]{:S(2)}, u32[]{:S(2)}) collective-permute-start(f32[10368]{0:T(1024)S(1)} %select_add_fusion.4), channel_id=1, source_target_pairs={{0,8},{1,9},{2,10},{3,11},{4,12},{5,13},{6,14},{7,15},{8,0},{9,1},... | collective-permute-start | bytes 124424 | tf_op jit(solution)/shard_map/ppermute | solution.py:23
  122.8 0.7 scatter_fusion.1
  123.5 3.4 %collective-permute-start.13 = (f32[10496]{0:T(1024)S(1)}, f32[10496]{0:T(1024)S(1)}, u32[]{:S(2)}, u32[]{:S(2)}) collective-permute-start(f32[10496]{0:T(1024)S(1)} %add.576), channel_id=1, source_target_pairs={{0,32},{1,33},{2,34},{3,35},{4,36},{5,37},{6,38},{7,39},{8,40},{9,... | collective-permute-start | bytes 125960 | tf_op jit(solution)/shard_map/ppermute | solution.py:23
  127.1 3.4 %collective-permute-start.24 = (f32[10368]{0:T(1024)S(1)}, f32[10368]{0:T(1024)S(1)}, u32[]{:S(2)}, u32[]{:S(2)}) collective-permute-start(f32[10368]{0:T(1024)S(1)} %add.584), channel_id=1, source_target_pairs={{0,16},{1,17},{2,18},{3,19},{4,20},{5,21},{6,22},{7,23},{8,24},{9,... | collective-permute-start | bytes 124424 | tf_op jit(solution)/shard_map/ppermute | solution.py:23
  130.6 1.9 collective-permute-start.14
  132.5 3.9 %collective-permute-start.25 = (f32[10368]{0:T(1024)S(1)}, f32[10368]{0:T(1024)S(1)}, u32[]{:S(2)}, u32[]{:S(2)}) collective-permute-start(f32[10368]{0:T(1024)S(1)} %add.585), channel_id=1, source_target_pairs={{0,32},{1,33},{2,34},{3,35},{4,36},{5,37},{6,38},{7,39},{8,40},{9,... | collective-permute-start | bytes 124424 | tf_op jit(solution)/shard_map/ppermute | solution.py:23
  136.6 9.4 %collective-permute-start.15 = (f32[10496]{0:T(1024)S(1)}, f32[10496]{0:T(1024)S(1)}, u32[]{:S(2)}, u32[]{:S(2)}) collective-permute-start(f32[10496]{0:T(1024)S(1)} %add.578), channel_id=1, source_target_pairs={{0,128},{1,129},{2,130},{3,131},{4,132},{5,133},{6,134},{7,135},{8... | collective-permute-start | bytes 125960 | tf_op jit(solution)/shard_map/ppermute | solution.py:23
  146.1 1.9 collective-permute-start.26
  148.3 4.8 %collective-permute-start.16 = (f32[10496]{0:T(1024)S(1)}, f32[10496]{0:T(1024)S(1)}, u32[]{:S(2)}, u32[]{:S(2)}) collective-permute-start(f32[10496]{0:T(1024)S(1)} %add.579), channel_id=1, source_target_pairs={{0,256},{1,257},{2,258},{3,259},{4,260},{5,261},{6,262},{7,263},{8... | collective-permute-start | bytes 125960 | tf_op jit(solution)/shard_map/ppermute | solution.py:23
  153.1 3.5 %collective-permute-start.27 = (f32[10368]{0:T(1024)S(1)}, f32[10368]{0:T(1024)S(1)}, u32[]{:S(2)}, u32[]{:S(2)}) collective-permute-start(f32[10368]{0:T(1024)S(1)} %add.587), channel_id=1, source_target_pairs={{0,128},{1,129},{2,130},{3,131},{4,132},{5,133},{6,134},{7,135},{8... | collective-permute-start | bytes 124424 | tf_op jit(solution)/shard_map/ppermute | solution.py:23
  157.0 2.2 %collective-permute-start.17 = (f32[10496]{0:T(1024)S(1)}, f32[10496]{0:T(1024)S(1)}, u32[]{:S(2)}, u32[]{:S(2)}) collective-permute-start(f32[10496]{0:T(1024)S(1)} %add.580), channel_id=1, source_target_pairs={{0,4},{1,5},{2,6},{3,7},{4,0},{5,1},{6,2},{7,3},{8,12},{9,13},{10,... | collective-permute-start | bytes 125960 | tf_op jit(solution)/shard_map/ppermute | solution.py:23
  159.3 4.8 %collective-permute-start.28 = (f32[10368]{0:T(1024)S(1)}, f32[10368]{0:T(1024)S(1)}, u32[]{:S(2)}, u32[]{:S(2)}) collective-permute-start(f32[10368]{0:T(1024)S(1)} %add.588), channel_id=1, source_target_pairs={{0,256},{1,257},{2,258},{3,259},{4,260},{5,261},{6,262},{7,263},{8... | collective-permute-start | bytes 124424 | tf_op jit(solution)/shard_map/ppermute | solution.py:23
  164.0 0.8 fusion.14
  165.5 2.8 %collective-permute-done.28 = f32[10368]{0:T(1024)S(1)} collective-permute-done((f32[10368]{0:T(1024)S(1)}, f32[10368]{0:T(1024)S(1)}, u32[]{:S(2)}, u32[]{:S(2)}) %collective-permute-start.28) | collective-permute-done | bytes 41504 | tf_op jit(solution)/shard_map/ppermute | solution.py:23
  168.3 3.6 %collective-permute-start.29 = (f32[10368]{0:T(1024)S(1)}, f32[10368]{0:T(1024)S(1)}, u32[]{:S(2)}, u32[]{:S(2)}) collective-permute-start(f32[10368]{0:T(1024)S(1)} %add.589), channel_id=1, source_target_pairs={{0,4},{1,5},{2,6},{3,7},{4,0},{5,1},{6,2},{7,3},{8,12},{9,13},{10,... | collective-permute-start | bytes 124424 | tf_op jit(solution)/shard_map/ppermute | solution.py:23
  172.0 1.9 collective-permute-start.18
  173.9 0.9 collective-permute-done.29
  174.8 2.5 %collective-permute-start.30 = (f32[20736]{0:T(1024)S(1)}, f32[20736]{0:T(1024)S(1)}, u32[]{:S(2)}, u32[]{:S(2)}) collective-permute-start(f32[20736]{0:T(1024)S(1)} %maximum_select_fusion.5), channel_id=1, source_target_pairs={{0,2},{1,3},{2,0},{3,1},{4,6},{5,7},{6,4},{7,5},{8,10},{9,11},{10,... | collective-permute-start | bytes 248840 | tf_op jit(solution)/shard_map/ppermute | solution.py:23
  177.3 11.4 %collective-permute-start.19 = (f32[41984]{0:T(1024)S(1)}, f32[41984]{0:T(1024)S(1)}, u32[]{:S(2)}, u32[]{:S(2)}) collective-permute-start(f32[41984]{0:T(1024)S(1)} %maximum_select_fusion.2), channel_id=1, source_target_pairs={{0,1},{1,0},{2,3},{3,2},{4,5},{5,4},{6,7},{7,6},{8,9},{9,8},{10,11... | collective-permute-start | bytes 503816 | tf_op jit(solution)/shard_map/ppermute | solution.py:23
  188.8 3.0 %collective-permute-start.31 = (f32[41472]{0:T(1024)S(1)}, f32[41472]{0:T(1024)S(1)}, u32[]{:S(2)}, u32[]{:S(2)}) collective-permute-start(f32[41472]{0:T(1024)S(1)} %maximum_select_fusion.3), channel_id=1, source_target_pairs={{0,1},{1,0},{2,3},{3,2},{4,5},{5,4},{6,7},{7,6},{8,9},{9,8},{10,11... | collective-permute-start | bytes 497672 | tf_op jit(solution)/shard_map/ppermute | solution.py:23
  191.9 0.9 mul.196
  193.4 0.9 mul.198
  (304 shorter events, 27.4 us)
Async XLA Ops:
  0.6 1.0 copy-start
  2.1 0.9 copy-start.1
  5.2 0.7 copy-start.12
  6.1 14.4 %collective-permute-start.1 = (bf16[9,96,16]{1,2,0:T(8,128)(2,1)S(1)}, bf16[9,96,16]{1,2,0:T(8,128)(2,1)S(1)}, u32[]{:S(2)}, u32[]{:S(2)}) collective-permute-start(bf16[9,96,16]{1,2,0:T(8,128)(2,1)S(1)} %constant_dynamic-update-slice_fusion), channel_id=1, source_target_pairs={{511,0},{0,1},{1,2},{2,3},{3,4},{4,5},{5,6},{6,7},{7,8},{8,9},{9,1... | collective-permute-start | bytes 82952 | tf_op jit(solution)/shard_map/ppermute | solution.py:18
  11.5 9.0 %collective-permute-start = (bf16[9,96,16]{1,2,0:T(8,128)(2,1)S(1)}, bf16[9,96,16]{1,2,0:T(8,128)(2,1)S(1)}, u32[]{:S(2)}, u32[]{:S(2)}) collective-permute-start(bf16[9,96,16]{1,2,0:T(8,128)(2,1)S(1)} %constant_dynamic-update-slice_fusion), channel_id=1, source_target_pairs={{1,0},{2,1},{3,2},{4,3},{5,4},{6,5},{7,6},{8,7},{9,8},{10,9},{11,1... | collective-permute-start | bytes 82952 | tf_op jit(solution)/shard_map/ppermute | solution.py:18
  17.5 0.7 copy-start.9
  18.2 0.7 copy-start.15
  19.1 0.7 copy-start.14
  20.5 13.6 %copy-start.4 = (bf16[9,96,16]{1,2,0:T(8,128)(2,1)}, bf16[9,96,16]{1,2,0:T(8,128)(2,1)S(1)}, u32[]{:S(2)}) copy-start(bf16[9,96,16]{1,2,0:T(8,128)(2,1)S(1)} %collective-permute-done.1) | copy-start | bytes 82948
  20.5 13.6 %copy-start.5 = (bf16[9,96,16]{1,2,0:T(8,128)(2,1)}, bf16[9,96,16]{1,2,0:T(8,128)(2,1)S(1)}, u32[]{:S(2)}) copy-start(bf16[9,96,16]{1,2,0:T(8,128)(2,1)S(1)} %collective-permute-done) | copy-start | bytes 82948
  20.5 13.6 %collective-permute-start.2 = (bf16[9,96,16]{1,2,0:T(8,128)(2,1)S(1)}, bf16[9,96,16]{1,2,0:T(8,128)(2,1)S(1)}, u32[]{:S(2)}, u32[]{:S(2)}) collective-permute-start(bf16[9,96,16]{1,2,0:T(8,128)(2,1)S(1)} %constant_dynamic-update-slice_fusion.9), channel_id=1, source_target_pairs={{504,0},{505,1},{506,2},{507,3},{508,4},{509,5},{510,6},{511,7},{0... | collective-permute-start | bytes 82952 | tf_op jit(solution)/shard_map/ppermute | solution.py:18
  27.0 8.6 %collective-permute-start.3 = (bf16[9,96,16]{1,2,0:T(8,128)(2,1)S(1)}, bf16[9,96,16]{1,2,0:T(8,128)(2,1)S(1)}, u32[]{:S(2)}, u32[]{:S(2)}) collective-permute-start(bf16[9,96,16]{1,2,0:T(8,128)(2,1)S(1)} %constant_dynamic-update-slice_fusion.9), channel_id=1, source_target_pairs={{8,0},{9,1},{10,2},{11,3},{12,4},{13,5},{14,6},{15,7},{16,8},{17,9... | collective-permute-start | bytes 82952 | tf_op jit(solution)/shard_map/ppermute | solution.py:18
  36.9 0.8 slice-start
  36.9 0.8 slice-start.1
  40.3 0.9 copy-start.2
  41.7 0.8 copy-start.3
  47.7 14.1 %collective-permute-start.5 = (bf16[9,96,16]{1,2,0:T(8,128)(2,1)S(1)}, bf16[9,96,16]{1,2,0:T(8,128)(2,1)S(1)}, u32[]{:S(2)}, u32[]{:S(2)}) collective-permute-start(bf16[9,96,16]{1,2,0:T(8,128)(2,1)S(1)} %constant_dynamic-update-slice_fusion.18), channel_id=1, source_target_pairs={{511,0},{0,1},{1,2},{2,3},{3,4},{4,5},{5,6},{6,7},{7,8},{8,9},{9,1... | collective-permute-start | bytes 82952 | tf_op jit(solution)/shard_map/ppermute | solution.py:18
  53.0 8.8 %collective-permute-start.4 = (bf16[9,96,16]{1,2,0:T(8,128)(2,1)S(1)}, bf16[9,96,16]{1,2,0:T(8,128)(2,1)S(1)}, u32[]{:S(2)}, u32[]{:S(2)}) collective-permute-start(bf16[9,96,16]{1,2,0:T(8,128)(2,1)S(1)} %constant_dynamic-update-slice_fusion.18), channel_id=1, source_target_pairs={{1,0},{2,1},{3,2},{4,3},{5,4},{6,5},{7,6},{8,7},{9,8},{10,9},{11,1... | collective-permute-start | bytes 82952 | tf_op jit(solution)/shard_map/ppermute | solution.py:18
  61.8 23.0 %copy-start.6 = (bf16[9,96,16]{1,2,0:T(8,128)(2,1)}, bf16[9,96,16]{1,2,0:T(8,128)(2,1)S(1)}, u32[]{:S(2)}) copy-start(bf16[9,96,16]{1,2,0:T(8,128)(2,1)S(1)} %collective-permute-done.5) | copy-start | bytes 82948
  61.8 23.0 %copy-start.7 = (bf16[9,96,16]{1,2,0:T(8,128)(2,1)}, bf16[9,96,16]{1,2,0:T(8,128)(2,1)S(1)}, u32[]{:S(2)}) copy-start(bf16[9,96,16]{1,2,0:T(8,128)(2,1)S(1)} %collective-permute-done.4) | copy-start | bytes 82948
  61.8 23.0 %collective-permute-start.6 = (bf16[9,96,16]{1,2,0:T(8,128)(2,1)S(1)}, bf16[9,96,16]{1,2,0:T(8,128)(2,1)S(1)}, u32[]{:S(2)}, u32[]{:S(2)}) collective-permute-start(bf16[9,96,16]{1,2,0:T(8,128)(2,1)S(1)} %constant_dynamic-update-slice_fusion.27), channel_id=1, source_target_pairs={{504,0},{505,1},{506,2},{507,3},{508,4},{509,5},{510,6},{511,7},{0... | collective-permute-start | bytes 82952 | tf_op jit(solution)/shard_map/ppermute | solution.py:18
  63.8 31.6 %collective-permute-start.8 = (f32[41984]{0:T(1024)S(1)}, f32[41984]{0:T(1024)S(1)}, u32[]{:S(2)}, u32[]{:S(2)}) collective-permute-start(f32[41984]{0:T(1024)S(1)} %slice_select_fusion.1), channel_id=1, source_target_pairs={{0,1},{1,0},{2,3},{3,2},{4,5},{5,4},{6,7},{7,6},{8,9},{9,8},{10,11... | collective-permute-start | bytes 503816 | tf_op jit(solution)/shard_map/ppermute | solution.py:23
  73.0 12.8 %collective-permute-start.7 = (bf16[9,96,16]{1,2,0:T(8,128)(2,1)S(1)}, bf16[9,96,16]{1,2,0:T(8,128)(2,1)S(1)}, u32[]{:S(2)}, u32[]{:S(2)}) collective-permute-start(bf16[9,96,16]{1,2,0:T(8,128)(2,1)S(1)} %constant_dynamic-update-slice_fusion.27), channel_id=1, source_target_pairs={{8,0},{9,1},{10,2},{11,3},{12,4},{13,5},{14,6},{15,7},{16,8},{17,9... | collective-permute-start | bytes 82952 | tf_op jit(solution)/shard_map/ppermute | solution.py:18
  87.0 0.8 slice-start.2
  87.0 0.8 slice-start.3
  92.6 4.8 %collective-permute-start.20 = (f32[41472]{0:T(1024)S(1)}, f32[41472]{0:T(1024)S(1)}, u32[]{:S(2)}, u32[]{:S(2)}) collective-permute-start(f32[41472]{0:T(1024)S(1)} %slice_select_fusion), channel_id=1, source_target_pairs={{0,1},{1,0},{2,3},{3,2},{4,5},{5,4},{6,7},{7,6},{8,9},{9,8},{10,11... | collective-permute-start | bytes 497672 | tf_op jit(solution)/shard_map/ppermute | solution.py:23
  95.5 6.0 %collective-permute-start.9 = (f32[20992]{0:T(1024)S(1)}, f32[20992]{0:T(1024)S(1)}, u32[]{:S(2)}, u32[]{:S(2)}) collective-permute-start(f32[20992]{0:T(1024)S(1)} %slice_select_fusion.3), channel_id=1, source_target_pairs={{0,2},{1,3},{2,0},{3,1},{4,6},{5,7},{6,4},{7,5},{8,10},{9,11},{10,... | collective-permute-start | bytes 251912 | tf_op jit(solution)/shard_map/ppermute | solution.py:23
  101.5 6.2 %collective-permute-start.10 = (f32[10496]{0:T(1024)S(1)}, f32[10496]{0:T(1024)S(1)}, u32[]{:S(2)}, u32[]{:S(2)}) collective-permute-start(f32[10496]{0:T(1024)S(1)} %slice_select_fusion.5), channel_id=1, source_target_pairs={{0,4},{1,5},{2,6},{3,7},{4,0},{5,1},{6,2},{7,3},{8,12},{9,13},{10,... | collective-permute-start | bytes 125960 | tf_op jit(solution)/shard_map/ppermute | solution.py:23
  103.4 6.2 %collective-permute-start.21 = (f32[20736]{0:T(1024)S(1)}, f32[20736]{0:T(1024)S(1)}, u32[]{:S(2)}, u32[]{:S(2)}) collective-permute-start(f32[20736]{0:T(1024)S(1)} %slice_select_fusion.2), channel_id=1, source_target_pairs={{0,2},{1,3},{2,0},{3,1},{4,6},{5,7},{6,4},{7,5},{8,10},{9,11},{10,... | collective-permute-start | bytes 248840 | tf_op jit(solution)/shard_map/ppermute | solution.py:23
  107.7 8.8 %collective-permute-start.11 = (f32[10496]{0:T(1024)S(1)}, f32[10496]{0:T(1024)S(1)}, u32[]{:S(2)}, u32[]{:S(2)}) collective-permute-start(f32[10496]{0:T(1024)S(1)} %select_add_fusion.5), channel_id=1, source_target_pairs={{0,8},{1,9},{2,10},{3,11},{4,12},{5,13},{6,14},{7,15},{8,0},{9,1},... | collective-permute-start | bytes 125960 | tf_op jit(solution)/shard_map/ppermute | solution.py:23
  109.6 8.8 %collective-permute-start.22 = (f32[10368]{0:T(1024)S(1)}, f32[10368]{0:T(1024)S(1)}, u32[]{:S(2)}, u32[]{:S(2)}) collective-permute-start(f32[10368]{0:T(1024)S(1)} %slice_select_fusion.4), channel_id=1, source_target_pairs={{0,4},{1,5},{2,6},{3,7},{4,0},{5,1},{6,2},{7,3},{8,12},{9,13},{10,... | collective-permute-start | bytes 124424 | tf_op jit(solution)/shard_map/ppermute | solution.py:23
  116.5 7.0 %collective-permute-start.12 = (f32[10496]{0:T(1024)S(1)}, f32[10496]{0:T(1024)S(1)}, u32[]{:S(2)}, u32[]{:S(2)}) collective-permute-start(f32[10496]{0:T(1024)S(1)} %add.575), channel_id=1, source_target_pairs={{0,16},{1,17},{2,18},{3,19},{4,20},{5,21},{6,22},{7,23},{8,24},{9,... | collective-permute-start | bytes 125960 | tf_op jit(solution)/shard_map/ppermute | solution.py:23
  118.4 8.7 %collective-permute-start.23 = (f32[10368]{0:T(1024)S(1)}, f32[10368]{0:T(1024)S(1)}, u32[]{:S(2)}, u32[]{:S(2)}) collective-permute-start(f32[10368]{0:T(1024)S(1)} %select_add_fusion.4), channel_id=1, source_target_pairs={{0,8},{1,9},{2,10},{3,11},{4,12},{5,13},{6,14},{7,15},{8,0},{9,1},... | collective-permute-start | bytes 124424 | tf_op jit(solution)/shard_map/ppermute | solution.py:23
  123.5 7.0 %collective-permute-start.13 = (f32[10496]{0:T(1024)S(1)}, f32[10496]{0:T(1024)S(1)}, u32[]{:S(2)}, u32[]{:S(2)}) collective-permute-start(f32[10496]{0:T(1024)S(1)} %add.576), channel_id=1, source_target_pairs={{0,32},{1,33},{2,34},{3,35},{4,36},{5,37},{6,38},{7,39},{8,40},{9,... | collective-permute-start | bytes 125960 | tf_op jit(solution)/shard_map/ppermute | solution.py:23
  127.1 5.4 %collective-permute-start.24 = (f32[10368]{0:T(1024)S(1)}, f32[10368]{0:T(1024)S(1)}, u32[]{:S(2)}, u32[]{:S(2)}) collective-permute-start(f32[10368]{0:T(1024)S(1)} %add.584), channel_id=1, source_target_pairs={{0,16},{1,17},{2,18},{3,19},{4,20},{5,21},{6,22},{7,23},{8,24},{9,... | collective-permute-start | bytes 124424 | tf_op jit(solution)/shard_map/ppermute | solution.py:23
  130.6 6.0 %collective-permute-start.14 = (f32[10496]{0:T(1024)S(1)}, f32[10496]{0:T(1024)S(1)}, u32[]{:S(2)}, u32[]{:S(2)}) collective-permute-start(f32[10496]{0:T(1024)S(1)} %add.577), channel_id=1, source_target_pairs={{0,64},{1,65},{2,66},{3,67},{4,68},{5,69},{6,70},{7,71},{8,72},{9,... | collective-permute-start | bytes 125960 | tf_op jit(solution)/shard_map/ppermute | solution.py:23
  132.5 13.6 %collective-permute-start.25 = (f32[10368]{0:T(1024)S(1)}, f32[10368]{0:T(1024)S(1)}, u32[]{:S(2)}, u32[]{:S(2)}) collective-permute-start(f32[10368]{0:T(1024)S(1)} %add.585), channel_id=1, source_target_pairs={{0,32},{1,33},{2,34},{3,35},{4,36},{5,37},{6,38},{7,39},{8,40},{9,... | collective-permute-start | bytes 124424 | tf_op jit(solution)/shard_map/ppermute | solution.py:23
  136.6 11.6 %collective-permute-start.15 = (f32[10496]{0:T(1024)S(1)}, f32[10496]{0:T(1024)S(1)}, u32[]{:S(2)}, u32[]{:S(2)}) collective-permute-start(f32[10496]{0:T(1024)S(1)} %add.578), channel_id=1, source_target_pairs={{0,128},{1,129},{2,130},{3,131},{4,132},{5,133},{6,134},{7,135},{8... | collective-permute-start | bytes 125960 | tf_op jit(solution)/shard_map/ppermute | solution.py:23
  146.1 6.9 %collective-permute-start.26 = (f32[10368]{0:T(1024)S(1)}, f32[10368]{0:T(1024)S(1)}, u32[]{:S(2)}, u32[]{:S(2)}) collective-permute-start(f32[10368]{0:T(1024)S(1)} %add.586), channel_id=1, source_target_pairs={{0,64},{1,65},{2,66},{3,67},{4,68},{5,69},{6,70},{7,71},{8,72},{9,... | collective-permute-start | bytes 124424 | tf_op jit(solution)/shard_map/ppermute | solution.py:23
  148.3 8.7 %collective-permute-start.16 = (f32[10496]{0:T(1024)S(1)}, f32[10496]{0:T(1024)S(1)}, u32[]{:S(2)}, u32[]{:S(2)}) collective-permute-start(f32[10496]{0:T(1024)S(1)} %add.579), channel_id=1, source_target_pairs={{0,256},{1,257},{2,258},{3,259},{4,260},{5,261},{6,262},{7,263},{8... | collective-permute-start | bytes 125960 | tf_op jit(solution)/shard_map/ppermute | solution.py:23
  153.1 6.1 %collective-permute-start.27 = (f32[10368]{0:T(1024)S(1)}, f32[10368]{0:T(1024)S(1)}, u32[]{:S(2)}, u32[]{:S(2)}) collective-permute-start(f32[10368]{0:T(1024)S(1)} %add.587), channel_id=1, source_target_pairs={{0,128},{1,129},{2,130},{3,131},{4,132},{5,133},{6,134},{7,135},{8... | collective-permute-start | bytes 124424 | tf_op jit(solution)/shard_map/ppermute | solution.py:23
  157.0 14.9 %collective-permute-start.17 = (f32[10496]{0:T(1024)S(1)}, f32[10496]{0:T(1024)S(1)}, u32[]{:S(2)}, u32[]{:S(2)}) collective-permute-start(f32[10496]{0:T(1024)S(1)} %add.580), channel_id=1, source_target_pairs={{0,4},{1,5},{2,6},{3,7},{4,0},{5,1},{6,2},{7,3},{8,12},{9,13},{10,... | collective-permute-start | bytes 125960 | tf_op jit(solution)/shard_map/ppermute | solution.py:23
  159.3 9.1 %collective-permute-start.28 = (f32[10368]{0:T(1024)S(1)}, f32[10368]{0:T(1024)S(1)}, u32[]{:S(2)}, u32[]{:S(2)}) collective-permute-start(f32[10368]{0:T(1024)S(1)} %add.588), channel_id=1, source_target_pairs={{0,256},{1,257},{2,258},{3,259},{4,260},{5,261},{6,262},{7,263},{8... | collective-permute-start | bytes 124424 | tf_op jit(solution)/shard_map/ppermute | solution.py:23
  168.3 6.5 %collective-permute-start.29 = (f32[10368]{0:T(1024)S(1)}, f32[10368]{0:T(1024)S(1)}, u32[]{:S(2)}, u32[]{:S(2)}) collective-permute-start(f32[10368]{0:T(1024)S(1)} %add.589), channel_id=1, source_target_pairs={{0,4},{1,5},{2,6},{3,7},{4,0},{5,1},{6,2},{7,3},{8,12},{9,13},{10,... | collective-permute-start | bytes 124424 | tf_op jit(solution)/shard_map/ppermute | solution.py:23
  172.0 5.3 %collective-permute-start.18 = (f32[20992]{0:T(1024)S(1)}, f32[20992]{0:T(1024)S(1)}, u32[]{:S(2)}, u32[]{:S(2)}) collective-permute-start(f32[20992]{0:T(1024)S(1)} %maximum_select_fusion.4), channel_id=1, source_target_pairs={{0,2},{1,3},{2,0},{3,1},{4,6},{5,7},{6,4},{7,5},{8,10},{9,11},{10,... | collective-permute-start | bytes 251912 | tf_op jit(solution)/shard_map/ppermute | solution.py:23
  174.8 14.0 %collective-permute-start.30 = (f32[20736]{0:T(1024)S(1)}, f32[20736]{0:T(1024)S(1)}, u32[]{:S(2)}, u32[]{:S(2)}) collective-permute-start(f32[20736]{0:T(1024)S(1)} %maximum_select_fusion.5), channel_id=1, source_target_pairs={{0,2},{1,3},{2,0},{3,1},{4,6},{5,7},{6,4},{7,5},{8,10},{9,11},{10,... | collective-permute-start | bytes 248840 | tf_op jit(solution)/shard_map/ppermute | solution.py:23
  177.3 14.5 %collective-permute-start.19 = (f32[41984]{0:T(1024)S(1)}, f32[41984]{0:T(1024)S(1)}, u32[]{:S(2)}, u32[]{:S(2)}) collective-permute-start(f32[41984]{0:T(1024)S(1)} %maximum_select_fusion.2), channel_id=1, source_target_pairs={{0,1},{1,0},{2,3},{3,2},{4,5},{5,4},{6,7},{7,6},{8,9},{9,8},{10,11... | collective-permute-start | bytes 503816 | tf_op jit(solution)/shard_map/ppermute | solution.py:23
  188.8 4.5 %collective-permute-start.31 = (f32[41472]{0:T(1024)S(1)}, f32[41472]{0:T(1024)S(1)}, u32[]{:S(2)}, u32[]{:S(2)}) collective-permute-start(f32[41472]{0:T(1024)S(1)} %maximum_select_fusion.3), channel_id=1, source_target_pairs={{0,1},{1,0},{2,3},{3,2},{4,5},{5,4},{6,7},{7,6},{8,9},{9,8},{10,11... | collective-permute-start | bytes 497672 | tf_op jit(solution)/shard_map/ppermute | solution.py:23
  (4 other events, 2.6 us)

commit v5 on v3

--- a/solution.py
+++ b/solution.py
@@ -48,6 +48,20 @@
     return cur[:length]
 
 
+def paired_shift(block, distance):
+    devices = lax.axis_size("tiles")
+    own = lax.axis_index("tiles")
+    flip = [(i, i ^ distance) for i in range(devices)]
+    other = [
+        (i, (i + distance) % devices if i & distance else (i - distance) % devices)
+        for i in range(devices)
+    ]
+    got_flip = lax.ppermute(block, "tiles", flip)
+    got_other = lax.ppermute(block, "tiles", other)
+    low = (own & distance) == 0
+    return jnp.where(low, got_flip, got_other), jnp.where(low, got_other, got_flip)
+
+
 def gelu_slope(values):
     return (
         0.5 * (1.0 + lax.erf(values * inv_root_two))
@@ -104,14 +118,12 @@
     corners = jnp.concatenate(corner_groups, axis=0)
     width = strips.shape[2]
     payload_a = jnp.concatenate([strips, corner_row(corners, width)], axis=0)
-    from_next = passed_along(payload_a, "tiles", -1)
-    from_prev = passed_along(payload_a, "tiles", 1)
+    from_next, from_prev = paired_shift(payload_a, 1)
     corners_next = jnp.transpose(from_next[n_strips, :, :n_strips], (1, 0))
     corners_prev = jnp.transpose(from_prev[n_strips, :, :n_strips], (1, 0))
     relay = jnp.concatenate([corners_next, corners_prev], axis=0)
     payload_b = jnp.concatenate([strips, corner_row(relay, width)], axis=0)
-    from_up = passed_along(payload_b, "tiles", row_length)
-    from_down = passed_along(payload_b, "tiles", -row_length)
+    from_down, from_up = paired_shift(payload_b, row_length)
     stacked = jnp.concatenate(
         [from_up[:n_strips], from_next[:n_strips], from_down[:n_strips], from_prev[:n_strips]],
         axis=0,

time: 189 us -> 180 us (0.952)
  starting transfers between devices: 93.6 us -> 84.1 us
    ppermute x8, starting transfers between devices: 50.7 us -> 43.1 us  [the longest x4 22.7 us: paired_shift(): got_flip = lax.ppermute(block, 'tiles', flip)]
    ppermute x12, starting transfers between devices: 42.9 us -> 41 us  [xor_partner(): lax.ppermute(block, 'tiles', [(i, i ^ distance) for i in range(devices)])]
    unnamed x53 -> x45, local copies, waits for them, and re-layouts: 8.69 us -> 8.66 us
  transfers between devices with their start and end apart: 20 -> 20, of which waited for: 14 -> 15; matrix products, arithmetic and copies ran while one was open for 3% -> 3% of each run, Pallas kernels for 0% -> 0%
where the time goes in v5:
time: 180 us; the launch traced here: 179 us
  starting transfers between devices  84.1 us (47%)
  waiting for transfers between devices  60.2 us (33%)
  local copies, waits for them, and re-layouts  19.6 us (11%)
  matrix products  10.5 us (6%)
  other arithmetic  2.68 us (1%)
  between operations  1.98 us (1%)
    ppermute x12, waiting for transfers between devices, xor_partner(): lax.ppermute(block, 'tiles', [(i, i ^ distance) for i in range(devices)])  48.2 us
    ppermute x12, starting transfers between devices, xor_partner(): lax.ppermute(block, 'tiles', [(i, i ^ distance) for i in range(devices)])  41 us
    ppermute x4, starting transfers between devices, paired_shift(): got_flip = lax.ppermute(block, 'tiles', flip)  22.7 us
    ppermute x4, starting transfers between devices, paired_shift(): got_other = lax.ppermute(block, 'tiles', other)  20.3 us
    ppermute x4, waiting for transfers between devices, paired_shift(): got_other = lax.ppermute(block, 'tiles', other)  11.5 us
    unnamed x45, local copies, waits for them, and re-layouts  8.66 us
    dot_general x18, matrix products, spread_back(): lax.dot_general(weights[tap_index], window, (((0,), (0,)), ((), ())), pre...  3.9 us
    dot_general x18, matrix products, conv_cells(): jnp.dot(weights[tap_index], window, preferred_element_type=jnp.float32)  3.74 us
  transfers between devices with their start and end apart: 20, of which 15 were waited for; matrix products, arithmetic and copies ran while one was open for 3% of the time, Pallas kernels for 0%

profile of v5, /device:TPU:1, one launch (start us, length us, event | category | flops | bytes accessed | tf_op | source)
XLA Modules:
  0.0 178.9 jit_solution(937537682552529450)
XLA Ops:
  0.6 0.9 copy.88
  2.2 0.9 copy-done.1
  6.1 5.4 %collective-permute-start.1 = (bf16[9,96,16]{1,2,0:T(8,128)(2,1)S(1)}, bf16[9,96,16]{1,2,0:T(8,128)(2,1)S(1)}, u32[]{:S(2)}, u32[]{:S(2)}) collective-permute-start(bf16[9,96,16]{1,2,0:T(8,128)(2,1)S(1)} %constant_dynamic-update-slice_fusion), channel_id=1, source_target_pairs={{0,511},{1,2},{2,1},{3,4},{4,3},{5,6},{6,5},{7,8},{8,7},{9,10},{10... | collective-permute-start | bytes 82952 | tf_op jit(solution)/shard_map/ppermute | solution.py:60
  11.5 13.5 %collective-permute-start = (bf16[9,96,16]{1,2,0:T(8,128)(2,1)S(1)}, bf16[9,96,16]{1,2,0:T(8,128)(2,1)S(1)}, u32[]{:S(2)}, u32[]{:S(2)}) collective-permute-start(bf16[9,96,16]{1,2,0:T(8,128)(2,1)S(1)} %constant_dynamic-update-slice_fusion), channel_id=1, source_target_pairs={{0,1},{1,0},{2,3},{3,2},{4,5},{5,4},{6,7},{7,6},{8,9},{9,8},{10,11... | collective-permute-start | bytes 82952 | tf_op jit(solution)/shard_map/ppermute | solution.py:59
  25.1 0.6 copy-done.6
  25.7 0.6 copy-done.4
  26.4 0.6 copy-done.11
  27.3 0.6 copy-done.10
  28.7 1.9 %collective-permute-start.3 = (bf16[9,96,16]{1,2,0:T(8,128)(2,1)S(1)}, bf16[9,96,16]{1,2,0:T(8,128)(2,1)S(1)}, u32[]{:S(2)}, u32[]{:S(2)}) collective-permute-start(bf16[9,96,16]{1,2,0:T(8,128)(2,1)S(1)} %constant_dynamic-update-slice_fusion.9), channel_id=1, source_target_pairs={{0,8},{1,9},{2,10},{3,11},{4,12},{5,13},{6,14},{7,15},{8,0},{9,1},... | collective-permute-start | bytes 82952 | tf_op jit(solution)/shard_map/ppermute | solution.py:59
  30.7 7.5 %collective-permute-start.2 = (bf16[9,96,16]{1,2,0:T(8,128)(2,1)S(1)}, bf16[9,96,16]{1,2,0:T(8,128)(2,1)S(1)}, u32[]{:S(2)}, u32[]{:S(2)}) collective-permute-start(bf16[9,96,16]{1,2,0:T(8,128)(2,1)S(1)} %constant_dynamic-update-slice_fusion.9), channel_id=1, source_target_pairs={{0,504},{1,505},{2,506},{3,507},{4,508},{5,509},{6,510},{7,511},{8... | collective-permute-start | bytes 82952 | tf_op jit(solution)/shard_map/ppermute | solution.py:60
  38.4 5.1 %collective-permute-done.2 = bf16[9,96,16]{1,2,0:T(8,128)(2,1)S(1)} collective-permute-done((bf16[9,96,16]{1,2,0:T(8,128)(2,1)S(1)}, bf16[9,96,16]{1,2,0:T(8,128)(2,1)S(1)}, u32[]{:S(2)}, u32[]{:S(2)}) %collective-permute-start.2) | collective-permute-done | bytes 27680 | tf_op jit(solution)/shard_map/ppermute | solution.py:60
  46.2 0.7 scatter_fusion
  47.5 0.9 copy-done.2
  49.0 0.6 copy-done.3
  50.3 0.6 copy-done.9
  54.8 1.9 %collective-permute-start.5 = (bf16[9,96,16]{1,2,0:T(8,128)(2,1)S(1)}, bf16[9,96,16]{1,2,0:T(8,128)(2,1)S(1)}, u32[]{:S(2)}, u32[]{:S(2)}) collective-permute-start(bf16[9,96,16]{1,2,0:T(8,128)(2,1)S(1)} %constant_dynamic-update-slice_fusion.18), channel_id=1, source_target_pairs={{0,511},{1,2},{2,1},{3,4},{4,3},{5,6},{6,5},{7,8},{8,7},{9,10},{10... | collective-permute-start | bytes 82952 | tf_op jit(solution)/shard_map/ppermute | solution.py:60
  56.7 5.2 %collective-permute-start.4 = (bf16[9,96,16]{1,2,0:T(8,128)(2,1)S(1)}, bf16[9,96,16]{1,2,0:T(8,128)(2,1)S(1)}, u32[]{:S(2)}, u32[]{:S(2)}) collective-permute-start(bf16[9,96,16]{1,2,0:T(8,128)(2,1)S(1)} %constant_dynamic-update-slice_fusion.18), channel_id=1, source_target_pairs={{0,1},{1,0},{2,3},{3,2},{4,5},{5,4},{6,7},{7,6},{8,9},{9,8},{10,11... | collective-permute-start | bytes 82952 | tf_op jit(solution)/shard_map/ppermute | solution.py:59
  62.9 2.1 %collective-permute-start.7 = (bf16[9,96,16]{1,2,0:T(8,128)(2,1)S(1)}, bf16[9,96,16]{1,2,0:T(8,128)(2,1)S(1)}, u32[]{:S(2)}, u32[]{:S(2)}) collective-permute-start(bf16[9,96,16]{1,2,0:T(8,128)(2,1)S(1)} %constant_dynamic-update-slice_fusion.27), channel_id=1, source_target_pairs={{0,8},{1,9},{2,10},{3,11},{4,12},{5,13},{6,14},{7,15},{8,0},{9,1},... | collective-permute-start | bytes 82952 | tf_op jit(solution)/shard_map/ppermute | solution.py:59
  65.1 5.5 %collective-permute-start.6 = (bf16[9,96,16]{1,2,0:T(8,128)(2,1)S(1)}, bf16[9,96,16]{1,2,0:T(8,128)(2,1)S(1)}, u32[]{:S(2)}, u32[]{:S(2)}) collective-permute-start(bf16[9,96,16]{1,2,0:T(8,128)(2,1)S(1)} %constant_dynamic-update-slice_fusion.27), channel_id=1, source_target_pairs={{0,504},{1,505},{2,506},{3,507},{4,508},{5,509},{6,510},{7,511},{8... | collective-permute-start | bytes 82952 | tf_op jit(solution)/shard_map/ppermute | solution.py:60
  71.5 6.4 %collective-permute-done.6 = bf16[9,96,16]{1,2,0:T(8,128)(2,1)S(1)} collective-permute-done((bf16[9,96,16]{1,2,0:T(8,128)(2,1)S(1)}, bf16[9,96,16]{1,2,0:T(8,128)(2,1)S(1)}, u32[]{:S(2)}, u32[]{:S(2)}) %collective-permute-start.6) | collective-permute-done | bytes 27680 | tf_op jit(solution)/shard_map/ppermute | solution.py:60
  82.8 6.8 %collective-permute-start.8 = (f32[83456]{0:T(1024)S(1)}, f32[83456]{0:T(1024)S(1)}, u32[]{:S(2)}, u32[]{:S(2)}) collective-permute-start(f32[83456]{0:T(1024)S(1)} %broadcast_select_fusion), channel_id=1, source_target_pairs={{0,1},{1,0},{2,3},{3,2},{4,5},{5,4},{6,7},{7,6},{8,9},{9,8},{10,11... | collective-permute-start | bytes 1001480 | tf_op jit(solution)/shard_map/ppermute | solution.py:23
  89.9 0.9 collective-permute-done.8
  90.9 1.9 %collective-permute-start.9 = (f32[41728]{0:T(1024)S(1)}, f32[41728]{0:T(1024)S(1)}, u32[]{:S(2)}, u32[]{:S(2)}) collective-permute-start(f32[41728]{0:T(1024)S(1)} %slice_select_fusion), channel_id=1, source_target_pairs={{0,2},{1,3},{2,0},{3,1},{4,6},{5,7},{6,4},{7,5},{8,10},{9,11},{10,... | collective-permute-start | bytes 500744 | tf_op jit(solution)/shard_map/ppermute | solution.py:23
  93.0 5.3 %collective-permute-done.9 = f32[41728]{0:T(1024)S(1)} collective-permute-done((f32[41728]{0:T(1024)S(1)}, f32[41728]{0:T(1024)S(1)}, u32[]{:S(2)}, u32[]{:S(2)}) %collective-permute-start.9) | collective-permute-done | bytes 166944 | tf_op jit(solution)/shard_map/ppermute | solution.py:23
  98.3 1.9 %collective-permute-start.10 = (f32[20864]{0:T(1024)S(1)}, f32[20864]{0:T(1024)S(1)}, u32[]{:S(2)}, u32[]{:S(2)}) collective-permute-start(f32[20864]{0:T(1024)S(1)} %slice_select_fusion.1), channel_id=1, source_target_pairs={{0,4},{1,5},{2,6},{3,7},{4,0},{5,1},{6,2},{7,3},{8,12},{9,13},{10,... | collective-permute-start | bytes 250376 | tf_op jit(solution)/shard_map/ppermute | solution.py:23
  100.4 6.6 %collective-permute-done.10 = f32[20864]{0:T(1024)S(1)} collective-permute-done((f32[20864]{0:T(1024)S(1)}, f32[20864]{0:T(1024)S(1)}, u32[]{:S(2)}, u32[]{:S(2)}) %collective-permute-start.10) | collective-permute-done | bytes 83488 | tf_op jit(solution)/shard_map/ppermute | solution.py:23
  107.0 4.2 %collective-permute-start.11 = (f32[20864]{0:T(1024)S(1)}, f32[20864]{0:T(1024)S(1)}, u32[]{:S(2)}, u32[]{:S(2)}) collective-permute-start(f32[20864]{0:T(1024)S(1)} %select_add_fusion.2), channel_id=1, source_target_pairs={{0,8},{1,9},{2,10},{3,11},{4,12},{5,13},{6,14},{7,15},{8,0},{9,1},... | collective-permute-start | bytes 250376 | tf_op jit(solution)/shard_map/ppermute | solution.py:23
  111.8 6.2 %collective-permute-done.11 = f32[20864]{0:T(1024)S(1)} collective-permute-done((f32[20864]{0:T(1024)S(1)}, f32[20864]{0:T(1024)S(1)}, u32[]{:S(2)}, u32[]{:S(2)}) %collective-permute-start.11) | collective-permute-done | bytes 83488 | tf_op jit(solution)/shard_map/ppermute | solution.py:23
  118.0 1.9 %collective-permute-start.12 = (f32[20864]{0:T(1024)S(1)}, f32[20864]{0:T(1024)S(1)}, u32[]{:S(2)}, u32[]{:S(2)}) collective-permute-start(f32[20864]{0:T(1024)S(1)} %add.548), channel_id=1, source_target_pairs={{0,16},{1,17},{2,18},{3,19},{4,20},{5,21},{6,22},{7,23},{8,24},{9,... | collective-permute-start | bytes 250376 | tf_op jit(solution)/shard_map/ppermute | solution.py:23
  120.0 3.3 %collective-permute-done.12 = f32[20864]{0:T(1024)S(1)} collective-permute-done((f32[20864]{0:T(1024)S(1)}, f32[20864]{0:T(1024)S(1)}, u32[]{:S(2)}, u32[]{:S(2)}) %collective-permute-start.12) | collective-permute-done | bytes 83488 | tf_op jit(solution)/shard_map/ppermute | solution.py:23
  123.3 1.9 %collective-permute-start.13 = (f32[20864]{0:T(1024)S(1)}, f32[20864]{0:T(1024)S(1)}, u32[]{:S(2)}, u32[]{:S(2)}) collective-permute-start(f32[20864]{0:T(1024)S(1)} %add.549), channel_id=1, source_target_pairs={{0,32},{1,33},{2,34},{3,35},{4,36},{5,37},{6,38},{7,39},{8,40},{9,... | collective-permute-start | bytes 250376 | tf_op jit(solution)/shard_map/ppermute | solution.py:23
  125.2 4.8 %collective-permute-done.13 = f32[20864]{0:T(1024)S(1)} collective-permute-done((f32[20864]{0:T(1024)S(1)}, f32[20864]{0:T(1024)S(1)}, u32[]{:S(2)}, u32[]{:S(2)}) %collective-permute-start.13) | collective-permute-done | bytes 83488 | tf_op jit(solution)/shard_map/ppermute | solution.py:23
  130.0 1.9 %collective-permute-start.14 = (f32[20864]{0:T(1024)S(1)}, f32[20864]{0:T(1024)S(1)}, u32[]{:S(2)}, u32[]{:S(2)}) collective-permute-start(f32[20864]{0:T(1024)S(1)} %add.550), channel_id=1, source_target_pairs={{0,64},{1,65},{2,66},{3,67},{4,68},{5,69},{6,70},{7,71},{8,72},{9,... | collective-permute-start | bytes 250376 | tf_op jit(solution)/shard_map/ppermute | solution.py:23
  132.0 3.3 %collective-permute-done.14 = f32[20864]{0:T(1024)S(1)} collective-permute-done((f32[20864]{0:T(1024)S(1)}, f32[20864]{0:T(1024)S(1)}, u32[]{:S(2)}, u32[]{:S(2)}) %collective-permute-start.14) | collective-permute-done | bytes 83488 | tf_op jit(solution)/shard_map/ppermute | solution.py:23
  135.3 1.9 %collective-permute-start.15 = (f32[20864]{0:T(1024)S(1)}, f32[20864]{0:T(1024)S(1)}, u32[]{:S(2)}, u32[]{:S(2)}) collective-permute-start(f32[20864]{0:T(1024)S(1)} %add.551), channel_id=1, source_target_pairs={{0,128},{1,129},{2,130},{3,131},{4,132},{5,133},{6,134},{7,135},{8... | collective-permute-start | bytes 250376 | tf_op jit(solution)/shard_map/ppermute | solution.py:23
  137.2 0.7 scatter_fusion.1
  138.0 4.1 %collective-permute-done.15 = f32[20864]{0:T(1024)S(1)} collective-permute-done((f32[20864]{0:T(1024)S(1)}, f32[20864]{0:T(1024)S(1)}, u32[]{:S(2)}, u32[]{:S(2)}) %collective-permute-start.15) | collective-permute-done | bytes 83488 | tf_op jit(solution)/shard_map/ppermute | solution.py:23
  142.1 4.6 %collective-permute-start.16 = (f32[20864]{0:T(1024)S(1)}, f32[20864]{0:T(1024)S(1)}, u32[]{:S(2)}, u32[]{:S(2)}) collective-permute-start(f32[20864]{0:T(1024)S(1)} %add.552), channel_id=1, source_target_pairs={{0,256},{1,257},{2,258},{3,259},{4,260},{5,261},{6,262},{7,263},{8... | collective-permute-start | bytes 250376 | tf_op jit(solution)/shard_map/ppermute | solution.py:23
  146.8 5.2 %collective-permute-done.16 = f32[20864]{0:T(1024)S(1)} collective-permute-done((f32[20864]{0:T(1024)S(1)}, f32[20864]{0:T(1024)S(1)}, u32[]{:S(2)}, u32[]{:S(2)}) %collective-permute-start.16) | collective-permute-done | bytes 83488 | tf_op jit(solution)/shard_map/ppermute | solution.py:23
  152.1 1.9 %collective-permute-start.17 = (f32[20864]{0:T(1024)S(1)}, f32[20864]{0:T(1024)S(1)}, u32[]{:S(2)}, u32[]{:S(2)}) collective-permute-start(f32[20864]{0:T(1024)S(1)} %add.553), channel_id=1, source_target_pairs={{0,4},{1,5},{2,6},{3,7},{4,0},{5,1},{6,2},{7,3},{8,12},{9,13},{10,... | collective-permute-start | bytes 250376 | tf_op jit(solution)/shard_map/ppermute | solution.py:23
  154.0 0.7 copy.119
  154.7 3.4 %collective-permute-done.17 = f32[20864]{0:T(1024)S(1)} collective-permute-done((f32[20864]{0:T(1024)S(1)}, f32[20864]{0:T(1024)S(1)}, u32[]{:S(2)}, u32[]{:S(2)}) %collective-permute-start.17) | collective-permute-done | bytes 83488 | tf_op jit(solution)/shard_map/ppermute | solution.py:23
  158.2 1.9 %collective-permute-start.18 = (f32[41728]{0:T(1024)S(1)}, f32[41728]{0:T(1024)S(1)}, u32[]{:S(2)}, u32[]{:S(2)}) collective-permute-start(f32[41728]{0:T(1024)S(1)} %maximum_select_fusion.2), channel_id=1, source_target_pairs={{0,2},{1,3},{2,0},{3,1},{4,6},{5,7},{6,4},{7,5},{8,10},{9,11},{10,... | collective-permute-start | bytes 500744 | tf_op jit(solution)/shard_map/ppermute | solution.py:23
  160.3 4.8 %collective-permute-done.18 = f32[41728]{0:T(1024)S(1)} collective-permute-done((f32[41728]{0:T(1024)S(1)}, f32[41728]{0:T(1024)S(1)}, u32[]{:S(2)}, u32[]{:S(2)}) %collective-permute-start.18) | collective-permute-done | bytes 166944 | tf_op jit(solution)/shard_map/ppermute | solution.py:23
  165.2 10.0 %collective-permute-start.19 = (f32[83456]{0:T(1024)S(1)}, f32[83456]{0:T(1024)S(1)}, u32[]{:S(2)}, u32[]{:S(2)}) collective-permute-start(f32[83456]{0:T(1024)S(1)} %maximum_select_fusion.1), channel_id=1, source_target_pairs={{0,1},{1,0},{2,3},{3,2},{4,5},{5,4},{6,7},{7,6},{8,9},{9,8},{10,11... | collective-permute-start | bytes 1001480 | tf_op jit(solution)/shard_map/ppermute | solution.py:23
  175.3 0.8 fusion.14
  177.1 0.9 mul.198
  178.0 0.9 mul.196
  (256 shorter events, 22.2 us)
Async XLA Ops:
  0.6 1.0 copy-start
  2.2 0.9 copy-start.1
  5.2 0.7 copy-start.8
  6.1 22.6 %collective-permute-start.1 = (bf16[9,96,16]{1,2,0:T(8,128)(2,1)S(1)}, bf16[9,96,16]{1,2,0:T(8,128)(2,1)S(1)}, u32[]{:S(2)}, u32[]{:S(2)}) collective-permute-start(bf16[9,96,16]{1,2,0:T(8,128)(2,1)S(1)} %constant_dynamic-update-slice_fusion), channel_id=1, source_target_pairs={{0,511},{1,2},{2,1},{3,4},{4,3},{5,6},{6,5},{7,8},{8,7},{9,10},{10... | collective-permute-start | bytes 82952 | tf_op jit(solution)/shard_map/ppermute | solution.py:60
  11.5 17.2 %collective-permute-start = (bf16[9,96,16]{1,2,0:T(8,128)(2,1)S(1)}, bf16[9,96,16]{1,2,0:T(8,128)(2,1)S(1)}, u32[]{:S(2)}, u32[]{:S(2)}) collective-permute-start(bf16[9,96,16]{1,2,0:T(8,128)(2,1)S(1)} %constant_dynamic-update-slice_fusion), channel_id=1, source_target_pairs={{0,1},{1,0},{2,3},{3,2},{4,5},{5,4},{6,7},{7,6},{8,9},{9,8},{10,11... | collective-permute-start | bytes 82952 | tf_op jit(solution)/shard_map/ppermute | solution.py:59
  25.0 0.7 copy-start.6
  25.7 0.7 copy-start.4
  25.7 0.7 copy-start.5
  26.4 0.7 copy-start.11
  27.3 0.7 copy-start.10
  27.9 0.7 copy-start.7
  28.7 9.6 %collective-permute-start.3 = (bf16[9,96,16]{1,2,0:T(8,128)(2,1)S(1)}, bf16[9,96,16]{1,2,0:T(8,128)(2,1)S(1)}, u32[]{:S(2)}, u32[]{:S(2)}) collective-permute-start(bf16[9,96,16]{1,2,0:T(8,128)(2,1)S(1)} %constant_dynamic-update-slice_fusion.9), channel_id=1, source_target_pairs={{0,8},{1,9},{2,10},{3,11},{4,12},{5,13},{6,14},{7,15},{8,0},{9,1},... | collective-permute-start | bytes 82952 | tf_op jit(solution)/shard_map/ppermute | solution.py:59
  30.7 12.8 %collective-permute-start.2 = (bf16[9,96,16]{1,2,0:T(8,128)(2,1)S(1)}, bf16[9,96,16]{1,2,0:T(8,128)(2,1)S(1)}, u32[]{:S(2)}, u32[]{:S(2)}) collective-permute-start(bf16[9,96,16]{1,2,0:T(8,128)(2,1)S(1)} %constant_dynamic-update-slice_fusion.9), channel_id=1, source_target_pairs={{0,504},{1,505},{2,506},{3,507},{4,508},{5,509},{6,510},{7,511},{8... | collective-permute-start | bytes 82952 | tf_op jit(solution)/shard_map/ppermute | solution.py:60
  47.4 0.9 copy-start.2
  48.9 0.8 copy-start.3
  50.3 0.7 copy-start.9
  54.8 8.1 %collective-permute-start.5 = (bf16[9,96,16]{1,2,0:T(8,128)(2,1)S(1)}, bf16[9,96,16]{1,2,0:T(8,128)(2,1)S(1)}, u32[]{:S(2)}, u32[]{:S(2)}) collective-permute-start(bf16[9,96,16]{1,2,0:T(8,128)(2,1)S(1)} %constant_dynamic-update-slice_fusion.18), channel_id=1, source_target_pairs={{0,511},{1,2},{2,1},{3,4},{4,3},{5,6},{6,5},{7,8},{8,7},{9,10},{10... | collective-permute-start | bytes 82952 | tf_op jit(solution)/shard_map/ppermute | solution.py:60
  56.7 6.2 %collective-permute-start.4 = (bf16[9,96,16]{1,2,0:T(8,128)(2,1)S(1)}, bf16[9,96,16]{1,2,0:T(8,128)(2,1)S(1)}, u32[]{:S(2)}, u32[]{:S(2)}) collective-permute-start(bf16[9,96,16]{1,2,0:T(8,128)(2,1)S(1)} %constant_dynamic-update-slice_fusion.18), channel_id=1, source_target_pairs={{0,1},{1,0},{2,3},{3,2},{4,5},{5,4},{6,7},{7,6},{8,9},{9,8},{10,11... | collective-permute-start | bytes 82952 | tf_op jit(solution)/shard_map/ppermute | solution.py:59
  62.9 8.6 %collective-permute-start.7 = (bf16[9,96,16]{1,2,0:T(8,128)(2,1)S(1)}, bf16[9,96,16]{1,2,0:T(8,128)(2,1)S(1)}, u32[]{:S(2)}, u32[]{:S(2)}) collective-permute-start(bf16[9,96,16]{1,2,0:T(8,128)(2,1)S(1)} %constant_dynamic-update-slice_fusion.27), channel_id=1, source_target_pairs={{0,8},{1,9},{2,10},{3,11},{4,12},{5,13},{6,14},{7,15},{8,0},{9,1},... | collective-permute-start | bytes 82952 | tf_op jit(solution)/shard_map/ppermute | solution.py:59
  65.1 12.8 %collective-permute-start.6 = (bf16[9,96,16]{1,2,0:T(8,128)(2,1)S(1)}, bf16[9,96,16]{1,2,0:T(8,128)(2,1)S(1)}, u32[]{:S(2)}, u32[]{:S(2)}) collective-permute-start(bf16[9,96,16]{1,2,0:T(8,128)(2,1)S(1)} %constant_dynamic-update-slice_fusion.27), channel_id=1, source_target_pairs={{0,504},{1,505},{2,506},{3,507},{4,508},{5,509},{6,510},{7,511},{8... | collective-permute-start | bytes 82952 | tf_op jit(solution)/shard_map/ppermute | solution.py:60
  82.8 8.0 %collective-permute-start.8 = (f32[83456]{0:T(1024)S(1)}, f32[83456]{0:T(1024)S(1)}, u32[]{:S(2)}, u32[]{:S(2)}) collective-permute-start(f32[83456]{0:T(1024)S(1)} %broadcast_select_fusion), channel_id=1, source_target_pairs={{0,1},{1,0},{2,3},{3,2},{4,5},{5,4},{6,7},{7,6},{8,9},{9,8},{10,11... | collective-permute-start | bytes 1001480 | tf_op jit(solution)/shard_map/ppermute | solution.py:23
  90.9 7.4 %collective-permute-start.9 = (f32[41728]{0:T(1024)S(1)}, f32[41728]{0:T(1024)S(1)}, u32[]{:S(2)}, u32[]{:S(2)}) collective-permute-start(f32[41728]{0:T(1024)S(1)} %slice_select_fusion), channel_id=1, source_target_pairs={{0,2},{1,3},{2,0},{3,1},{4,6},{5,7},{6,4},{7,5},{8,10},{9,11},{10,... | collective-permute-start | bytes 500744 | tf_op jit(solution)/shard_map/ppermute | solution.py:23
  98.3 8.7 %collective-permute-start.10 = (f32[20864]{0:T(1024)S(1)}, f32[20864]{0:T(1024)S(1)}, u32[]{:S(2)}, u32[]{:S(2)}) collective-permute-start(f32[20864]{0:T(1024)S(1)} %slice_select_fusion.1), channel_id=1, source_target_pairs={{0,4},{1,5},{2,6},{3,7},{4,0},{5,1},{6,2},{7,3},{8,12},{9,13},{10,... | collective-permute-start | bytes 250376 | tf_op jit(solution)/shard_map/ppermute | solution.py:23
  107.0 11.0 %collective-permute-start.11 = (f32[20864]{0:T(1024)S(1)}, f32[20864]{0:T(1024)S(1)}, u32[]{:S(2)}, u32[]{:S(2)}) collective-permute-start(f32[20864]{0:T(1024)S(1)} %select_add_fusion.2), channel_id=1, source_target_pairs={{0,8},{1,9},{2,10},{3,11},{4,12},{5,13},{6,14},{7,15},{8,0},{9,1},... | collective-permute-start | bytes 250376 | tf_op jit(solution)/shard_map/ppermute | solution.py:23
  118.0 5.2 %collective-permute-start.12 = (f32[20864]{0:T(1024)S(1)}, f32[20864]{0:T(1024)S(1)}, u32[]{:S(2)}, u32[]{:S(2)}) collective-permute-start(f32[20864]{0:T(1024)S(1)} %add.548), channel_id=1, source_target_pairs={{0,16},{1,17},{2,18},{3,19},{4,20},{5,21},{6,22},{7,23},{8,24},{9,... | collective-permute-start | bytes 250376 | tf_op jit(solution)/shard_map/ppermute | solution.py:23
  123.3 6.7 %collective-permute-start.13 = (f32[20864]{0:T(1024)S(1)}, f32[20864]{0:T(1024)S(1)}, u32[]{:S(2)}, u32[]{:S(2)}) collective-permute-start(f32[20864]{0:T(1024)S(1)} %add.549), channel_id=1, source_target_pairs={{0,32},{1,33},{2,34},{3,35},{4,36},{5,37},{6,38},{7,39},{8,40},{9,... | collective-permute-start | bytes 250376 | tf_op jit(solution)/shard_map/ppermute | solution.py:23
  130.0 5.2 %collective-permute-start.14 = (f32[20864]{0:T(1024)S(1)}, f32[20864]{0:T(1024)S(1)}, u32[]{:S(2)}, u32[]{:S(2)}) collective-permute-start(f32[20864]{0:T(1024)S(1)} %add.550), channel_id=1, source_target_pairs={{0,64},{1,65},{2,66},{3,67},{4,68},{5,69},{6,70},{7,71},{8,72},{9,... | collective-permute-start | bytes 250376 | tf_op jit(solution)/shard_map/ppermute | solution.py:23
  135.3 6.8 %collective-permute-start.15 = (f32[20864]{0:T(1024)S(1)}, f32[20864]{0:T(1024)S(1)}, u32[]{:S(2)}, u32[]{:S(2)}) collective-permute-start(f32[20864]{0:T(1024)S(1)} %add.551), channel_id=1, source_target_pairs={{0,128},{1,129},{2,130},{3,131},{4,132},{5,133},{6,134},{7,135},{8... | collective-permute-start | bytes 250376 | tf_op jit(solution)/shard_map/ppermute | solution.py:23
  142.1 10.0 %collective-permute-start.16 = (f32[20864]{0:T(1024)S(1)}, f32[20864]{0:T(1024)S(1)}, u32[]{:S(2)}, u32[]{:S(2)}) collective-permute-start(f32[20864]{0:T(1024)S(1)} %add.552), channel_id=1, source_target_pairs={{0,256},{1,257},{2,258},{3,259},{4,260},{5,261},{6,262},{7,263},{8... | collective-permute-start | bytes 250376 | tf_op jit(solution)/shard_map/ppermute | solution.py:23
  152.1 6.1 %collective-permute-start.17 = (f32[20864]{0:T(1024)S(1)}, f32[20864]{0:T(1024)S(1)}, u32[]{:S(2)}, u32[]{:S(2)}) collective-permute-start(f32[20864]{0:T(1024)S(1)} %add.553), channel_id=1, source_target_pairs={{0,4},{1,5},{2,6},{3,7},{4,0},{5,1},{6,2},{7,3},{8,12},{9,13},{10,... | collective-permute-start | bytes 250376 | tf_op jit(solution)/shard_map/ppermute | solution.py:23
  158.2 6.9 %collective-permute-start.18 = (f32[41728]{0:T(1024)S(1)}, f32[41728]{0:T(1024)S(1)}, u32[]{:S(2)}, u32[]{:S(2)}) collective-permute-start(f32[41728]{0:T(1024)S(1)} %maximum_select_fusion.2), channel_id=1, source_target_pairs={{0,2},{1,3},{2,0},{3,1},{4,6},{5,7},{6,4},{7,5},{8,10},{9,11},{10,... | collective-permute-start | bytes 500744 | tf_op jit(solution)/shard_map/ppermute | solution.py:23
  165.2 11.3 %collective-permute-start.19 = (f32[83456]{0:T(1024)S(1)}, f32[83456]{0:T(1024)S(1)}, u32[]{:S(2)}, u32[]{:S(2)}) collective-permute-start(f32[83456]{0:T(1024)S(1)} %maximum_select_fusion.1), channel_id=1, source_target_pairs={{0,1},{1,0},{2,3},{3,2},{4,5},{5,4},{6,7},{7,6},{8,9},{9,8},{10,11... | collective-permute-start | bytes 1001480 | tf_op jit(solution)/shard_map/ppermute | solution.py:23

commit v6 on v5

--- a/solution.py
+++ b/solution.py
@@ -136,13 +136,15 @@
     )
     reverse = (edge_codes >= 4)[:, None, None]
     their_side = edge_codes % 4
-    out = []
-    for g in range(groups):
-        picked = stacked[edge_class * n_strips + 4 * g + their_side]
-        picked = jnp.where(reverse, picked[:, :, ::-1], picked)
-        corner_got = corner_stack[diag_class * n_strips + 4 * g + corner_codes]
-        out.append((picked, corner_got))
-    return out
+    group_ids = jnp.arange(groups, dtype=jnp.int32)[:, None] * 4
+    strip_index = (edge_class * n_strips + their_side)[None, :] + group_ids
+    corner_index = (diag_class * n_strips + corner_codes)[None, :] + group_ids
+    picked_all = stacked[strip_index.reshape(-1)].reshape((groups, 4) + stacked.shape[1:])
+    picked_all = jnp.where(reverse[None], picked_all[..., ::-1], picked_all)
+    corner_all = corner_stack[corner_index.reshape(-1)].reshape(
+        (groups, 4) + corner_stack.shape[1:]
+    )
+    return [(picked_all[g], corner_all[g]) for g in range(groups)]
 
 
 def assemble_padded(tile_field, picked, corner_got, missing):
@@ -181,8 +183,7 @@
         ],
         axis=-2,
     )
-    full = jnp.zeros_like(summed)
-    full = full.at[:, 0::side - 1, 0::side - 1].set(corner_grid)
+    full = lax.pad(corner_grid, jnp.float32(0), ((0, 0, 0), (0, 0, side - 2), (0, 0, side - 2)))
     return summed + full
 
 

time: 180 us -> 178 us (0.989)
  local copies, waits for them, and re-layouts: 19.6 us -> 16 us
    gather x8 -> x4, local copies, waits for them, and re-layouts: 4.49 us -> 2.26 us  [the longest x2 1.13 us: exchange_groups(): corner_stack[corner_index.reshape(-1)]]
where the time goes in v6:
time: 178 us; the launch traced here: 177 us
  starting transfers between devices  84.1 us (47%)
  waiting for transfers between devices  61.7 us (35%)
  local copies, waits for them, and re-layouts  16 us (9%)
  matrix products  10.5 us (6%)
  other arithmetic  2.6 us (1%)
  between operations  1.95 us (1%)
    ppermute x12, waiting for transfers between devices, xor_partner(): lax.ppermute(block, 'tiles', [(i, i ^ distance) for i in range(devices)])  49.6 us
    ppermute x12, starting transfers between devices, xor_partner(): lax.ppermute(block, 'tiles', [(i, i ^ distance) for i in range(devices)])  41 us
    ppermute x4, starting transfers between devices, paired_shift(): got_flip = lax.ppermute(block, 'tiles', flip)  22.7 us
    ppermute x4, starting transfers between devices, paired_shift(): got_other = lax.ppermute(block, 'tiles', other)  20.3 us
    ppermute x4, waiting for transfers between devices, paired_shift(): got_other = lax.ppermute(block, 'tiles', other)  11.6 us
    unnamed x45, local copies, waits for them, and re-layouts  8.66 us
    dot_general x18, matrix products, spread_back(): lax.dot_general(weights[tap_index], window, (((0,), (0,)), ((), ())), pre...  3.9 us
    dot_general x18, matrix products, conv_cells(): jnp.dot(weights[tap_index], window, preferred_element_type=jnp.float32)  3.77 us
  transfers between devices with their start and end apart: 20, of which 15 were waited for; matrix products, arithmetic and copies ran while one was open for 3% of the time, Pallas kernels for 0%

profile of v6, /device:TPU:1, one launch (start us, length us, event | category | flops | bytes accessed | tf_op | source)
XLA Modules:
  0.0 176.8 jit_solution(18443735533978226488)
XLA Ops:
  0.6 0.9 copy.140
  2.2 0.9 copy-done.1
  5.3 0.6 copy-done.6
  6.1 5.4 %collective-permute-start.1 = (bf16[9,96,16]{1,2,0:T(8,128)(2,1)S(1)}, bf16[9,96,16]{1,2,0:T(8,128)(2,1)S(1)}, u32[]{:S(2)}, u32[]{:S(2)}) collective-permute-start(bf16[9,96,16]{1,2,0:T(8,128)(2,1)S(1)} %constant_dynamic-update-slice_fusion), channel_id=1, source_target_pairs={{0,511},{1,2},{2,1},{3,4},{4,3},{5,6},{6,5},{7,8},{8,7},{9,10},{10... | collective-permute-start | bytes 82952 | tf_op jit(solution)/shard_map/ppermute | solution.py:60
  11.5 13.5 %collective-permute-start = (bf16[9,96,16]{1,2,0:T(8,128)(2,1)S(1)}, bf16[9,96,16]{1,2,0:T(8,128)(2,1)S(1)}, u32[]{:S(2)}, u32[]{:S(2)}) collective-permute-start(bf16[9,96,16]{1,2,0:T(8,128)(2,1)S(1)} %constant_dynamic-update-slice_fusion), channel_id=1, source_target_pairs={{0,1},{1,0},{2,3},{3,2},{4,5},{5,4},{6,7},{7,6},{8,9},{9,8},{10,11... | collective-permute-start | bytes 82952 | tf_op jit(solution)/shard_map/ppermute | solution.py:59
  25.0 0.6 copy-done.7
  25.7 0.6 copy-done.4
  26.4 0.6 copy-done.11
  27.2 0.6 copy-done.10
  28.9 1.9 %collective-permute-start.3 = (bf16[9,96,16]{1,2,0:T(8,128)(2,1)S(1)}, bf16[9,96,16]{1,2,0:T(8,128)(2,1)S(1)}, u32[]{:S(2)}, u32[]{:S(2)}) collective-permute-start(bf16[9,96,16]{1,2,0:T(8,128)(2,1)S(1)} %constant_dynamic-update-slice_fusion.9), channel_id=1, source_target_pairs={{0,8},{1,9},{2,10},{3,11},{4,12},{5,13},{6,14},{7,15},{8,0},{9,1},... | collective-permute-start | bytes 82952 | tf_op jit(solution)/shard_map/ppermute | solution.py:59
  30.8 7.5 %collective-permute-start.2 = (bf16[9,96,16]{1,2,0:T(8,128)(2,1)S(1)}, bf16[9,96,16]{1,2,0:T(8,128)(2,1)S(1)}, u32[]{:S(2)}, u32[]{:S(2)}) collective-permute-start(bf16[9,96,16]{1,2,0:T(8,128)(2,1)S(1)} %constant_dynamic-update-slice_fusion.9), channel_id=1, source_target_pairs={{0,504},{1,505},{2,506},{3,507},{4,508},{5,509},{6,510},{7,511},{8... | collective-permute-start | bytes 82952 | tf_op jit(solution)/shard_map/ppermute | solution.py:60
  38.4 5.2 %collective-permute-done.2 = bf16[9,96,16]{1,2,0:T(8,128)(2,1)S(1)} collective-permute-done((bf16[9,96,16]{1,2,0:T(8,128)(2,1)S(1)}, bf16[9,96,16]{1,2,0:T(8,128)(2,1)S(1)}, u32[]{:S(2)}, u32[]{:S(2)}) %collective-permute-start.2) | collective-permute-done | bytes 27680 | tf_op jit(solution)/shard_map/ppermute | solution.py:60
  44.4 0.6 gather_fusion
  45.7 0.9 copy-done.2
  47.3 0.6 copy-done.3
  48.6 0.6 copy-done.9
  53.0 1.9 %collective-permute-start.5 = (bf16[9,96,16]{1,2,0:T(8,128)(2,1)S(1)}, bf16[9,96,16]{1,2,0:T(8,128)(2,1)S(1)}, u32[]{:S(2)}, u32[]{:S(2)}) collective-permute-start(bf16[9,96,16]{1,2,0:T(8,128)(2,1)S(1)} %constant_dynamic-update-slice_fusion.18), channel_id=1, source_target_pairs={{0,511},{1,2},{2,1},{3,4},{4,3},{5,6},{6,5},{7,8},{8,7},{9,10},{10... | collective-permute-start | bytes 82952 | tf_op jit(solution)/shard_map/ppermute | solution.py:60
  54.9 5.2 %collective-permute-start.4 = (bf16[9,96,16]{1,2,0:T(8,128)(2,1)S(1)}, bf16[9,96,16]{1,2,0:T(8,128)(2,1)S(1)}, u32[]{:S(2)}, u32[]{:S(2)}) collective-permute-start(bf16[9,96,16]{1,2,0:T(8,128)(2,1)S(1)} %constant_dynamic-update-slice_fusion.18), channel_id=1, source_target_pairs={{0,1},{1,0},{2,3},{3,2},{4,5},{5,4},{6,7},{7,6},{8,9},{9,8},{10,11... | collective-permute-start | bytes 82952 | tf_op jit(solution)/shard_map/ppermute | solution.py:59
  61.2 2.1 %collective-permute-start.7 = (bf16[9,96,16]{1,2,0:T(8,128)(2,1)S(1)}, bf16[9,96,16]{1,2,0:T(8,128)(2,1)S(1)}, u32[]{:S(2)}, u32[]{:S(2)}) collective-permute-start(bf16[9,96,16]{1,2,0:T(8,128)(2,1)S(1)} %constant_dynamic-update-slice_fusion.27), channel_id=1, source_target_pairs={{0,8},{1,9},{2,10},{3,11},{4,12},{5,13},{6,14},{7,15},{8,0},{9,1},... | collective-permute-start | bytes 82952 | tf_op jit(solution)/shard_map/ppermute | solution.py:59
  63.3 5.5 %collective-permute-start.6 = (bf16[9,96,16]{1,2,0:T(8,128)(2,1)S(1)}, bf16[9,96,16]{1,2,0:T(8,128)(2,1)S(1)}, u32[]{:S(2)}, u32[]{:S(2)}) collective-permute-start(bf16[9,96,16]{1,2,0:T(8,128)(2,1)S(1)} %constant_dynamic-update-slice_fusion.27), channel_id=1, source_target_pairs={{0,504},{1,505},{2,506},{3,507},{4,508},{5,509},{6,510},{7,511},{8... | collective-permute-start | bytes 82952 | tf_op jit(solution)/shard_map/ppermute | solution.py:60
  69.8 6.4 %collective-permute-done.6 = bf16[9,96,16]{1,2,0:T(8,128)(2,1)S(1)} collective-permute-done((bf16[9,96,16]{1,2,0:T(8,128)(2,1)S(1)}, bf16[9,96,16]{1,2,0:T(8,128)(2,1)S(1)}, u32[]{:S(2)}, u32[]{:S(2)}) %collective-permute-start.6) | collective-permute-done | bytes 27680 | tf_op jit(solution)/shard_map/ppermute | solution.py:60
  80.6 6.8 %collective-permute-start.8 = (f32[83456]{0:T(1024)S(1)}, f32[83456]{0:T(1024)S(1)}, u32[]{:S(2)}, u32[]{:S(2)}) collective-permute-start(f32[83456]{0:T(1024)S(1)} %broadcast_select_fusion), channel_id=1, source_target_pairs={{0,1},{1,0},{2,3},{3,2},{4,5},{5,4},{6,7},{7,6},{8,9},{9,8},{10,11... | collective-permute-start | bytes 1001480 | tf_op jit(solution)/shard_map/ppermute | solution.py:23
  87.7 0.9 collective-permute-done.8
  88.7 1.9 %collective-permute-start.9 = (f32[41728]{0:T(1024)S(1)}, f32[41728]{0:T(1024)S(1)}, u32[]{:S(2)}, u32[]{:S(2)}) collective-permute-start(f32[41728]{0:T(1024)S(1)} %slice_select_fusion), channel_id=1, source_target_pairs={{0,2},{1,3},{2,0},{3,1},{4,6},{5,7},{6,4},{7,5},{8,10},{9,11},{10,... | collective-permute-start | bytes 500744 | tf_op jit(solution)/shard_map/ppermute | solution.py:23
  90.8 5.3 %collective-permute-done.9 = f32[41728]{0:T(1024)S(1)} collective-permute-done((f32[41728]{0:T(1024)S(1)}, f32[41728]{0:T(1024)S(1)}, u32[]{:S(2)}, u32[]{:S(2)}) %collective-permute-start.9) | collective-permute-done | bytes 166944 | tf_op jit(solution)/shard_map/ppermute | solution.py:23
  96.1 1.9 %collective-permute-start.10 = (f32[20864]{0:T(1024)S(1)}, f32[20864]{0:T(1024)S(1)}, u32[]{:S(2)}, u32[]{:S(2)}) collective-permute-start(f32[20864]{0:T(1024)S(1)} %slice_select_fusion.1), channel_id=1, source_target_pairs={{0,4},{1,5},{2,6},{3,7},{4,0},{5,1},{6,2},{7,3},{8,12},{9,13},{10,... | collective-permute-start | bytes 250376 | tf_op jit(solution)/shard_map/ppermute | solution.py:23
  98.1 6.7 %collective-permute-done.10 = f32[20864]{0:T(1024)S(1)} collective-permute-done((f32[20864]{0:T(1024)S(1)}, f32[20864]{0:T(1024)S(1)}, u32[]{:S(2)}, u32[]{:S(2)}) %collective-permute-start.10) | collective-permute-done | bytes 83488 | tf_op jit(solution)/shard_map/ppermute | solution.py:23
  104.8 4.2 %collective-permute-start.11 = (f32[20864]{0:T(1024)S(1)}, f32[20864]{0:T(1024)S(1)}, u32[]{:S(2)}, u32[]{:S(2)}) collective-permute-start(f32[20864]{0:T(1024)S(1)} %select_add_fusion.2), channel_id=1, source_target_pairs={{0,8},{1,9},{2,10},{3,11},{4,12},{5,13},{6,14},{7,15},{8,0},{9,1},... | collective-permute-start | bytes 250376 | tf_op jit(solution)/shard_map/ppermute | solution.py:23
  109.1 6.7 %collective-permute-done.11 = f32[20864]{0:T(1024)S(1)} collective-permute-done((f32[20864]{0:T(1024)S(1)}, f32[20864]{0:T(1024)S(1)}, u32[]{:S(2)}, u32[]{:S(2)}) %collective-permute-start.11) | collective-permute-done | bytes 83488 | tf_op jit(solution)/shard_map/ppermute | solution.py:23
  115.8 1.9 %collective-permute-start.12 = (f32[20864]{0:T(1024)S(1)}, f32[20864]{0:T(1024)S(1)}, u32[]{:S(2)}, u32[]{:S(2)}) collective-permute-start(f32[20864]{0:T(1024)S(1)} %add.500), channel_id=1, source_target_pairs={{0,16},{1,17},{2,18},{3,19},{4,20},{5,21},{6,22},{7,23},{8,24},{9,... | collective-permute-start | bytes 250376 | tf_op jit(solution)/shard_map/ppermute | solution.py:23
  117.8 3.3 %collective-permute-done.12 = f32[20864]{0:T(1024)S(1)} collective-permute-done((f32[20864]{0:T(1024)S(1)}, f32[20864]{0:T(1024)S(1)}, u32[]{:S(2)}, u32[]{:S(2)}) %collective-permute-start.12) | collective-permute-done | bytes 83488 | tf_op jit(solution)/shard_map/ppermute | solution.py:23
  121.1 1.9 %collective-permute-start.13 = (f32[20864]{0:T(1024)S(1)}, f32[20864]{0:T(1024)S(1)}, u32[]{:S(2)}, u32[]{:S(2)}) collective-permute-start(f32[20864]{0:T(1024)S(1)} %add.501), channel_id=1, source_target_pairs={{0,32},{1,33},{2,34},{3,35},{4,36},{5,37},{6,38},{7,39},{8,40},{9,... | collective-permute-start | bytes 250376 | tf_op jit(solution)/shard_map/ppermute | solution.py:23
  123.0 4.8 %collective-permute-done.13 = f32[20864]{0:T(1024)S(1)} collective-permute-done((f32[20864]{0:T(1024)S(1)}, f32[20864]{0:T(1024)S(1)}, u32[]{:S(2)}, u32[]{:S(2)}) %collective-permute-start.13) | collective-permute-done | bytes 83488 | tf_op jit(solution)/shard_map/ppermute | solution.py:23
  127.8 1.9 %collective-permute-start.14 = (f32[20864]{0:T(1024)S(1)}, f32[20864]{0:T(1024)S(1)}, u32[]{:S(2)}, u32[]{:S(2)}) collective-permute-start(f32[20864]{0:T(1024)S(1)} %add.502), channel_id=1, source_target_pairs={{0,64},{1,65},{2,66},{3,67},{4,68},{5,69},{6,70},{7,71},{8,72},{9,... | collective-permute-start | bytes 250376 | tf_op jit(solution)/shard_map/ppermute | solution.py:23
  129.8 3.3 %collective-permute-done.14 = f32[20864]{0:T(1024)S(1)} collective-permute-done((f32[20864]{0:T(1024)S(1)}, f32[20864]{0:T(1024)S(1)}, u32[]{:S(2)}, u32[]{:S(2)}) %collective-permute-start.14) | collective-permute-done | bytes 83488 | tf_op jit(solution)/shard_map/ppermute | solution.py:23
  133.1 1.9 %collective-permute-start.15 = (f32[20864]{0:T(1024)S(1)}, f32[20864]{0:T(1024)S(1)}, u32[]{:S(2)}, u32[]{:S(2)}) collective-permute-start(f32[20864]{0:T(1024)S(1)} %add.503), channel_id=1, source_target_pairs={{0,128},{1,129},{2,130},{3,131},{4,132},{5,133},{6,134},{7,135},{8... | collective-permute-start | bytes 250376 | tf_op jit(solution)/shard_map/ppermute | solution.py:23
  135.1 4.8 %collective-permute-done.15 = f32[20864]{0:T(1024)S(1)} collective-permute-done((f32[20864]{0:T(1024)S(1)}, f32[20864]{0:T(1024)S(1)}, u32[]{:S(2)}, u32[]{:S(2)}) %collective-permute-start.15) | collective-permute-done | bytes 83488 | tf_op jit(solution)/shard_map/ppermute | solution.py:23
  139.9 4.6 %collective-permute-start.16 = (f32[20864]{0:T(1024)S(1)}, f32[20864]{0:T(1024)S(1)}, u32[]{:S(2)}, u32[]{:S(2)}) collective-permute-start(f32[20864]{0:T(1024)S(1)} %add.504), channel_id=1, source_target_pairs={{0,256},{1,257},{2,258},{3,259},{4,260},{5,261},{6,262},{7,263},{8... | collective-permute-start | bytes 250376 | tf_op jit(solution)/shard_map/ppermute | solution.py:23
  144.6 5.2 %collective-permute-done.16 = f32[20864]{0:T(1024)S(1)} collective-permute-done((f32[20864]{0:T(1024)S(1)}, f32[20864]{0:T(1024)S(1)}, u32[]{:S(2)}, u32[]{:S(2)}) %collective-permute-start.16) | collective-permute-done | bytes 83488 | tf_op jit(solution)/shard_map/ppermute | solution.py:23
  149.9 1.9 %collective-permute-start.17 = (f32[20864]{0:T(1024)S(1)}, f32[20864]{0:T(1024)S(1)}, u32[]{:S(2)}, u32[]{:S(2)}) collective-permute-start(f32[20864]{0:T(1024)S(1)} %add.505), channel_id=1, source_target_pairs={{0,4},{1,5},{2,6},{3,7},{4,0},{5,1},{6,2},{7,3},{8,12},{9,13},{10,... | collective-permute-start | bytes 250376 | tf_op jit(solution)/shard_map/ppermute | solution.py:23
  151.8 0.7 copy.169
  152.6 3.4 %collective-permute-done.17 = f32[20864]{0:T(1024)S(1)} collective-permute-done((f32[20864]{0:T(1024)S(1)}, f32[20864]{0:T(1024)S(1)}, u32[]{:S(2)}, u32[]{:S(2)}) %collective-permute-start.17) | collective-permute-done | bytes 83488 | tf_op jit(solution)/shard_map/ppermute | solution.py:23
  156.0 1.9 %collective-permute-start.18 = (f32[41728]{0:T(1024)S(1)}, f32[41728]{0:T(1024)S(1)}, u32[]{:S(2)}, u32[]{:S(2)}) collective-permute-start(f32[41728]{0:T(1024)S(1)} %maximum_select_fusion.2), channel_id=1, source_target_pairs={{0,2},{1,3},{2,0},{3,1},{4,6},{5,7},{6,4},{7,5},{8,10},{9,11},{10,... | collective-permute-start | bytes 500744 | tf_op jit(solution)/shard_map/ppermute | solution.py:23
  158.1 4.8 %collective-permute-done.18 = f32[41728]{0:T(1024)S(1)} collective-permute-done((f32[41728]{0:T(1024)S(1)}, f32[41728]{0:T(1024)S(1)}, u32[]{:S(2)}, u32[]{:S(2)}) %collective-permute-start.18) | collective-permute-done | bytes 166944 | tf_op jit(solution)/shard_map/ppermute | solution.py:23
  163.0 10.0 %collective-permute-start.19 = (f32[83456]{0:T(1024)S(1)}, f32[83456]{0:T(1024)S(1)}, u32[]{:S(2)}, u32[]{:S(2)}) collective-permute-start(f32[83456]{0:T(1024)S(1)} %maximum_select_fusion.1), channel_id=1, source_target_pairs={{0,1},{1,0},{2,3},{3,2},{4,5},{5,4},{6,7},{7,6},{8,9},{9,8},{10,11... | collective-permute-start | bytes 1001480 | tf_op jit(solution)/shard_map/ppermute | solution.py:23
  173.2 0.8 fusion.14
  174.9 0.9 mul.185
  175.8 0.9 mul.183
  (247 shorter events, 18.8 us)
Async XLA Ops:
  0.6 1.0 copy-start
  2.1 0.9 copy-start.1
  5.2 0.7 copy-start.6
  6.1 22.7 %collective-permute-start.1 = (bf16[9,96,16]{1,2,0:T(8,128)(2,1)S(1)}, bf16[9,96,16]{1,2,0:T(8,128)(2,1)S(1)}, u32[]{:S(2)}, u32[]{:S(2)}) collective-permute-start(bf16[9,96,16]{1,2,0:T(8,128)(2,1)S(1)} %constant_dynamic-update-slice_fusion), channel_id=1, source_target_pairs={{0,511},{1,2},{2,1},{3,4},{4,3},{5,6},{6,5},{7,8},{8,7},{9,10},{10... | collective-permute-start | bytes 82952 | tf_op jit(solution)/shard_map/ppermute | solution.py:60
  11.5 17.3 %collective-permute-start = (bf16[9,96,16]{1,2,0:T(8,128)(2,1)S(1)}, bf16[9,96,16]{1,2,0:T(8,128)(2,1)S(1)}, u32[]{:S(2)}, u32[]{:S(2)}) collective-permute-start(bf16[9,96,16]{1,2,0:T(8,128)(2,1)S(1)} %constant_dynamic-update-slice_fusion), channel_id=1, source_target_pairs={{0,1},{1,0},{2,3},{3,2},{4,5},{5,4},{6,7},{7,6},{8,9},{9,8},{10,11... | collective-permute-start | bytes 82952 | tf_op jit(solution)/shard_map/ppermute | solution.py:59
  25.0 0.7 copy-start.7
  25.7 0.7 copy-start.4
  25.7 0.7 copy-start.5
  26.4 0.7 copy-start.11
  27.2 0.7 copy-start.10
  27.9 0.7 copy-start.8
  28.9 9.6 %collective-permute-start.3 = (bf16[9,96,16]{1,2,0:T(8,128)(2,1)S(1)}, bf16[9,96,16]{1,2,0:T(8,128)(2,1)S(1)}, u32[]{:S(2)}, u32[]{:S(2)}) collective-permute-start(bf16[9,96,16]{1,2,0:T(8,128)(2,1)S(1)} %constant_dynamic-update-slice_fusion.9), channel_id=1, source_target_pairs={{0,8},{1,9},{2,10},{3,11},{4,12},{5,13},{6,14},{7,15},{8,0},{9,1},... | collective-permute-start | bytes 82952 | tf_op jit(solution)/shard_map/ppermute | solution.py:59
  30.8 12.8 %collective-permute-start.2 = (bf16[9,96,16]{1,2,0:T(8,128)(2,1)S(1)}, bf16[9,96,16]{1,2,0:T(8,128)(2,1)S(1)}, u32[]{:S(2)}, u32[]{:S(2)}) collective-permute-start(bf16[9,96,16]{1,2,0:T(8,128)(2,1)S(1)} %constant_dynamic-update-slice_fusion.9), channel_id=1, source_target_pairs={{0,504},{1,505},{2,506},{3,507},{4,508},{5,509},{6,510},{7,511},{8... | collective-permute-start | bytes 82952 | tf_op jit(solution)/shard_map/ppermute | solution.py:60
  45.7 0.9 copy-start.2
  47.1 0.8 copy-start.3
  48.5 0.7 copy-start.9
  53.0 8.1 %collective-permute-start.5 = (bf16[9,96,16]{1,2,0:T(8,128)(2,1)S(1)}, bf16[9,96,16]{1,2,0:T(8,128)(2,1)S(1)}, u32[]{:S(2)}, u32[]{:S(2)}) collective-permute-start(bf16[9,96,16]{1,2,0:T(8,128)(2,1)S(1)} %constant_dynamic-update-slice_fusion.18), channel_id=1, source_target_pairs={{0,511},{1,2},{2,1},{3,4},{4,3},{5,6},{6,5},{7,8},{8,7},{9,10},{10... | collective-permute-start | bytes 82952 | tf_op jit(solution)/shard_map/ppermute | solution.py:60
  54.9 6.2 %collective-permute-start.4 = (bf16[9,96,16]{1,2,0:T(8,128)(2,1)S(1)}, bf16[9,96,16]{1,2,0:T(8,128)(2,1)S(1)}, u32[]{:S(2)}, u32[]{:S(2)}) collective-permute-start(bf16[9,96,16]{1,2,0:T(8,128)(2,1)S(1)} %constant_dynamic-update-slice_fusion.18), channel_id=1, source_target_pairs={{0,1},{1,0},{2,3},{3,2},{4,5},{5,4},{6,7},{7,6},{8,9},{9,8},{10,11... | collective-permute-start | bytes 82952 | tf_op jit(solution)/shard_map/ppermute | solution.py:59
  61.2 8.6 %collective-permute-start.7 = (bf16[9,96,16]{1,2,0:T(8,128)(2,1)S(1)}, bf16[9,96,16]{1,2,0:T(8,128)(2,1)S(1)}, u32[]{:S(2)}, u32[]{:S(2)}) collective-permute-start(bf16[9,96,16]{1,2,0:T(8,128)(2,1)S(1)} %constant_dynamic-update-slice_fusion.27), channel_id=1, source_target_pairs={{0,8},{1,9},{2,10},{3,11},{4,12},{5,13},{6,14},{7,15},{8,0},{9,1},... | collective-permute-start | bytes 82952 | tf_op jit(solution)/shard_map/ppermute | solution.py:59
  63.3 12.8 %collective-permute-start.6 = (bf16[9,96,16]{1,2,0:T(8,128)(2,1)S(1)}, bf16[9,96,16]{1,2,0:T(8,128)(2,1)S(1)}, u32[]{:S(2)}, u32[]{:S(2)}) collective-permute-start(bf16[9,96,16]{1,2,0:T(8,128)(2,1)S(1)} %constant_dynamic-update-slice_fusion.27), channel_id=1, source_target_pairs={{0,504},{1,505},{2,506},{3,507},{4,508},{5,509},{6,510},{7,511},{8... | collective-permute-start | bytes 82952 | tf_op jit(solution)/shard_map/ppermute | solution.py:60
  80.6 8.0 %collective-permute-start.8 = (f32[83456]{0:T(1024)S(1)}, f32[83456]{0:T(1024)S(1)}, u32[]{:S(2)}, u32[]{:S(2)}) collective-permute-start(f32[83456]{0:T(1024)S(1)} %broadcast_select_fusion), channel_id=1, source_target_pairs={{0,1},{1,0},{2,3},{3,2},{4,5},{5,4},{6,7},{7,6},{8,9},{9,8},{10,11... | collective-permute-start | bytes 1001480 | tf_op jit(solution)/shard_map/ppermute | solution.py:23
  88.7 7.4 %collective-permute-start.9 = (f32[41728]{0:T(1024)S(1)}, f32[41728]{0:T(1024)S(1)}, u32[]{:S(2)}, u32[]{:S(2)}) collective-permute-start(f32[41728]{0:T(1024)S(1)} %slice_select_fusion), channel_id=1, source_target_pairs={{0,2},{1,3},{2,0},{3,1},{4,6},{5,7},{6,4},{7,5},{8,10},{9,11},{10,... | collective-permute-start | bytes 500744 | tf_op jit(solution)/shard_map/ppermute | solution.py:23
  96.1 8.7 %collective-permute-start.10 = (f32[20864]{0:T(1024)S(1)}, f32[20864]{0:T(1024)S(1)}, u32[]{:S(2)}, u32[]{:S(2)}) collective-permute-start(f32[20864]{0:T(1024)S(1)} %slice_select_fusion.1), channel_id=1, source_target_pairs={{0,4},{1,5},{2,6},{3,7},{4,0},{5,1},{6,2},{7,3},{8,12},{9,13},{10,... | collective-permute-start | bytes 250376 | tf_op jit(solution)/shard_map/ppermute | solution.py:23
  104.8 11.0 %collective-permute-start.11 = (f32[20864]{0:T(1024)S(1)}, f32[20864]{0:T(1024)S(1)}, u32[]{:S(2)}, u32[]{:S(2)}) collective-permute-start(f32[20864]{0:T(1024)S(1)} %select_add_fusion.2), channel_id=1, source_target_pairs={{0,8},{1,9},{2,10},{3,11},{4,12},{5,13},{6,14},{7,15},{8,0},{9,1},... | collective-permute-start | bytes 250376 | tf_op jit(solution)/shard_map/ppermute | solution.py:23
  115.8 5.2 %collective-permute-start.12 = (f32[20864]{0:T(1024)S(1)}, f32[20864]{0:T(1024)S(1)}, u32[]{:S(2)}, u32[]{:S(2)}) collective-permute-start(f32[20864]{0:T(1024)S(1)} %add.500), channel_id=1, source_target_pairs={{0,16},{1,17},{2,18},{3,19},{4,20},{5,21},{6,22},{7,23},{8,24},{9,... | collective-permute-start | bytes 250376 | tf_op jit(solution)/shard_map/ppermute | solution.py:23
  121.1 6.7 %collective-permute-start.13 = (f32[20864]{0:T(1024)S(1)}, f32[20864]{0:T(1024)S(1)}, u32[]{:S(2)}, u32[]{:S(2)}) collective-permute-start(f32[20864]{0:T(1024)S(1)} %add.501), channel_id=1, source_target_pairs={{0,32},{1,33},{2,34},{3,35},{4,36},{5,37},{6,38},{7,39},{8,40},{9,... | collective-permute-start | bytes 250376 | tf_op jit(solution)/shard_map/ppermute | solution.py:23
  127.8 5.2 %collective-permute-start.14 = (f32[20864]{0:T(1024)S(1)}, f32[20864]{0:T(1024)S(1)}, u32[]{:S(2)}, u32[]{:S(2)}) collective-permute-start(f32[20864]{0:T(1024)S(1)} %add.502), channel_id=1, source_target_pairs={{0,64},{1,65},{2,66},{3,67},{4,68},{5,69},{6,70},{7,71},{8,72},{9,... | collective-permute-start | bytes 250376 | tf_op jit(solution)/shard_map/ppermute | solution.py:23
  133.1 6.8 %collective-permute-start.15 = (f32[20864]{0:T(1024)S(1)}, f32[20864]{0:T(1024)S(1)}, u32[]{:S(2)}, u32[]{:S(2)}) collective-permute-start(f32[20864]{0:T(1024)S(1)} %add.503), channel_id=1, source_target_pairs={{0,128},{1,129},{2,130},{3,131},{4,132},{5,133},{6,134},{7,135},{8... | collective-permute-start | bytes 250376 | tf_op jit(solution)/shard_map/ppermute | solution.py:23
  139.9 10.0 %collective-permute-start.16 = (f32[20864]{0:T(1024)S(1)}, f32[20864]{0:T(1024)S(1)}, u32[]{:S(2)}, u32[]{:S(2)}) collective-permute-start(f32[20864]{0:T(1024)S(1)} %add.504), channel_id=1, source_target_pairs={{0,256},{1,257},{2,258},{3,259},{4,260},{5,261},{6,262},{7,263},{8... | collective-permute-start | bytes 250376 | tf_op jit(solution)/shard_map/ppermute | solution.py:23
  149.9 6.1 %collective-permute-start.17 = (f32[20864]{0:T(1024)S(1)}, f32[20864]{0:T(1024)S(1)}, u32[]{:S(2)}, u32[]{:S(2)}) collective-permute-start(f32[20864]{0:T(1024)S(1)} %add.505), channel_id=1, source_target_pairs={{0,4},{1,5},{2,6},{3,7},{4,0},{5,1},{6,2},{7,3},{8,12},{9,13},{10,... | collective-permute-start | bytes 250376 | tf_op jit(solution)/shard_map/ppermute | solution.py:23
  156.0 6.9 %collective-permute-start.18 = (f32[41728]{0:T(1024)S(1)}, f32[41728]{0:T(1024)S(1)}, u32[]{:S(2)}, u32[]{:S(2)}) collective-permute-start(f32[41728]{0:T(1024)S(1)} %maximum_select_fusion.2), channel_id=1, source_target_pairs={{0,2},{1,3},{2,0},{3,1},{4,6},{5,7},{6,4},{7,5},{8,10},{9,11},{10,... | collective-permute-start | bytes 500744 | tf_op jit(solution)/shard_map/ppermute | solution.py:23
  163.0 11.3 %collective-permute-start.19 = (f32[83456]{0:T(1024)S(1)}, f32[83456]{0:T(1024)S(1)}, u32[]{:S(2)}, u32[]{:S(2)}) collective-permute-start(f32[83456]{0:T(1024)S(1)} %maximum_select_fusion.1), channel_id=1, source_target_pairs={{0,1},{1,0},{2,3},{3,2},{4,5},{5,4},{6,7},{7,6},{8,9},{9,8},{10,11... | collective-permute-start | bytes 1001480 | tf_op jit(solution)/shard_map/ppermute | solution.py:23

commit v7 on v6

--- a/solution.py
+++ b/solution.py
@@ -190,30 +190,41 @@
 def conv_cells(padded, weights):
     channels = padded.shape[0]
     cell_width = padded.shape[1] - 2
-    result = jnp.zeros((weights.shape[1], cell_width * cell_width), jnp.float32)
-    for tap_index in range(9):
-        row_off, col_off = divmod(tap_index, 3)
-        window = padded[:, row_off : row_off + cell_width, col_off : col_off + cell_width].reshape(
-            channels, cell_width * cell_width
-        )
-        result = result + jnp.dot(weights[tap_index], window, preferred_element_type=jnp.float32)
-    return result
+    windows = jnp.concatenate(
+        [
+            padded[:, r : r + cell_width, c : c + cell_width].reshape(
+                channels, cell_width * cell_width
+            )
+            for r, c in (divmod(t, 3) for t in range(9))
+        ],
+        axis=0,
+    )
+    taps, outs, ins = weights.shape
+    flat_weights = jnp.transpose(weights, (1, 0, 2)).reshape(outs, taps * ins)
+    return jnp.dot(flat_weights, windows, preferred_element_type=jnp.float32)
 
 
 def spread_back(grad_rows, weights, cell_width):
     grad_grid = grad_rows.reshape(grad_rows.shape[0], cell_width, cell_width)
     wide_grid = jnp.pad(grad_grid, ((0, 0), (2, 2), (2, 2)))
     ext_width = cell_width + 2
-    result = jnp.zeros((weights.shape[2], ext_width * ext_width), jnp.float32)
-    for tap_index in range(9):
-        row_off, col_off = divmod(tap_index, 3)
-        window = wide_grid[
-            :, 2 - row_off : 2 - row_off + ext_width, 2 - col_off : 2 - col_off + ext_width
-        ].reshape(grad_rows.shape[0], ext_width * ext_width)
-        result = result + lax.dot_general(
-            weights[tap_index], window, (((0,), (0,)), ((), ())), preferred_element_type=jnp.float32
-        )
-    return result.reshape(weights.shape[2], ext_width, ext_width)
+    windows = jnp.concatenate(
+        [
+            wide_grid[:, 2 - r : 2 - r + ext_width, 2 - c : 2 - c + ext_width].reshape(
+                grad_rows.shape[0], ext_width * ext_width
+            )
+            for r, c in (divmod(t, 3) for t in range(9))
+        ],
+        axis=0,
+    )
+    taps, outs, ins = weights.shape
+    result = lax.dot_general(
+        weights.reshape(taps * outs, ins),
+        windows,
+        (((0,), (0,)), ((), ())),
+        preferred_element_type=jnp.float32,
+    )
+    return result.reshape(ins, ext_width, ext_width)
 
 
 def weight_terms(padded, grad_rows, cell_width):

time: 178 us -> 176 us (0.989)
  matrix products: 10.5 us -> 4.91 us
  starting transfers between devices: 84.1 us -> 87.6 us
    ppermute x4, waiting for transfers between devices: 0.45 us -> 12 us  [paired_shift(): got_flip = lax.ppermute(block, 'tiles', flip)]
    ppermute x12, waiting for transfers between devices: 49.6 us -> 42.3 us  [xor_partner(): lax.ppermute(block, 'tiles', [(i, i ^ distance) for i in range(devices)])]
    ppermute x12, starting transfers between devices: 41 us -> 47.7 us  [xor_partner(): lax.ppermute(block, 'tiles', [(i, i ^ distance) for i in range(devices)])]
    ppermute x4, starting transfers between devices: 22.7 us -> 16.1 us  [paired_shift(): got_flip = lax.ppermute(block, 'tiles', flip)]
    dot_general x36 -> x4, matrix products: 7.67 us -> 2.13 us  [the longest x2 1.47 us: conv_cells(): return jnp.dot(flat_weights, windows, preferred_element_type=jnp.float32)]
    ppermute x4, waiting for transfers between devices: 11.6 us -> 6.16 us  [paired_shift(): got_other = lax.ppermute(block, 'tiles', other)]
    unnamed x45 -> x61, local copies, waits for them, and re-layouts: 8.66 us -> 4.06 us
    concatenate x0 -> x4, local copies, waits for them, and re-layouts: none -> 4.21 us  [the longest x2 4.19 us: spread_back(): jnp.concatenate([wide_grid[:, 2 - r:2 - r + ext_width, 2 - c:2 - c + ext_...]
  transfers between devices with their start and end apart: 20 -> 20, of which waited for: 15 -> 17; matrix products, arithmetic and copies ran while one was open for 3% -> 3% of each run, Pallas kernels for 0% -> 0%
where the time goes in v7:
time: 176 us; the launch traced here: 175 us
  starting transfers between devices  87.6 us (50%)
  waiting for transfers between devices  60.5 us (34%)
  local copies, waits for them, and re-layouts  17.5 us (10%)
  matrix products  4.91 us (3%)
  other arithmetic  2.62 us (1%)
  between operations  2.18 us (1%)
    ppermute x12, starting transfers between devices, xor_partner(): lax.ppermute(block, 'tiles', [(i, i ^ distance) for i in range(devices)])  47.7 us
    ppermute x12, waiting for transfers between devices, xor_partner(): lax.ppermute(block, 'tiles', [(i, i ^ distance) for i in range(devices)])  42.3 us
    ppermute x4, starting transfers between devices, paired_shift(): got_other = lax.ppermute(block, 'tiles', other)  23.8 us
    ppermute x4, starting transfers between devices, paired_shift(): got_flip = lax.ppermute(block, 'tiles', flip)  16.1 us
    ppermute x4, waiting for transfers between devices, paired_shift(): got_flip = lax.ppermute(block, 'tiles', flip)  12 us
    ppermute x4, waiting for transfers between devices, paired_shift(): got_other = lax.ppermute(block, 'tiles', other)  6.16 us
    concatenate x2, local copies, waits for them, and re-layouts, spread_back(): jnp.concatenate([wide_grid[:, 2 - r:2 - r + ext_width, 2 - c:2 - c + ext_...  4.19 us
    unnamed x61, local copies, waits for them, and re-layouts  4.06 us
  transfers between devices with their start and end apart: 20, of which 17 were waited for; matrix products, arithmetic and copies ran while one was open for 3% of the time, Pallas kernels for 0%

profile of v7, /device:TPU:1, one launch (start us, length us, event | category | flops | bytes accessed | tf_op | source)
XLA Modules:
  0.0 175.3 jit_solution(2241457025761016578)
XLA Ops:
  0.6 0.9 copy.202
  2.2 2.1 %concatenate.132 = bf16[864,324]{0,1:T(8,128)(2,1)S(1)} concatenate(bf16[96,324]{0,1:T(8,128)(2,1)S(1)} %reshape.435, bf16[96,324]{0,1:T(8,128)(2,1)S(1)} %reshape.436, bf16[96,324]{0,1:T(8,128)(2,1)S(1)} %reshape.437, bf16[96,324]{0,1:T(8,128)(2,1)S(1)} %reshape.438, bf16[96,324]{0,1:T(8,128)(2,1)S(1)} %reshape.439, bf16[96,324]{0,1:T(8,128)(2,1)S(1)} %reshape.440, ...), dimensions={0} | concatenate | bytes 1119744 | tf_op jit(solution)/shard_map/concatenate | solution.py:211
  5.8 8.7 %collective-permute-start = (bf16[9,96,16]{1,2,0:T(8,128)(2,1)S(1)}, bf16[9,96,16]{1,2,0:T(8,128)(2,1)S(1)}, u32[]{:S(2)}, u32[]{:S(2)}) collective-permute-start(bf16[9,96,16]{1,2,0:T(8,128)(2,1)S(1)} %constant_dynamic-update-slice_fusion), channel_id=1, source_target_pairs={{0,1},{1,0},{2,3},{3,2},{4,5},{5,4},{6,7},{7,6},{8,9},{9,8},{10,11... | collective-permute-start | bytes 82952 | tf_op jit(solution)/shard_map/ppermute | solution.py:59
  14.5 1.9 %collective-permute-start.1 = (bf16[9,96,16]{1,2,0:T(8,128)(2,1)S(1)}, bf16[9,96,16]{1,2,0:T(8,128)(2,1)S(1)}, u32[]{:S(2)}, u32[]{:S(2)}) collective-permute-start(bf16[9,96,16]{1,2,0:T(8,128)(2,1)S(1)} %constant_dynamic-update-slice_fusion), channel_id=1, source_target_pairs={{0,511},{1,2},{2,1},{3,4},{4,3},{5,6},{6,5},{7,8},{8,7},{9,10},{10... | collective-permute-start | bytes 82952 | tf_op jit(solution)/shard_map/ppermute | solution.py:60
  17.2 2.6 %collective-permute-done.1 = bf16[9,96,16]{1,2,0:T(8,128)(2,1)S(1)} collective-permute-done((bf16[9,96,16]{1,2,0:T(8,128)(2,1)S(1)}, bf16[9,96,16]{1,2,0:T(8,128)(2,1)S(1)}, u32[]{:S(2)}, u32[]{:S(2)}) %collective-permute-start.1) | collective-permute-done | bytes 27680 | tf_op jit(solution)/shard_map/ppermute | solution.py:60
  19.8 10.7 %collective-permute-start.2 = (bf16[9,96,16]{1,2,0:T(8,128)(2,1)S(1)}, bf16[9,96,16]{1,2,0:T(8,128)(2,1)S(1)}, u32[]{:S(2)}, u32[]{:S(2)}) collective-permute-start(bf16[9,96,16]{1,2,0:T(8,128)(2,1)S(1)} %constant_dynamic-update-slice_fusion.9), channel_id=1, source_target_pairs={{0,504},{1,505},{2,506},{3,507},{4,508},{5,509},{6,510},{7,511},{8... | collective-permute-start | bytes 82952 | tf_op jit(solution)/shard_map/ppermute | solution.py:60
  30.5 1.9 %collective-permute-start.3 = (bf16[9,96,16]{1,2,0:T(8,128)(2,1)S(1)}, bf16[9,96,16]{1,2,0:T(8,128)(2,1)S(1)}, u32[]{:S(2)}, u32[]{:S(2)}) collective-permute-start(bf16[9,96,16]{1,2,0:T(8,128)(2,1)S(1)} %constant_dynamic-update-slice_fusion.9), channel_id=1, source_target_pairs={{0,8},{1,9},{2,10},{3,11},{4,12},{5,13},{6,14},{7,15},{8,0},{9,1},... | collective-permute-start | bytes 82952 | tf_op jit(solution)/shard_map/ppermute | solution.py:59
  32.9 6.9 %collective-permute-done.3 = bf16[9,96,16]{1,2,0:T(8,128)(2,1)S(1)} collective-permute-done((bf16[9,96,16]{1,2,0:T(8,128)(2,1)S(1)}, bf16[9,96,16]{1,2,0:T(8,128)(2,1)S(1)}, u32[]{:S(2)}, u32[]{:S(2)}) %collective-permute-start.3) | collective-permute-done | bytes 27680 | tf_op jit(solution)/shard_map/ppermute | solution.py:59
  40.7 0.6 gather_fusion
  42.4 0.8 copy-done.3
  43.7 0.6 copy-done.9
  44.4 0.6 convert_reduce_fusion
  45.7 2.1 %concatenate.147 = bf16[864,324]{0,1:T(8,128)(2,1)S(1)} concatenate(bf16[96,324]{0,1:T(8,128)(2,1)S(1)} %reshape.458, bf16[96,324]{0,1:T(8,128)(2,1)S(1)} %reshape.459, bf16[96,324]{0,1:T(8,128)(2,1)S(1)} %reshape.460, bf16[96,324]{0,1:T(8,128)(2,1)S(1)} %reshape.461, bf16[96,324]{0,1:T(8,128)(2,1)S(1)} %reshape.462, bf16[96,324]{0,1:T(8,128)(2,1)S(1)} %reshape.463, ...), dimensions={0} | concatenate | bytes 1119744 | tf_op jit(solution)/shard_map/concatenate | solution.py:211
  48.6 3.5 %collective-permute-start.4 = (bf16[9,96,16]{1,2,0:T(8,128)(2,1)S(1)}, bf16[9,96,16]{1,2,0:T(8,128)(2,1)S(1)}, u32[]{:S(2)}, u32[]{:S(2)}) collective-permute-start(bf16[9,96,16]{1,2,0:T(8,128)(2,1)S(1)} %constant_dynamic-update-slice_fusion.27), channel_id=1, source_target_pairs={{0,1},{1,0},{2,3},{3,2},{4,5},{5,4},{6,7},{7,6},{8,9},{9,8},{10,11... | collective-permute-start | bytes 82952 | tf_op jit(solution)/shard_map/ppermute | solution.py:59
  52.1 1.9 %collective-permute-start.5 = (bf16[9,96,16]{1,2,0:T(8,128)(2,1)S(1)}, bf16[9,96,16]{1,2,0:T(8,128)(2,1)S(1)}, u32[]{:S(2)}, u32[]{:S(2)}) collective-permute-start(bf16[9,96,16]{1,2,0:T(8,128)(2,1)S(1)} %constant_dynamic-update-slice_fusion.27), channel_id=1, source_target_pairs={{0,511},{1,2},{2,1},{3,4},{4,3},{5,6},{6,5},{7,8},{8,7},{9,10},{10... | collective-permute-start | bytes 82952 | tf_op jit(solution)/shard_map/ppermute | solution.py:60
  55.2 2.2 %collective-permute-done.5 = bf16[9,96,16]{1,2,0:T(8,128)(2,1)S(1)} collective-permute-done((bf16[9,96,16]{1,2,0:T(8,128)(2,1)S(1)}, bf16[9,96,16]{1,2,0:T(8,128)(2,1)S(1)}, u32[]{:S(2)}, u32[]{:S(2)}) %collective-permute-start.5) | collective-permute-done | bytes 27680 | tf_op jit(solution)/shard_map/ppermute | solution.py:60
  57.5 9.3 %collective-permute-start.6 = (bf16[9,96,16]{1,2,0:T(8,128)(2,1)S(1)}, bf16[9,96,16]{1,2,0:T(8,128)(2,1)S(1)}, u32[]{:S(2)}, u32[]{:S(2)}) collective-permute-start(bf16[9,96,16]{1,2,0:T(8,128)(2,1)S(1)} %constant_dynamic-update-slice_fusion.36), channel_id=1, source_target_pairs={{0,504},{1,505},{2,506},{3,507},{4,508},{5,509},{6,510},{7,511},{8... | collective-permute-start | bytes 82952 | tf_op jit(solution)/shard_map/ppermute | solution.py:60
  66.7 1.9 %collective-permute-start.7 = (bf16[9,96,16]{1,2,0:T(8,128)(2,1)S(1)}, bf16[9,96,16]{1,2,0:T(8,128)(2,1)S(1)}, u32[]{:S(2)}, u32[]{:S(2)}) collective-permute-start(bf16[9,96,16]{1,2,0:T(8,128)(2,1)S(1)} %constant_dynamic-update-slice_fusion.36), channel_id=1, source_target_pairs={{0,8},{1,9},{2,10},{3,11},{4,12},{5,13},{6,14},{7,15},{8,0},{9,1},... | collective-permute-start | bytes 82952 | tf_op jit(solution)/shard_map/ppermute | solution.py:59
  69.1 1.4 collective-permute-done.6
  70.5 5.1 %collective-permute-done.7 = bf16[9,96,16]{1,2,0:T(8,128)(2,1)S(1)} collective-permute-done((bf16[9,96,16]{1,2,0:T(8,128)(2,1)S(1)}, bf16[9,96,16]{1,2,0:T(8,128)(2,1)S(1)}, u32[]{:S(2)}, u32[]{:S(2)}) %collective-permute-start.7) | collective-permute-done | bytes 27680 | tf_op jit(solution)/shard_map/ppermute | solution.py:59
  76.4 0.6 gather_fusion.2
  79.6 4.0 %collective-permute-start.8 = (f32[83456]{0:T(1024)S(1)}, f32[83456]{0:T(1024)S(1)}, u32[]{:S(2)}, u32[]{:S(2)}) collective-permute-start(f32[83456]{0:T(1024)S(1)} %broadcast_select_fusion), channel_id=1, source_target_pairs={{0,1},{1,0},{2,3},{3,2},{4,5},{5,4},{6,7},{7,6},{8,9},{9,8},{10,11... | collective-permute-start | bytes 1001480 | tf_op jit(solution)/shard_map/ppermute | solution.py:23
  83.6 1.2 collective-permute-done.8
  84.9 1.9 %collective-permute-start.9 = (f32[41728]{0:T(1024)S(1)}, f32[41728]{0:T(1024)S(1)}, u32[]{:S(2)}, u32[]{:S(2)}) collective-permute-start(f32[41728]{0:T(1024)S(1)} %slice_select_fusion), channel_id=1, source_target_pairs={{0,2},{1,3},{2,0},{3,1},{4,6},{5,7},{6,4},{7,5},{8,10},{9,11},{10,... | collective-permute-start | bytes 500744 | tf_op jit(solution)/shard_map/ppermute | solution.py:23
  86.9 5.4 %collective-permute-done.9 = f32[41728]{0:T(1024)S(1)} collective-permute-done((f32[41728]{0:T(1024)S(1)}, f32[41728]{0:T(1024)S(1)}, u32[]{:S(2)}, u32[]{:S(2)}) %collective-permute-start.9) | collective-permute-done | bytes 166944 | tf_op jit(solution)/shard_map/ppermute | solution.py:23
  92.3 5.5 %collective-permute-start.10 = (f32[20864]{0:T(1024)S(1)}, f32[20864]{0:T(1024)S(1)}, u32[]{:S(2)}, u32[]{:S(2)}) collective-permute-start(f32[20864]{0:T(1024)S(1)} %slice_select_fusion.1), channel_id=1, source_target_pairs={{0,4},{1,5},{2,6},{3,7},{4,0},{5,1},{6,2},{7,3},{8,12},{9,13},{10,... | collective-permute-start | bytes 250376 | tf_op jit(solution)/shard_map/ppermute | solution.py:23
  97.8 2.1 %collective-permute-done.10 = f32[20864]{0:T(1024)S(1)} collective-permute-done((f32[20864]{0:T(1024)S(1)}, f32[20864]{0:T(1024)S(1)}, u32[]{:S(2)}, u32[]{:S(2)}) %collective-permute-start.10) | collective-permute-done | bytes 83488 | tf_op jit(solution)/shard_map/ppermute | solution.py:23
  100.0 1.9 %collective-permute-start.11 = (f32[20864]{0:T(1024)S(1)}, f32[20864]{0:T(1024)S(1)}, u32[]{:S(2)}, u32[]{:S(2)}) collective-permute-start(f32[20864]{0:T(1024)S(1)} %select_add_fusion.2), channel_id=1, source_target_pairs={{0,8},{1,9},{2,10},{3,11},{4,12},{5,13},{6,14},{7,15},{8,0},{9,1},... | collective-permute-start | bytes 250376 | tf_op jit(solution)/shard_map/ppermute | solution.py:23
  102.0 8.0 %collective-permute-done.11 = f32[20864]{0:T(1024)S(1)} collective-permute-done((f32[20864]{0:T(1024)S(1)}, f32[20864]{0:T(1024)S(1)}, u32[]{:S(2)}, u32[]{:S(2)}) %collective-permute-start.11) | collective-permute-done | bytes 83488 | tf_op jit(solution)/shard_map/ppermute | solution.py:23
  110.1 1.9 %collective-permute-start.12 = (f32[20864]{0:T(1024)S(1)}, f32[20864]{0:T(1024)S(1)}, u32[]{:S(2)}, u32[]{:S(2)}) collective-permute-start(f32[20864]{0:T(1024)S(1)} %add.346), channel_id=1, source_target_pairs={{0,16},{1,17},{2,18},{3,19},{4,20},{5,21},{6,22},{7,23},{8,24},{9,... | collective-permute-start | bytes 250376 | tf_op jit(solution)/shard_map/ppermute | solution.py:23
  112.6 2.7 %collective-permute-done.12 = f32[20864]{0:T(1024)S(1)} collective-permute-done((f32[20864]{0:T(1024)S(1)}, f32[20864]{0:T(1024)S(1)}, u32[]{:S(2)}, u32[]{:S(2)}) %collective-permute-start.12) | collective-permute-done | bytes 83488 | tf_op jit(solution)/shard_map/ppermute | solution.py:23
  115.3 1.9 %collective-permute-start.13 = (f32[20864]{0:T(1024)S(1)}, f32[20864]{0:T(1024)S(1)}, u32[]{:S(2)}, u32[]{:S(2)}) collective-permute-start(f32[20864]{0:T(1024)S(1)} %add.347), channel_id=1, source_target_pairs={{0,32},{1,33},{2,34},{3,35},{4,36},{5,37},{6,38},{7,39},{8,40},{9,... | collective-permute-start | bytes 250376 | tf_op jit(solution)/shard_map/ppermute | solution.py:23
  117.3 4.8 %collective-permute-done.13 = f32[20864]{0:T(1024)S(1)} collective-permute-done((f32[20864]{0:T(1024)S(1)}, f32[20864]{0:T(1024)S(1)}, u32[]{:S(2)}, u32[]{:S(2)}) %collective-permute-start.13) | collective-permute-done | bytes 83488 | tf_op jit(solution)/shard_map/ppermute | solution.py:23
  122.1 1.9 %collective-permute-start.14 = (f32[20864]{0:T(1024)S(1)}, f32[20864]{0:T(1024)S(1)}, u32[]{:S(2)}, u32[]{:S(2)}) collective-permute-start(f32[20864]{0:T(1024)S(1)} %add.348), channel_id=1, source_target_pairs={{0,64},{1,65},{2,66},{3,67},{4,68},{5,69},{6,70},{7,71},{8,72},{9,... | collective-permute-start | bytes 250376 | tf_op jit(solution)/shard_map/ppermute | solution.py:23
  124.0 3.6 %collective-permute-done.14 = f32[20864]{0:T(1024)S(1)} collective-permute-done((f32[20864]{0:T(1024)S(1)}, f32[20864]{0:T(1024)S(1)}, u32[]{:S(2)}, u32[]{:S(2)}) %collective-permute-start.14) | collective-permute-done | bytes 83488 | tf_op jit(solution)/shard_map/ppermute | solution.py:23
  127.6 1.9 %collective-permute-start.15 = (f32[20864]{0:T(1024)S(1)}, f32[20864]{0:T(1024)S(1)}, u32[]{:S(2)}, u32[]{:S(2)}) collective-permute-start(f32[20864]{0:T(1024)S(1)} %add.349), channel_id=1, source_target_pairs={{0,128},{1,129},{2,130},{3,131},{4,132},{5,133},{6,134},{7,135},{8... | collective-permute-start | bytes 250376 | tf_op jit(solution)/shard_map/ppermute | solution.py:23
  129.6 4.6 %collective-permute-done.15 = f32[20864]{0:T(1024)S(1)} collective-permute-done((f32[20864]{0:T(1024)S(1)}, f32[20864]{0:T(1024)S(1)}, u32[]{:S(2)}, u32[]{:S(2)}) %collective-permute-start.15) | collective-permute-done | bytes 83488 | tf_op jit(solution)/shard_map/ppermute | solution.py:23
  134.2 4.7 %collective-permute-start.16 = (f32[20864]{0:T(1024)S(1)}, f32[20864]{0:T(1024)S(1)}, u32[]{:S(2)}, u32[]{:S(2)}) collective-permute-start(f32[20864]{0:T(1024)S(1)} %add.350), channel_id=1, source_target_pairs={{0,256},{1,257},{2,258},{3,259},{4,260},{5,261},{6,262},{7,263},{8... | collective-permute-start | bytes 250376 | tf_op jit(solution)/shard_map/ppermute | solution.py:23
  138.9 5.3 %collective-permute-done.16 = f32[20864]{0:T(1024)S(1)} collective-permute-done((f32[20864]{0:T(1024)S(1)}, f32[20864]{0:T(1024)S(1)}, u32[]{:S(2)}, u32[]{:S(2)}) %collective-permute-start.16) | collective-permute-done | bytes 83488 | tf_op jit(solution)/shard_map/ppermute | solution.py:23
  144.3 3.6 %collective-permute-start.17 = (f32[20864]{0:T(1024)S(1)}, f32[20864]{0:T(1024)S(1)}, u32[]{:S(2)}, u32[]{:S(2)}) collective-permute-start(f32[20864]{0:T(1024)S(1)} %add.351), channel_id=1, source_target_pairs={{0,4},{1,5},{2,6},{3,7},{4,0},{5,1},{6,2},{7,3},{8,12},{9,13},{10,... | collective-permute-start | bytes 250376 | tf_op jit(solution)/shard_map/ppermute | solution.py:23
  147.9 2.5 %collective-permute-done.17 = f32[20864]{0:T(1024)S(1)} collective-permute-done((f32[20864]{0:T(1024)S(1)}, f32[20864]{0:T(1024)S(1)}, u32[]{:S(2)}, u32[]{:S(2)}) %collective-permute-start.17) | collective-permute-done | bytes 83488 | tf_op jit(solution)/shard_map/ppermute | solution.py:23
  150.4 4.6 %collective-permute-start.18 = (f32[41728]{0:T(1024)S(1)}, f32[41728]{0:T(1024)S(1)}, u32[]{:S(2)}, u32[]{:S(2)}) collective-permute-start(f32[41728]{0:T(1024)S(1)} %maximum_select_fusion.2), channel_id=1, source_target_pairs={{0,2},{1,3},{2,0},{3,1},{4,6},{5,7},{6,4},{7,5},{8,10},{9,11},{10,... | collective-permute-start | bytes 500744 | tf_op jit(solution)/shard_map/ppermute | solution.py:23
  155.3 0.7 copy.249
  156.0 1.7 collective-permute-done.18
  157.8 13.8 %collective-permute-start.19 = (f32[83456]{0:T(1024)S(1)}, f32[83456]{0:T(1024)S(1)}, u32[]{:S(2)}, u32[]{:S(2)}) collective-permute-start(f32[83456]{0:T(1024)S(1)} %maximum_select_fusion.1), channel_id=1, source_target_pairs={{0,1},{1,0},{2,3},{3,2},{4,5},{5,4},{6,7},{7,6},{8,9},{9,8},{10,11... | collective-permute-start | bytes 1001480 | tf_op jit(solution)/shard_map/ppermute | solution.py:23
  171.6 0.9 fusion.4
  173.5 0.9 mul.191
  174.4 0.9 mul.193
  (253 shorter events, 13.7 us)
Async XLA Ops:
  0.6 1.0 copy-start
  2.2 2.1 %copy-start.1 = (bf16[9,96,96]{2,1,0:T(8,128)(2,1)S(1)}, bf16[9,96,96]{2,1,0:T(8,128)(2,1)}, u32[]{:S(2)}) copy-start(bf16[9,96,96]{2,1,0:T(8,128)(2,1)} %param.17) | copy-start | bytes 497668
  4.9 11.6 %copy-start.7 = (s32[1,4]{1,0:T(1,128)S(1)}, s32[1,4]{1,0:T(1,128)}, u32[]{:S(2)}) copy-start(s32[1,4]{1,0:T(1,128)} %param.20) | copy-start | bytes 52
  4.9 11.6 %copy-start.4 = (s32[1,4]{1,0:T(1,128)S(1)}, s32[1,4]{1,0:T(1,128)}, u32[]{:S(2)}) copy-start(s32[1,4]{1,0:T(1,128)} %param.19) | copy-start | bytes 52
  4.9 11.6 %copy-start.5 = (s32[1,4]{1,0:T(1,128)S(1)}, s32[1,4]{1,0:T(1,128)}, u32[]{:S(2)}) copy-start(s32[1,4]{1,0:T(1,128)} %param.21) | copy-start | bytes 52
  4.9 11.6 %copy-start.11 = (s32[4]{0:T(128)S(1)}, s32[4]{0:T(128)}, u32[]{:S(2)}) copy-start(s32[4]{0:T(128)} %constant.138.clone) | copy-start | bytes 52
  4.9 11.8 %copy-start.10 = (s32[4]{0:T(128)S(1)}, s32[4]{0:T(128)}, u32[]{:S(2)}) copy-start(s32[4]{0:T(128)} %constant.139.clone) | copy-start | bytes 52
  5.0 12.0 %copy-start.8 = (s32[1,4]{1,0:T(1,128)S(1)}, s32[1,4]{1,0:T(1,128)}, u32[]{:S(2)}) copy-start(s32[1,4]{1,0:T(1,128)} %param.22) | copy-start | bytes 52
  5.0 0.7 copy-start.6
  5.1 27.5 %copy-start.2 = (bf16[9,96,96]{2,1,0:T(8,128)(2,1)S(1)}, bf16[9,96,96]{2,1,0:T(8,128)(2,1)}, u32[]{:S(2)}) copy-start(bf16[9,96,96]{2,1,0:T(8,128)(2,1)} %param.15) | copy-start | bytes 497668
  5.8 11.4 %collective-permute-start = (bf16[9,96,16]{1,2,0:T(8,128)(2,1)S(1)}, bf16[9,96,16]{1,2,0:T(8,128)(2,1)S(1)}, u32[]{:S(2)}, u32[]{:S(2)}) collective-permute-start(bf16[9,96,16]{1,2,0:T(8,128)(2,1)S(1)} %constant_dynamic-update-slice_fusion), channel_id=1, source_target_pairs={{0,1},{1,0},{2,3},{3,2},{4,5},{5,4},{6,7},{7,6},{8,9},{9,8},{10,11... | collective-permute-start | bytes 82952 | tf_op jit(solution)/shard_map/ppermute | solution.py:59
  14.5 5.3 %collective-permute-start.1 = (bf16[9,96,16]{1,2,0:T(8,128)(2,1)S(1)}, bf16[9,96,16]{1,2,0:T(8,128)(2,1)S(1)}, u32[]{:S(2)}, u32[]{:S(2)}) collective-permute-start(bf16[9,96,16]{1,2,0:T(8,128)(2,1)S(1)} %constant_dynamic-update-slice_fusion), channel_id=1, source_target_pairs={{0,511},{1,2},{2,1},{3,4},{4,3},{5,6},{6,5},{7,8},{8,7},{9,10},{10... | collective-permute-start | bytes 82952 | tf_op jit(solution)/shard_map/ppermute | solution.py:60
  19.8 13.1 %collective-permute-start.2 = (bf16[9,96,16]{1,2,0:T(8,128)(2,1)S(1)}, bf16[9,96,16]{1,2,0:T(8,128)(2,1)S(1)}, u32[]{:S(2)}, u32[]{:S(2)}) collective-permute-start(bf16[9,96,16]{1,2,0:T(8,128)(2,1)S(1)} %constant_dynamic-update-slice_fusion.9), channel_id=1, source_target_pairs={{0,504},{1,505},{2,506},{3,507},{4,508},{5,509},{6,510},{7,511},{8... | collective-permute-start | bytes 82952 | tf_op jit(solution)/shard_map/ppermute | solution.py:60
  30.5 9.3 %collective-permute-start.3 = (bf16[9,96,16]{1,2,0:T(8,128)(2,1)S(1)}, bf16[9,96,16]{1,2,0:T(8,128)(2,1)S(1)}, u32[]{:S(2)}, u32[]{:S(2)}) collective-permute-start(bf16[9,96,16]{1,2,0:T(8,128)(2,1)S(1)} %constant_dynamic-update-slice_fusion.9), channel_id=1, source_target_pairs={{0,8},{1,9},{2,10},{3,11},{4,12},{5,13},{6,14},{7,15},{8,0},{9,1},... | collective-permute-start | bytes 82952 | tf_op jit(solution)/shard_map/ppermute | solution.py:59
  42.4 0.8 copy-start.3
  43.7 0.7 copy-start.9
  48.6 6.6 %collective-permute-start.4 = (bf16[9,96,16]{1,2,0:T(8,128)(2,1)S(1)}, bf16[9,96,16]{1,2,0:T(8,128)(2,1)S(1)}, u32[]{:S(2)}, u32[]{:S(2)}) collective-permute-start(bf16[9,96,16]{1,2,0:T(8,128)(2,1)S(1)} %constant_dynamic-update-slice_fusion.27), channel_id=1, source_target_pairs={{0,1},{1,0},{2,3},{3,2},{4,5},{5,4},{6,7},{7,6},{8,9},{9,8},{10,11... | collective-permute-start | bytes 82952 | tf_op jit(solution)/shard_map/ppermute | solution.py:59
  52.1 5.3 %collective-permute-start.5 = (bf16[9,96,16]{1,2,0:T(8,128)(2,1)S(1)}, bf16[9,96,16]{1,2,0:T(8,128)(2,1)S(1)}, u32[]{:S(2)}, u32[]{:S(2)}) collective-permute-start(bf16[9,96,16]{1,2,0:T(8,128)(2,1)S(1)} %constant_dynamic-update-slice_fusion.27), channel_id=1, source_target_pairs={{0,511},{1,2},{2,1},{3,4},{4,3},{5,6},{6,5},{7,8},{8,7},{9,10},{10... | collective-permute-start | bytes 82952 | tf_op jit(solution)/shard_map/ppermute | solution.py:60
  57.5 13.1 %collective-permute-start.6 = (bf16[9,96,16]{1,2,0:T(8,128)(2,1)S(1)}, bf16[9,96,16]{1,2,0:T(8,128)(2,1)S(1)}, u32[]{:S(2)}, u32[]{:S(2)}) collective-permute-start(bf16[9,96,16]{1,2,0:T(8,128)(2,1)S(1)} %constant_dynamic-update-slice_fusion.36), channel_id=1, source_target_pairs={{0,504},{1,505},{2,506},{3,507},{4,508},{5,509},{6,510},{7,511},{8... | collective-permute-start | bytes 82952 | tf_op jit(solution)/shard_map/ppermute | solution.py:60
  66.7 8.9 %collective-permute-start.7 = (bf16[9,96,16]{1,2,0:T(8,128)(2,1)S(1)}, bf16[9,96,16]{1,2,0:T(8,128)(2,1)S(1)}, u32[]{:S(2)}, u32[]{:S(2)}) collective-permute-start(bf16[9,96,16]{1,2,0:T(8,128)(2,1)S(1)} %constant_dynamic-update-slice_fusion.36), channel_id=1, source_target_pairs={{0,8},{1,9},{2,10},{3,11},{4,12},{5,13},{6,14},{7,15},{8,0},{9,1},... | collective-permute-start | bytes 82952 | tf_op jit(solution)/shard_map/ppermute | solution.py:59
  79.6 5.2 %collective-permute-start.8 = (f32[83456]{0:T(1024)S(1)}, f32[83456]{0:T(1024)S(1)}, u32[]{:S(2)}, u32[]{:S(2)}) collective-permute-start(f32[83456]{0:T(1024)S(1)} %broadcast_select_fusion), channel_id=1, source_target_pairs={{0,1},{1,0},{2,3},{3,2},{4,5},{5,4},{6,7},{7,6},{8,9},{9,8},{10,11... | collective-permute-start | bytes 1001480 | tf_op jit(solution)/shard_map/ppermute | solution.py:23
  84.9 7.4 %collective-permute-start.9 = (f32[41728]{0:T(1024)S(1)}, f32[41728]{0:T(1024)S(1)}, u32[]{:S(2)}, u32[]{:S(2)}) collective-permute-start(f32[41728]{0:T(1024)S(1)} %slice_select_fusion), channel_id=1, source_target_pairs={{0,2},{1,3},{2,0},{3,1},{4,6},{5,7},{6,4},{7,5},{8,10},{9,11},{10,... | collective-permute-start | bytes 500744 | tf_op jit(solution)/shard_map/ppermute | solution.py:23
  92.3 7.7 %collective-permute-start.10 = (f32[20864]{0:T(1024)S(1)}, f32[20864]{0:T(1024)S(1)}, u32[]{:S(2)}, u32[]{:S(2)}) collective-permute-start(f32[20864]{0:T(1024)S(1)} %slice_select_fusion.1), channel_id=1, source_target_pairs={{0,4},{1,5},{2,6},{3,7},{4,0},{5,1},{6,2},{7,3},{8,12},{9,13},{10,... | collective-permute-start | bytes 250376 | tf_op jit(solution)/shard_map/ppermute | solution.py:23
  100.0 10.1 %collective-permute-start.11 = (f32[20864]{0:T(1024)S(1)}, f32[20864]{0:T(1024)S(1)}, u32[]{:S(2)}, u32[]{:S(2)}) collective-permute-start(f32[20864]{0:T(1024)S(1)} %select_add_fusion.2), channel_id=1, source_target_pairs={{0,8},{1,9},{2,10},{3,11},{4,12},{5,13},{6,14},{7,15},{8,0},{9,1},... | collective-permute-start | bytes 250376 | tf_op jit(solution)/shard_map/ppermute | solution.py:23
  110.1 5.2 %collective-permute-start.12 = (f32[20864]{0:T(1024)S(1)}, f32[20864]{0:T(1024)S(1)}, u32[]{:S(2)}, u32[]{:S(2)}) collective-permute-start(f32[20864]{0:T(1024)S(1)} %add.346), channel_id=1, source_target_pairs={{0,16},{1,17},{2,18},{3,19},{4,20},{5,21},{6,22},{7,23},{8,24},{9,... | collective-permute-start | bytes 250376 | tf_op jit(solution)/shard_map/ppermute | solution.py:23
  115.3 6.7 %collective-permute-start.13 = (f32[20864]{0:T(1024)S(1)}, f32[20864]{0:T(1024)S(1)}, u32[]{:S(2)}, u32[]{:S(2)}) collective-permute-start(f32[20864]{0:T(1024)S(1)} %add.347), channel_id=1, source_target_pairs={{0,32},{1,33},{2,34},{3,35},{4,36},{5,37},{6,38},{7,39},{8,40},{9,... | collective-permute-start | bytes 250376 | tf_op jit(solution)/shard_map/ppermute | solution.py:23
  122.1 5.5 %collective-permute-start.14 = (f32[20864]{0:T(1024)S(1)}, f32[20864]{0:T(1024)S(1)}, u32[]{:S(2)}, u32[]{:S(2)}) collective-permute-start(f32[20864]{0:T(1024)S(1)} %add.348), channel_id=1, source_target_pairs={{0,64},{1,65},{2,66},{3,67},{4,68},{5,69},{6,70},{7,71},{8,72},{9,... | collective-permute-start | bytes 250376 | tf_op jit(solution)/shard_map/ppermute | solution.py:23
  127.6 6.6 %collective-permute-start.15 = (f32[20864]{0:T(1024)S(1)}, f32[20864]{0:T(1024)S(1)}, u32[]{:S(2)}, u32[]{:S(2)}) collective-permute-start(f32[20864]{0:T(1024)S(1)} %add.349), channel_id=1, source_target_pairs={{0,128},{1,129},{2,130},{3,131},{4,132},{5,133},{6,134},{7,135},{8... | collective-permute-start | bytes 250376 | tf_op jit(solution)/shard_map/ppermute | solution.py:23
  134.2 10.1 %collective-permute-start.16 = (f32[20864]{0:T(1024)S(1)}, f32[20864]{0:T(1024)S(1)}, u32[]{:S(2)}, u32[]{:S(2)}) collective-permute-start(f32[20864]{0:T(1024)S(1)} %add.350), channel_id=1, source_target_pairs={{0,256},{1,257},{2,258},{3,259},{4,260},{5,261},{6,262},{7,263},{8... | collective-permute-start | bytes 250376 | tf_op jit(solution)/shard_map/ppermute | solution.py:23
  144.3 6.1 %collective-permute-start.17 = (f32[20864]{0:T(1024)S(1)}, f32[20864]{0:T(1024)S(1)}, u32[]{:S(2)}, u32[]{:S(2)}) collective-permute-start(f32[20864]{0:T(1024)S(1)} %add.351), channel_id=1, source_target_pairs={{0,4},{1,5},{2,6},{3,7},{4,0},{5,1},{6,2},{7,3},{8,12},{9,13},{10,... | collective-permute-start | bytes 250376 | tf_op jit(solution)/shard_map/ppermute | solution.py:23
  150.4 7.3 %collective-permute-start.18 = (f32[41728]{0:T(1024)S(1)}, f32[41728]{0:T(1024)S(1)}, u32[]{:S(2)}, u32[]{:S(2)}) collective-permute-start(f32[41728]{0:T(1024)S(1)} %maximum_select_fusion.2), channel_id=1, source_target_pairs={{0,2},{1,3},{2,0},{3,1},{4,6},{5,7},{6,4},{7,5},{8,10},{9,11},{10,... | collective-permute-start | bytes 500744 | tf_op jit(solution)/shard_map/ppermute | solution.py:23
  157.8 15.0 %collective-permute-start.19 = (f32[83456]{0:T(1024)S(1)}, f32[83456]{0:T(1024)S(1)}, u32[]{:S(2)}, u32[]{:S(2)}) collective-permute-start(f32[83456]{0:T(1024)S(1)} %maximum_select_fusion.1), channel_id=1, source_target_pairs={{0,1},{1,0},{2,3},{3,2},{4,5},{5,4},{6,7},{7,6},{8,9},{9,8},{10,11... | collective-permute-start | bytes 1001480 | tf_op jit(solution)/shard_map/ppermute | solution.py:23

commit v8 on v7

--- a/solution.py
+++ b/solution.py
@@ -229,18 +229,19 @@
 
 def weight_terms(padded, grad_rows, cell_width):
     channels = padded.shape[0]
-    term_list = []
-    for tap_index in range(9):
-        row_off, col_off = divmod(tap_index, 3)
-        window = padded[:, row_off : row_off + cell_width, col_off : col_off + cell_width].reshape(
-            channels, cell_width * cell_width
-        )
-        term_list.append(
-            lax.dot_general(
-                grad_rows, window, (((1,), (1,)), ((), ())), preferred_element_type=jnp.float32
+    windows = jnp.concatenate(
+        [
+            padded[:, r : r + cell_width, c : c + cell_width].reshape(
+                channels, cell_width * cell_width
             )
-        )
-    return jnp.stack(term_list, axis=0)
+            for r, c in (divmod(t, 3) for t in range(9))
+        ],
+        axis=0,
+    )
+    terms = lax.dot_general(
+        grad_rows, windows, (((1,), (1,)), ((), ())), preferred_element_type=jnp.float32
+    )
+    return jnp.transpose(terms.reshape(grad_rows.shape[0], 9, channels), (1, 0, 2))
 
 
 def body(

time: 176 us -> 176 us (level)
  matrix products: 4.91 us -> 2.66 us
  waiting for transfers between devices: 60.5 us -> 62.7 us
    dot_general x18 -> x2, matrix products: 2.79 us -> 0.54 us  [weight_terms(): lax.dot_general(grad_rows, windows, (((1,), (1,)), ((), ())), preferred_e...]
  transfers between devices with their start and end apart: 20 -> 20, of which waited for: 17 -> 16; matrix products, arithmetic and copies ran while one was open for 3% -> 2% of each run, Pallas kernels for 0% -> 0%
where the time goes in v8:
time: 176 us
  starting transfers between devices  87.6 us (50%)
  waiting for transfers between devices  62.7 us (36%)
  local copies, waits for them, and re-layouts  17.9 us (10%)
  matrix products  2.66 us (2%)
  other arithmetic  2.61 us (1%)
  between operations  2.07 us (1%)
    ppermute x12, starting transfers between devices, xor_partner(): lax.ppermute(block, 'tiles', [(i, i ^ distance) for i in range(devices)])  47.7 us
    ppermute x12, waiting for transfers between devices, xor_partner(): lax.ppermute(block, 'tiles', [(i, i ^ distance) for i in range(devices)])  43.4 us
    ppermute x4, starting transfers between devices, paired_shift(): got_other = lax.ppermute(block, 'tiles', other)  23.8 us
    ppermute x4, starting transfers between devices, paired_shift(): got_flip = lax.ppermute(block, 'tiles', flip)  16.1 us
    ppermute x4, waiting for transfers between devices, paired_shift(): got_flip = lax.ppermute(block, 'tiles', flip)  12.2 us
    ppermute x4, waiting for transfers between devices, paired_shift(): got_other = lax.ppermute(block, 'tiles', other)  7 us
    concatenate x2, local copies, waits for them, and re-layouts, spread_back(): jnp.concatenate([wide_grid[:, 2 - r:2 - r + ext_width, 2 - c:2 - c + ext_...  4.19 us
    unnamed x61, local copies, waits for them, and re-layouts  4.07 us
  transfers between devices with their start and end apart: 20, of which 16 were waited for; matrix products, arithmetic and copies ran while one was open for 2% of the time, Pallas kernels for 0%

profile of v8, /device:TPU:1, one launch (start us, length us, event | category | flops | bytes accessed | tf_op | source)
XLA Modules:
  0.0 175.5 jit_solution(11100258340371742745)
XLA Ops:
  0.6 0.9 copy.211
  2.2 2.1 %concatenate.134 = bf16[864,324]{0,1:T(8,128)(2,1)S(1)} concatenate(bf16[96,324]{0,1:T(8,128)(2,1)S(1)} %reshape.441, bf16[96,324]{0,1:T(8,128)(2,1)S(1)} %reshape.442, bf16[96,324]{0,1:T(8,128)(2,1)S(1)} %reshape.443, bf16[96,324]{0,1:T(8,128)(2,1)S(1)} %reshape.444, bf16[96,324]{0,1:T(8,128)(2,1)S(1)} %reshape.445, bf16[96,324]{0,1:T(8,128)(2,1)S(1)} %reshape.446, ...), dimensions={0} | concatenate | bytes 1119744 | tf_op jit(solution)/shard_map/concatenate | solution.py:211
  5.8 8.7 %collective-permute-start = (bf16[9,96,16]{1,2,0:T(8,128)(2,1)S(1)}, bf16[9,96,16]{1,2,0:T(8,128)(2,1)S(1)}, u32[]{:S(2)}, u32[]{:S(2)}) collective-permute-start(bf16[9,96,16]{1,2,0:T(8,128)(2,1)S(1)} %constant_dynamic-update-slice_fusion), channel_id=1, source_target_pairs={{0,1},{1,0},{2,3},{3,2},{4,5},{5,4},{6,7},{7,6},{8,9},{9,8},{10,11... | collective-permute-start | bytes 82952 | tf_op jit(solution)/shard_map/ppermute | solution.py:59
  14.5 1.9 %collective-permute-start.1 = (bf16[9,96,16]{1,2,0:T(8,128)(2,1)S(1)}, bf16[9,96,16]{1,2,0:T(8,128)(2,1)S(1)}, u32[]{:S(2)}, u32[]{:S(2)}) collective-permute-start(bf16[9,96,16]{1,2,0:T(8,128)(2,1)S(1)} %constant_dynamic-update-slice_fusion), channel_id=1, source_target_pairs={{0,511},{1,2},{2,1},{3,4},{4,3},{5,6},{6,5},{7,8},{8,7},{9,10},{10... | collective-permute-start | bytes 82952 | tf_op jit(solution)/shard_map/ppermute | solution.py:60
  17.2 2.6 %collective-permute-done.1 = bf16[9,96,16]{1,2,0:T(8,128)(2,1)S(1)} collective-permute-done((bf16[9,96,16]{1,2,0:T(8,128)(2,1)S(1)}, bf16[9,96,16]{1,2,0:T(8,128)(2,1)S(1)}, u32[]{:S(2)}, u32[]{:S(2)}) %collective-permute-start.1) | collective-permute-done | bytes 27680 | tf_op jit(solution)/shard_map/ppermute | solution.py:60
  19.8 10.7 %collective-permute-start.2 = (bf16[9,96,16]{1,2,0:T(8,128)(2,1)S(1)}, bf16[9,96,16]{1,2,0:T(8,128)(2,1)S(1)}, u32[]{:S(2)}, u32[]{:S(2)}) collective-permute-start(bf16[9,96,16]{1,2,0:T(8,128)(2,1)S(1)} %constant_dynamic-update-slice_fusion.9), channel_id=1, source_target_pairs={{0,504},{1,505},{2,506},{3,507},{4,508},{5,509},{6,510},{7,511},{8... | collective-permute-start | bytes 82952 | tf_op jit(solution)/shard_map/ppermute | solution.py:60
  30.5 1.9 %collective-permute-start.3 = (bf16[9,96,16]{1,2,0:T(8,128)(2,1)S(1)}, bf16[9,96,16]{1,2,0:T(8,128)(2,1)S(1)}, u32[]{:S(2)}, u32[]{:S(2)}) collective-permute-start(bf16[9,96,16]{1,2,0:T(8,128)(2,1)S(1)} %constant_dynamic-update-slice_fusion.9), channel_id=1, source_target_pairs={{0,8},{1,9},{2,10},{3,11},{4,12},{5,13},{6,14},{7,15},{8,0},{9,1},... | collective-permute-start | bytes 82952 | tf_op jit(solution)/shard_map/ppermute | solution.py:59
  32.7 7.1 %collective-permute-done.3 = bf16[9,96,16]{1,2,0:T(8,128)(2,1)S(1)} collective-permute-done((bf16[9,96,16]{1,2,0:T(8,128)(2,1)S(1)}, bf16[9,96,16]{1,2,0:T(8,128)(2,1)S(1)}, u32[]{:S(2)}, u32[]{:S(2)}) %collective-permute-start.3) | collective-permute-done | bytes 27680 | tf_op jit(solution)/shard_map/ppermute | solution.py:59
  40.7 0.6 gather_fusion
  42.4 0.8 copy-done.2
  43.7 0.6 copy-done.9
  44.4 0.6 convert_reduce_fusion
  45.7 2.1 %concatenate.149 = bf16[864,324]{0,1:T(8,128)(2,1)S(1)} concatenate(bf16[96,324]{0,1:T(8,128)(2,1)S(1)} %reshape.464, bf16[96,324]{0,1:T(8,128)(2,1)S(1)} %reshape.465, bf16[96,324]{0,1:T(8,128)(2,1)S(1)} %reshape.466, bf16[96,324]{0,1:T(8,128)(2,1)S(1)} %reshape.467, bf16[96,324]{0,1:T(8,128)(2,1)S(1)} %reshape.468, bf16[96,324]{0,1:T(8,128)(2,1)S(1)} %reshape.469, ...), dimensions={0} | concatenate | bytes 1119744 | tf_op jit(solution)/shard_map/concatenate | solution.py:211
  48.6 3.5 %collective-permute-start.4 = (bf16[9,96,16]{1,2,0:T(8,128)(2,1)S(1)}, bf16[9,96,16]{1,2,0:T(8,128)(2,1)S(1)}, u32[]{:S(2)}, u32[]{:S(2)}) collective-permute-start(bf16[9,96,16]{1,2,0:T(8,128)(2,1)S(1)} %constant_dynamic-update-slice_fusion.27), channel_id=1, source_target_pairs={{0,1},{1,0},{2,3},{3,2},{4,5},{5,4},{6,7},{7,6},{8,9},{9,8},{10,11... | collective-permute-start | bytes 82952 | tf_op jit(solution)/shard_map/ppermute | solution.py:59
  52.1 1.9 %collective-permute-start.5 = (bf16[9,96,16]{1,2,0:T(8,128)(2,1)S(1)}, bf16[9,96,16]{1,2,0:T(8,128)(2,1)S(1)}, u32[]{:S(2)}, u32[]{:S(2)}) collective-permute-start(bf16[9,96,16]{1,2,0:T(8,128)(2,1)S(1)} %constant_dynamic-update-slice_fusion.27), channel_id=1, source_target_pairs={{0,511},{1,2},{2,1},{3,4},{4,3},{5,6},{6,5},{7,8},{8,7},{9,10},{10... | collective-permute-start | bytes 82952 | tf_op jit(solution)/shard_map/ppermute | solution.py:60
  54.1 3.3 %collective-permute-done.5 = bf16[9,96,16]{1,2,0:T(8,128)(2,1)S(1)} collective-permute-done((bf16[9,96,16]{1,2,0:T(8,128)(2,1)S(1)}, bf16[9,96,16]{1,2,0:T(8,128)(2,1)S(1)}, u32[]{:S(2)}, u32[]{:S(2)}) %collective-permute-start.5) | collective-permute-done | bytes 27680 | tf_op jit(solution)/shard_map/ppermute | solution.py:60
  57.5 9.3 %collective-permute-start.6 = (bf16[9,96,16]{1,2,0:T(8,128)(2,1)S(1)}, bf16[9,96,16]{1,2,0:T(8,128)(2,1)S(1)}, u32[]{:S(2)}, u32[]{:S(2)}) collective-permute-start(bf16[9,96,16]{1,2,0:T(8,128)(2,1)S(1)} %constant_dynamic-update-slice_fusion.36), channel_id=1, source_target_pairs={{0,504},{1,505},{2,506},{3,507},{4,508},{5,509},{6,510},{7,511},{8... | collective-permute-start | bytes 82952 | tf_op jit(solution)/shard_map/ppermute | solution.py:60
  66.7 1.9 %collective-permute-start.7 = (bf16[9,96,16]{1,2,0:T(8,128)(2,1)S(1)}, bf16[9,96,16]{1,2,0:T(8,128)(2,1)S(1)}, u32[]{:S(2)}, u32[]{:S(2)}) collective-permute-start(bf16[9,96,16]{1,2,0:T(8,128)(2,1)S(1)} %constant_dynamic-update-slice_fusion.36), channel_id=1, source_target_pairs={{0,8},{1,9},{2,10},{3,11},{4,12},{5,13},{6,14},{7,15},{8,0},{9,1},... | collective-permute-start | bytes 82952 | tf_op jit(solution)/shard_map/ppermute | solution.py:59
  69.4 1.1 collective-permute-done.6
  70.5 5.1 %collective-permute-done.7 = bf16[9,96,16]{1,2,0:T(8,128)(2,1)S(1)} collective-permute-done((bf16[9,96,16]{1,2,0:T(8,128)(2,1)S(1)}, bf16[9,96,16]{1,2,0:T(8,128)(2,1)S(1)}, u32[]{:S(2)}, u32[]{:S(2)}) %collective-permute-start.7) | collective-permute-done | bytes 27680 | tf_op jit(solution)/shard_map/ppermute | solution.py:59
  75.7 0.6 gather_fusion.2
  79.4 4.0 %collective-permute-start.8 = (f32[83456]{0:T(1024)S(1)}, f32[83456]{0:T(1024)S(1)}, u32[]{:S(2)}, u32[]{:S(2)}) collective-permute-start(f32[83456]{0:T(1024)S(1)} %broadcast_select_fusion), channel_id=1, source_target_pairs={{0,1},{1,0},{2,3},{3,2},{4,5},{5,4},{6,7},{7,6},{8,9},{9,8},{10,11... | collective-permute-start | bytes 1001480 | tf_op jit(solution)/shard_map/ppermute | solution.py:23
  83.4 1.2 collective-permute-done.8
  84.7 1.9 %collective-permute-start.9 = (f32[41728]{0:T(1024)S(1)}, f32[41728]{0:T(1024)S(1)}, u32[]{:S(2)}, u32[]{:S(2)}) collective-permute-start(f32[41728]{0:T(1024)S(1)} %slice_select_fusion), channel_id=1, source_target_pairs={{0,2},{1,3},{2,0},{3,1},{4,6},{5,7},{6,4},{7,5},{8,10},{9,11},{10,... | collective-permute-start | bytes 500744 | tf_op jit(solution)/shard_map/ppermute | solution.py:23
  86.6 5.4 %collective-permute-done.9 = f32[41728]{0:T(1024)S(1)} collective-permute-done((f32[41728]{0:T(1024)S(1)}, f32[41728]{0:T(1024)S(1)}, u32[]{:S(2)}, u32[]{:S(2)}) %collective-permute-start.9) | collective-permute-done | bytes 166944 | tf_op jit(solution)/shard_map/ppermute | solution.py:23
  92.1 5.5 %collective-permute-start.10 = (f32[20864]{0:T(1024)S(1)}, f32[20864]{0:T(1024)S(1)}, u32[]{:S(2)}, u32[]{:S(2)}) collective-permute-start(f32[20864]{0:T(1024)S(1)} %slice_select_fusion.1), channel_id=1, source_target_pairs={{0,4},{1,5},{2,6},{3,7},{4,0},{5,1},{6,2},{7,3},{8,12},{9,13},{10,... | collective-permute-start | bytes 250376 | tf_op jit(solution)/shard_map/ppermute | solution.py:23
  97.6 2.2 %collective-permute-done.10 = f32[20864]{0:T(1024)S(1)} collective-permute-done((f32[20864]{0:T(1024)S(1)}, f32[20864]{0:T(1024)S(1)}, u32[]{:S(2)}, u32[]{:S(2)}) %collective-permute-start.10) | collective-permute-done | bytes 83488 | tf_op jit(solution)/shard_map/ppermute | solution.py:23
  99.8 1.9 %collective-permute-start.11 = (f32[20864]{0:T(1024)S(1)}, f32[20864]{0:T(1024)S(1)}, u32[]{:S(2)}, u32[]{:S(2)}) collective-permute-start(f32[20864]{0:T(1024)S(1)} %select_add_fusion.2), channel_id=1, source_target_pairs={{0,8},{1,9},{2,10},{3,11},{4,12},{5,13},{6,14},{7,15},{8,0},{9,1},... | collective-permute-start | bytes 250376 | tf_op jit(solution)/shard_map/ppermute | solution.py:23
  102.0 7.9 %collective-permute-done.11 = f32[20864]{0:T(1024)S(1)} collective-permute-done((f32[20864]{0:T(1024)S(1)}, f32[20864]{0:T(1024)S(1)}, u32[]{:S(2)}, u32[]{:S(2)}) %collective-permute-start.11) | collective-permute-done | bytes 83488 | tf_op jit(solution)/shard_map/ppermute | solution.py:23
  109.9 1.9 %collective-permute-start.12 = (f32[20864]{0:T(1024)S(1)}, f32[20864]{0:T(1024)S(1)}, u32[]{:S(2)}, u32[]{:S(2)}) collective-permute-start(f32[20864]{0:T(1024)S(1)} %add.346), channel_id=1, source_target_pairs={{0,16},{1,17},{2,18},{3,19},{4,20},{5,21},{6,22},{7,23},{8,24},{9,... | collective-permute-start | bytes 250376 | tf_op jit(solution)/shard_map/ppermute | solution.py:23
  111.8 3.3 %collective-permute-done.12 = f32[20864]{0:T(1024)S(1)} collective-permute-done((f32[20864]{0:T(1024)S(1)}, f32[20864]{0:T(1024)S(1)}, u32[]{:S(2)}, u32[]{:S(2)}) %collective-permute-start.12) | collective-permute-done | bytes 83488 | tf_op jit(solution)/shard_map/ppermute | solution.py:23
  115.1 1.9 %collective-permute-start.13 = (f32[20864]{0:T(1024)S(1)}, f32[20864]{0:T(1024)S(1)}, u32[]{:S(2)}, u32[]{:S(2)}) collective-permute-start(f32[20864]{0:T(1024)S(1)} %add.347), channel_id=1, source_target_pairs={{0,32},{1,33},{2,34},{3,35},{4,36},{5,37},{6,38},{7,39},{8,40},{9,... | collective-permute-start | bytes 250376 | tf_op jit(solution)/shard_map/ppermute | solution.py:23
  117.1 4.8 %collective-permute-done.13 = f32[20864]{0:T(1024)S(1)} collective-permute-done((f32[20864]{0:T(1024)S(1)}, f32[20864]{0:T(1024)S(1)}, u32[]{:S(2)}, u32[]{:S(2)}) %collective-permute-start.13) | collective-permute-done | bytes 83488 | tf_op jit(solution)/shard_map/ppermute | solution.py:23
  121.9 1.9 %collective-permute-start.14 = (f32[20864]{0:T(1024)S(1)}, f32[20864]{0:T(1024)S(1)}, u32[]{:S(2)}, u32[]{:S(2)}) collective-permute-start(f32[20864]{0:T(1024)S(1)} %add.348), channel_id=1, source_target_pairs={{0,64},{1,65},{2,66},{3,67},{4,68},{5,69},{6,70},{7,71},{8,72},{9,... | collective-permute-start | bytes 250376 | tf_op jit(solution)/shard_map/ppermute | solution.py:23
  123.8 3.6 %collective-permute-done.14 = f32[20864]{0:T(1024)S(1)} collective-permute-done((f32[20864]{0:T(1024)S(1)}, f32[20864]{0:T(1024)S(1)}, u32[]{:S(2)}, u32[]{:S(2)}) %collective-permute-start.14) | collective-permute-done | bytes 83488 | tf_op jit(solution)/shard_map/ppermute | solution.py:23
  127.4 1.9 %collective-permute-start.15 = (f32[20864]{0:T(1024)S(1)}, f32[20864]{0:T(1024)S(1)}, u32[]{:S(2)}, u32[]{:S(2)}) collective-permute-start(f32[20864]{0:T(1024)S(1)} %add.349), channel_id=1, source_target_pairs={{0,128},{1,129},{2,130},{3,131},{4,132},{5,133},{6,134},{7,135},{8... | collective-permute-start | bytes 250376 | tf_op jit(solution)/shard_map/ppermute | solution.py:23
  129.4 4.6 %collective-permute-done.15 = f32[20864]{0:T(1024)S(1)} collective-permute-done((f32[20864]{0:T(1024)S(1)}, f32[20864]{0:T(1024)S(1)}, u32[]{:S(2)}, u32[]{:S(2)}) %collective-permute-start.15) | collective-permute-done | bytes 83488 | tf_op jit(solution)/shard_map/ppermute | solution.py:23
  134.0 4.7 %collective-permute-start.16 = (f32[20864]{0:T(1024)S(1)}, f32[20864]{0:T(1024)S(1)}, u32[]{:S(2)}, u32[]{:S(2)}) collective-permute-start(f32[20864]{0:T(1024)S(1)} %add.350), channel_id=1, source_target_pairs={{0,256},{1,257},{2,258},{3,259},{4,260},{5,261},{6,262},{7,263},{8... | collective-permute-start | bytes 250376 | tf_op jit(solution)/shard_map/ppermute | solution.py:23
  138.7 5.3 %collective-permute-done.16 = f32[20864]{0:T(1024)S(1)} collective-permute-done((f32[20864]{0:T(1024)S(1)}, f32[20864]{0:T(1024)S(1)}, u32[]{:S(2)}, u32[]{:S(2)}) %collective-permute-start.16) | collective-permute-done | bytes 83488 | tf_op jit(solution)/shard_map/ppermute | solution.py:23
  144.1 3.6 %collective-permute-start.17 = (f32[20864]{0:T(1024)S(1)}, f32[20864]{0:T(1024)S(1)}, u32[]{:S(2)}, u32[]{:S(2)}) collective-permute-start(f32[20864]{0:T(1024)S(1)} %add.351), channel_id=1, source_target_pairs={{0,4},{1,5},{2,6},{3,7},{4,0},{5,1},{6,2},{7,3},{8,12},{9,13},{10,... | collective-permute-start | bytes 250376 | tf_op jit(solution)/shard_map/ppermute | solution.py:23
  147.7 2.4 %collective-permute-done.17 = f32[20864]{0:T(1024)S(1)} collective-permute-done((f32[20864]{0:T(1024)S(1)}, f32[20864]{0:T(1024)S(1)}, u32[]{:S(2)}, u32[]{:S(2)}) %collective-permute-start.17) | collective-permute-done | bytes 83488 | tf_op jit(solution)/shard_map/ppermute | solution.py:23
  150.2 4.6 %collective-permute-start.18 = (f32[41728]{0:T(1024)S(1)}, f32[41728]{0:T(1024)S(1)}, u32[]{:S(2)}, u32[]{:S(2)}) collective-permute-start(f32[41728]{0:T(1024)S(1)} %maximum_select_fusion.2), channel_id=1, source_target_pairs={{0,2},{1,3},{2,0},{3,1},{4,6},{5,7},{6,4},{7,5},{8,10},{9,11},{10,... | collective-permute-start | bytes 500744 | tf_op jit(solution)/shard_map/ppermute | solution.py:23
  154.9 2.6 %collective-permute-done.18 = f32[41728]{0:T(1024)S(1)} collective-permute-done((f32[41728]{0:T(1024)S(1)}, f32[41728]{0:T(1024)S(1)}, u32[]{:S(2)}, u32[]{:S(2)}) %collective-permute-start.18) | collective-permute-done | bytes 166944 | tf_op jit(solution)/shard_map/ppermute | solution.py:23
  157.6 13.8 %collective-permute-start.19 = (f32[83456]{0:T(1024)S(1)}, f32[83456]{0:T(1024)S(1)}, u32[]{:S(2)}, u32[]{:S(2)}) collective-permute-start(f32[83456]{0:T(1024)S(1)} %maximum_select_fusion.1), channel_id=1, source_target_pairs={{0,1},{1,0},{2,3},{3,2},{4,5},{5,4},{6,7},{7,6},{8,9},{9,8},{10,11... | collective-permute-start | bytes 1001480 | tf_op jit(solution)/shard_map/ppermute | solution.py:23
  171.4 0.7 copy.261
  172.1 0.9 fusion.4
  173.7 0.9 mul.191
  174.6 0.9 mul.193
  (239 shorter events, 11.5 us)
Async XLA Ops:
  0.6 1.0 copy-start.3
  2.2 2.1 %copy-start.1 = (bf16[9,96,96]{2,1,0:T(8,128)(2,1)S(1)}, bf16[9,96,96]{2,1,0:T(8,128)(2,1)}, u32[]{:S(2)}) copy-start(bf16[9,96,96]{2,1,0:T(8,128)(2,1)} %param.17) | copy-start | bytes 497668
  4.9 11.6 %copy-start.7 = (s32[1,4]{1,0:T(1,128)S(1)}, s32[1,4]{1,0:T(1,128)}, u32[]{:S(2)}) copy-start(s32[1,4]{1,0:T(1,128)} %param.20) | copy-start | bytes 52
  4.9 11.6 %copy-start.4 = (s32[1,4]{1,0:T(1,128)S(1)}, s32[1,4]{1,0:T(1,128)}, u32[]{:S(2)}) copy-start(s32[1,4]{1,0:T(1,128)} %param.19) | copy-start | bytes 52
  4.9 11.6 %copy-start.5 = (s32[1,4]{1,0:T(1,128)S(1)}, s32[1,4]{1,0:T(1,128)}, u32[]{:S(2)}) copy-start(s32[1,4]{1,0:T(1,128)} %param.21) | copy-start | bytes 52
  4.9 11.6 %copy-start.11 = (s32[4]{0:T(128)S(1)}, s32[4]{0:T(128)}, u32[]{:S(2)}) copy-start(s32[4]{0:T(128)} %constant.138.clone) | copy-start | bytes 52
  4.9 11.8 %copy-start.10 = (s32[4]{0:T(128)S(1)}, s32[4]{0:T(128)}, u32[]{:S(2)}) copy-start(s32[4]{0:T(128)} %constant.139.clone) | copy-start | bytes 52
  5.0 12.0 %copy-start.8 = (s32[1,4]{1,0:T(1,128)S(1)}, s32[1,4]{1,0:T(1,128)}, u32[]{:S(2)}) copy-start(s32[1,4]{1,0:T(1,128)} %param.22) | copy-start | bytes 52
  5.0 0.7 copy-start.6
  5.1 27.5 %copy-start = (bf16[9,96,96]{2,1,0:T(8,128)(2,1)S(1)}, bf16[9,96,96]{2,1,0:T(8,128)(2,1)}, u32[]{:S(2)}) copy-start(bf16[9,96,96]{2,1,0:T(8,128)(2,1)} %param.15) | copy-start | bytes 497668
  5.8 11.4 %collective-permute-start = (bf16[9,96,16]{1,2,0:T(8,128)(2,1)S(1)}, bf16[9,96,16]{1,2,0:T(8,128)(2,1)S(1)}, u32[]{:S(2)}, u32[]{:S(2)}) collective-permute-start(bf16[9,96,16]{1,2,0:T(8,128)(2,1)S(1)} %constant_dynamic-update-slice_fusion), channel_id=1, source_target_pairs={{0,1},{1,0},{2,3},{3,2},{4,5},{5,4},{6,7},{7,6},{8,9},{9,8},{10,11... | collective-permute-start | bytes 82952 | tf_op jit(solution)/shard_map/ppermute | solution.py:59
  14.5 5.3 %collective-permute-start.1 = (bf16[9,96,16]{1,2,0:T(8,128)(2,1)S(1)}, bf16[9,96,16]{1,2,0:T(8,128)(2,1)S(1)}, u32[]{:S(2)}, u32[]{:S(2)}) collective-permute-start(bf16[9,96,16]{1,2,0:T(8,128)(2,1)S(1)} %constant_dynamic-update-slice_fusion), channel_id=1, source_target_pairs={{0,511},{1,2},{2,1},{3,4},{4,3},{5,6},{6,5},{7,8},{8,7},{9,10},{10... | collective-permute-start | bytes 82952 | tf_op jit(solution)/shard_map/ppermute | solution.py:60
  19.8 12.9 %collective-permute-start.2 = (bf16[9,96,16]{1,2,0:T(8,128)(2,1)S(1)}, bf16[9,96,16]{1,2,0:T(8,128)(2,1)S(1)}, u32[]{:S(2)}, u32[]{:S(2)}) collective-permute-start(bf16[9,96,16]{1,2,0:T(8,128)(2,1)S(1)} %constant_dynamic-update-slice_fusion.9), channel_id=1, source_target_pairs={{0,504},{1,505},{2,506},{3,507},{4,508},{5,509},{6,510},{7,511},{8... | collective-permute-start | bytes 82952 | tf_op jit(solution)/shard_map/ppermute | solution.py:60
  30.5 9.3 %collective-permute-start.3 = (bf16[9,96,16]{1,2,0:T(8,128)(2,1)S(1)}, bf16[9,96,16]{1,2,0:T(8,128)(2,1)S(1)}, u32[]{:S(2)}, u32[]{:S(2)}) collective-permute-start(bf16[9,96,16]{1,2,0:T(8,128)(2,1)S(1)} %constant_dynamic-update-slice_fusion.9), channel_id=1, source_target_pairs={{0,8},{1,9},{2,10},{3,11},{4,12},{5,13},{6,14},{7,15},{8,0},{9,1},... | collective-permute-start | bytes 82952 | tf_op jit(solution)/shard_map/ppermute | solution.py:59
  42.4 0.8 copy-start.2
  43.7 0.7 copy-start.9
  48.6 5.5 %collective-permute-start.4 = (bf16[9,96,16]{1,2,0:T(8,128)(2,1)S(1)}, bf16[9,96,16]{1,2,0:T(8,128)(2,1)S(1)}, u32[]{:S(2)}, u32[]{:S(2)}) collective-permute-start(bf16[9,96,16]{1,2,0:T(8,128)(2,1)S(1)} %constant_dynamic-update-slice_fusion.27), channel_id=1, source_target_pairs={{0,1},{1,0},{2,3},{3,2},{4,5},{5,4},{6,7},{7,6},{8,9},{9,8},{10,11... | collective-permute-start | bytes 82952 | tf_op jit(solution)/shard_map/ppermute | solution.py:59
  52.1 5.3 %collective-permute-start.5 = (bf16[9,96,16]{1,2,0:T(8,128)(2,1)S(1)}, bf16[9,96,16]{1,2,0:T(8,128)(2,1)S(1)}, u32[]{:S(2)}, u32[]{:S(2)}) collective-permute-start(bf16[9,96,16]{1,2,0:T(8,128)(2,1)S(1)} %constant_dynamic-update-slice_fusion.27), channel_id=1, source_target_pairs={{0,511},{1,2},{2,1},{3,4},{4,3},{5,6},{6,5},{7,8},{8,7},{9,10},{10... | collective-permute-start | bytes 82952 | tf_op jit(solution)/shard_map/ppermute | solution.py:60
  57.5 13.1 %collective-permute-start.6 = (bf16[9,96,16]{1,2,0:T(8,128)(2,1)S(1)}, bf16[9,96,16]{1,2,0:T(8,128)(2,1)S(1)}, u32[]{:S(2)}, u32[]{:S(2)}) collective-permute-start(bf16[9,96,16]{1,2,0:T(8,128)(2,1)S(1)} %constant_dynamic-update-slice_fusion.36), channel_id=1, source_target_pairs={{0,504},{1,505},{2,506},{3,507},{4,508},{5,509},{6,510},{7,511},{8... | collective-permute-start | bytes 82952 | tf_op jit(solution)/shard_map/ppermute | solution.py:60
  66.7 8.9 %collective-permute-start.7 = (bf16[9,96,16]{1,2,0:T(8,128)(2,1)S(1)}, bf16[9,96,16]{1,2,0:T(8,128)(2,1)S(1)}, u32[]{:S(2)}, u32[]{:S(2)}) collective-permute-start(bf16[9,96,16]{1,2,0:T(8,128)(2,1)S(1)} %constant_dynamic-update-slice_fusion.36), channel_id=1, source_target_pairs={{0,8},{1,9},{2,10},{3,11},{4,12},{5,13},{6,14},{7,15},{8,0},{9,1},... | collective-permute-start | bytes 82952 | tf_op jit(solution)/shard_map/ppermute | solution.py:59
  79.4 5.2 %collective-permute-start.8 = (f32[83456]{0:T(1024)S(1)}, f32[83456]{0:T(1024)S(1)}, u32[]{:S(2)}, u32[]{:S(2)}) collective-permute-start(f32[83456]{0:T(1024)S(1)} %broadcast_select_fusion), channel_id=1, source_target_pairs={{0,1},{1,0},{2,3},{3,2},{4,5},{5,4},{6,7},{7,6},{8,9},{9,8},{10,11... | collective-permute-start | bytes 1001480 | tf_op jit(solution)/shard_map/ppermute | solution.py:23
  84.7 7.4 %collective-permute-start.9 = (f32[41728]{0:T(1024)S(1)}, f32[41728]{0:T(1024)S(1)}, u32[]{:S(2)}, u32[]{:S(2)}) collective-permute-start(f32[41728]{0:T(1024)S(1)} %slice_select_fusion), channel_id=1, source_target_pairs={{0,2},{1,3},{2,0},{3,1},{4,6},{5,7},{6,4},{7,5},{8,10},{9,11},{10,... | collective-permute-start | bytes 500744 | tf_op jit(solution)/shard_map/ppermute | solution.py:23
  92.1 7.7 %collective-permute-start.10 = (f32[20864]{0:T(1024)S(1)}, f32[20864]{0:T(1024)S(1)}, u32[]{:S(2)}, u32[]{:S(2)}) collective-permute-start(f32[20864]{0:T(1024)S(1)} %slice_select_fusion.1), channel_id=1, source_target_pairs={{0,4},{1,5},{2,6},{3,7},{4,0},{5,1},{6,2},{7,3},{8,12},{9,13},{10,... | collective-permute-start | bytes 250376 | tf_op jit(solution)/shard_map/ppermute | solution.py:23
  99.8 10.1 %collective-permute-start.11 = (f32[20864]{0:T(1024)S(1)}, f32[20864]{0:T(1024)S(1)}, u32[]{:S(2)}, u32[]{:S(2)}) collective-permute-start(f32[20864]{0:T(1024)S(1)} %select_add_fusion.2), channel_id=1, source_target_pairs={{0,8},{1,9},{2,10},{3,11},{4,12},{5,13},{6,14},{7,15},{8,0},{9,1},... | collective-permute-start | bytes 250376 | tf_op jit(solution)/shard_map/ppermute | solution.py:23
  109.9 5.2 %collective-permute-start.12 = (f32[20864]{0:T(1024)S(1)}, f32[20864]{0:T(1024)S(1)}, u32[]{:S(2)}, u32[]{:S(2)}) collective-permute-start(f32[20864]{0:T(1024)S(1)} %add.346), channel_id=1, source_target_pairs={{0,16},{1,17},{2,18},{3,19},{4,20},{5,21},{6,22},{7,23},{8,24},{9,... | collective-permute-start | bytes 250376 | tf_op jit(solution)/shard_map/ppermute | solution.py:23
  115.1 6.7 %collective-permute-start.13 = (f32[20864]{0:T(1024)S(1)}, f32[20864]{0:T(1024)S(1)}, u32[]{:S(2)}, u32[]{:S(2)}) collective-permute-start(f32[20864]{0:T(1024)S(1)} %add.347), channel_id=1, source_target_pairs={{0,32},{1,33},{2,34},{3,35},{4,36},{5,37},{6,38},{7,39},{8,40},{9,... | collective-permute-start | bytes 250376 | tf_op jit(solution)/shard_map/ppermute | solution.py:23
  121.9 5.5 %collective-permute-start.14 = (f32[20864]{0:T(1024)S(1)}, f32[20864]{0:T(1024)S(1)}, u32[]{:S(2)}, u32[]{:S(2)}) collective-permute-start(f32[20864]{0:T(1024)S(1)} %add.348), channel_id=1, source_target_pairs={{0,64},{1,65},{2,66},{3,67},{4,68},{5,69},{6,70},{7,71},{8,72},{9,... | collective-permute-start | bytes 250376 | tf_op jit(solution)/shard_map/ppermute | solution.py:23
  127.4 6.6 %collective-permute-start.15 = (f32[20864]{0:T(1024)S(1)}, f32[20864]{0:T(1024)S(1)}, u32[]{:S(2)}, u32[]{:S(2)}) collective-permute-start(f32[20864]{0:T(1024)S(1)} %add.349), channel_id=1, source_target_pairs={{0,128},{1,129},{2,130},{3,131},{4,132},{5,133},{6,134},{7,135},{8... | collective-permute-start | bytes 250376 | tf_op jit(solution)/shard_map/ppermute | solution.py:23
  134.0 10.1 %collective-permute-start.16 = (f32[20864]{0:T(1024)S(1)}, f32[20864]{0:T(1024)S(1)}, u32[]{:S(2)}, u32[]{:S(2)}) collective-permute-start(f32[20864]{0:T(1024)S(1)} %add.350), channel_id=1, source_target_pairs={{0,256},{1,257},{2,258},{3,259},{4,260},{5,261},{6,262},{7,263},{8... | collective-permute-start | bytes 250376 | tf_op jit(solution)/shard_map/ppermute | solution.py:23
  144.1 6.1 %collective-permute-start.17 = (f32[20864]{0:T(1024)S(1)}, f32[20864]{0:T(1024)S(1)}, u32[]{:S(2)}, u32[]{:S(2)}) collective-permute-start(f32[20864]{0:T(1024)S(1)} %add.351), channel_id=1, source_target_pairs={{0,4},{1,5},{2,6},{3,7},{4,0},{5,1},{6,2},{7,3},{8,12},{9,13},{10,... | collective-permute-start | bytes 250376 | tf_op jit(solution)/shard_map/ppermute | solution.py:23
  150.2 7.3 %collective-permute-start.18 = (f32[41728]{0:T(1024)S(1)}, f32[41728]{0:T(1024)S(1)}, u32[]{:S(2)}, u32[]{:S(2)}) collective-permute-start(f32[41728]{0:T(1024)S(1)} %maximum_select_fusion.2), channel_id=1, source_target_pairs={{0,2},{1,3},{2,0},{3,1},{4,6},{5,7},{6,4},{7,5},{8,10},{9,11},{10,... | collective-permute-start | bytes 500744 | tf_op jit(solution)/shard_map/ppermute | solution.py:23
  157.6 15.4 %collective-permute-start.19 = (f32[83456]{0:T(1024)S(1)}, f32[83456]{0:T(1024)S(1)}, u32[]{:S(2)}, u32[]{:S(2)}) collective-permute-start(f32[83456]{0:T(1024)S(1)} %maximum_select_fusion.1), channel_id=1, source_target_pairs={{0,1},{1,0},{2,3},{3,2},{4,5},{5,4},{6,7},{7,6},{8,9},{9,8},{10,11... | collective-permute-start | bytes 1001480 | tf_op jit(solution)/shard_map/ppermute | solution.py:23

commit v9 on v7

--- a/solution.py
+++ b/solution.py
@@ -291,7 +291,8 @@
     output = (fields[0].astype(jnp.float32) + conv_cells(padded_act, conv_b)).astype(jnp.bfloat16)
     terms_b = weight_terms(padded_act, upstream, cell_width)
     tap_size = terms_a.size
-    flat = jnp.concatenate([terms_a.reshape(-1), terms_b.reshape(-1), terms_bias])
+    grad_scale = (lax.axis_size("tiles") * cell_width * cell_width) ** (-0.5)
+    flat = jnp.concatenate([terms_a.reshape(-1), terms_b.reshape(-1), terms_bias]) * grad_scale
     summed = tree_all_reduce(flat, HALVING_ROUNDS)
     summed_a = summed[:tap_size].reshape(terms_a.shape)
     summed_b = summed[tap_size : 2 * tap_size].reshape(terms_b.shape)
@@ -300,14 +301,7 @@
         channels, cell_width * cell_width
     )
     grad_fields = (upstream.astype(jnp.float32) + pulled_x).astype(jnp.bfloat16)
-    grad_scale = (lax.axis_size("tiles") * cell_width * cell_width) ** (-0.5)
-    return (
-        output[None],
-        grad_fields[None],
-        summed_a * grad_scale,
-        summed_b * grad_scale,
-        summed_bias * grad_scale,
-    )
+    return (output[None], grad_fields[None], summed_a, summed_b, summed_bias)
 
 
 def solution(mesh):

time: 176 us -> 176 us (level)
    mul x2 -> x0, local copies, waits for them, and re-layouts: 1.85 us -> none  [the longest x1 0.93 us: body(): summed_a * grad_scale]
    reshape x0 -> x2, local copies, waits for them, and re-layouts: none -> 1.85 us  [the longest x1 0.93 us: body(): summed_a = summed[:tap_size].reshape(terms_a.shape)]
where the time goes in v9:
time: 176 us; the launch traced here: 175 us
  starting transfers between devices  87.6 us (50%)
  waiting for transfers between devices  60.5 us (34%)
  local copies, waits for them, and re-layouts  18.1 us (10%)
  matrix products  4.91 us (3%)
  between operations  2.19 us (1%)
  other arithmetic  2.08 us (1%)
    ppermute x12, starting transfers between devices, xor_partner(): lax.ppermute(block, 'tiles', [(i, i ^ distance) for i in range(devices)])  47.7 us
    ppermute x12, waiting for transfers between devices, xor_partner(): lax.ppermute(block, 'tiles', [(i, i ^ distance) for i in range(devices)])  42.3 us
    ppermute x4, starting transfers between devices, paired_shift(): got_other = lax.ppermute(block, 'tiles', other)  23.8 us
    ppermute x4, starting transfers between devices, paired_shift(): got_flip = lax.ppermute(block, 'tiles', flip)  16.1 us
    ppermute x4, waiting for transfers between devices, paired_shift(): got_flip = lax.ppermute(block, 'tiles', flip)  12 us
    ppermute x4, waiting for transfers between devices, paired_shift(): got_other = lax.ppermute(block, 'tiles', other)  6.16 us
    concatenate x2, local copies, waits for them, and re-layouts, spread_back(): jnp.concatenate([wide_grid[:, 2 - r:2 - r + ext_width, 2 - c:2 - c + ext_...  4.19 us
    unnamed x61, local copies, waits for them, and re-layouts  4.06 us
  transfers between devices with their start and end apart: 20, of which 17 were waited for; matrix products, arithmetic and copies ran while one was open for 3% of the time, Pallas kernels for 0%

profile of v9, /device:TPU:1, one launch (start us, length us, event | category | flops | bytes accessed | tf_op | source)
XLA Modules:
  0.0 175.4 jit_solution(3173200601946863904)
XLA Ops:
  0.6 0.9 copy.202
  2.2 2.1 %concatenate.129 = bf16[864,324]{0,1:T(8,128)(2,1)S(1)} concatenate(bf16[96,324]{0,1:T(8,128)(2,1)S(1)} %reshape.435, bf16[96,324]{0,1:T(8,128)(2,1)S(1)} %reshape.436, bf16[96,324]{0,1:T(8,128)(2,1)S(1)} %reshape.437, bf16[96,324]{0,1:T(8,128)(2,1)S(1)} %reshape.438, bf16[96,324]{0,1:T(8,128)(2,1)S(1)} %reshape.439, bf16[96,324]{0,1:T(8,128)(2,1)S(1)} %reshape.440, ...), dimensions={0} | concatenate | bytes 1119744 | tf_op jit(solution)/shard_map/concatenate | solution.py:211
  5.8 8.7 %collective-permute-start = (bf16[9,96,16]{1,2,0:T(8,128)(2,1)S(1)}, bf16[9,96,16]{1,2,0:T(8,128)(2,1)S(1)}, u32[]{:S(2)}, u32[]{:S(2)}) collective-permute-start(bf16[9,96,16]{1,2,0:T(8,128)(2,1)S(1)} %constant_dynamic-update-slice_fusion), channel_id=1, source_target_pairs={{0,1},{1,0},{2,3},{3,2},{4,5},{5,4},{6,7},{7,6},{8,9},{9,8},{10,11... | collective-permute-start | bytes 82952 | tf_op jit(solution)/shard_map/ppermute | solution.py:59
  14.5 1.9 %collective-permute-start.1 = (bf16[9,96,16]{1,2,0:T(8,128)(2,1)S(1)}, bf16[9,96,16]{1,2,0:T(8,128)(2,1)S(1)}, u32[]{:S(2)}, u32[]{:S(2)}) collective-permute-start(bf16[9,96,16]{1,2,0:T(8,128)(2,1)S(1)} %constant_dynamic-update-slice_fusion), channel_id=1, source_target_pairs={{0,511},{1,2},{2,1},{3,4},{4,3},{5,6},{6,5},{7,8},{8,7},{9,10},{10... | collective-permute-start | bytes 82952 | tf_op jit(solution)/shard_map/ppermute | solution.py:60
  17.2 2.6 %collective-permute-done.1 = bf16[9,96,16]{1,2,0:T(8,128)(2,1)S(1)} collective-permute-done((bf16[9,96,16]{1,2,0:T(8,128)(2,1)S(1)}, bf16[9,96,16]{1,2,0:T(8,128)(2,1)S(1)}, u32[]{:S(2)}, u32[]{:S(2)}) %collective-permute-start.1) | collective-permute-done | bytes 27680 | tf_op jit(solution)/shard_map/ppermute | solution.py:60
  19.8 10.7 %collective-permute-start.2 = (bf16[9,96,16]{1,2,0:T(8,128)(2,1)S(1)}, bf16[9,96,16]{1,2,0:T(8,128)(2,1)S(1)}, u32[]{:S(2)}, u32[]{:S(2)}) collective-permute-start(bf16[9,96,16]{1,2,0:T(8,128)(2,1)S(1)} %constant_dynamic-update-slice_fusion.9), channel_id=1, source_target_pairs={{0,504},{1,505},{2,506},{3,507},{4,508},{5,509},{6,510},{7,511},{8... | collective-permute-start | bytes 82952 | tf_op jit(solution)/shard_map/ppermute | solution.py:60
  30.5 1.9 %collective-permute-start.3 = (bf16[9,96,16]{1,2,0:T(8,128)(2,1)S(1)}, bf16[9,96,16]{1,2,0:T(8,128)(2,1)S(1)}, u32[]{:S(2)}, u32[]{:S(2)}) collective-permute-start(bf16[9,96,16]{1,2,0:T(8,128)(2,1)S(1)} %constant_dynamic-update-slice_fusion.9), channel_id=1, source_target_pairs={{0,8},{1,9},{2,10},{3,11},{4,12},{5,13},{6,14},{7,15},{8,0},{9,1},... | collective-permute-start | bytes 82952 | tf_op jit(solution)/shard_map/ppermute | solution.py:59
  32.9 6.9 %collective-permute-done.3 = bf16[9,96,16]{1,2,0:T(8,128)(2,1)S(1)} collective-permute-done((bf16[9,96,16]{1,2,0:T(8,128)(2,1)S(1)}, bf16[9,96,16]{1,2,0:T(8,128)(2,1)S(1)}, u32[]{:S(2)}, u32[]{:S(2)}) %collective-permute-start.3) | collective-permute-done | bytes 27680 | tf_op jit(solution)/shard_map/ppermute | solution.py:59
  40.7 0.6 gather_fusion
  42.4 0.8 copy-done.3
  43.7 0.6 copy-done.9
  44.3 0.6 convert_reduce_fusion
  45.7 2.1 %concatenate.144 = bf16[864,324]{0,1:T(8,128)(2,1)S(1)} concatenate(bf16[96,324]{0,1:T(8,128)(2,1)S(1)} %reshape.458, bf16[96,324]{0,1:T(8,128)(2,1)S(1)} %reshape.459, bf16[96,324]{0,1:T(8,128)(2,1)S(1)} %reshape.460, bf16[96,324]{0,1:T(8,128)(2,1)S(1)} %reshape.461, bf16[96,324]{0,1:T(8,128)(2,1)S(1)} %reshape.462, bf16[96,324]{0,1:T(8,128)(2,1)S(1)} %reshape.463, ...), dimensions={0} | concatenate | bytes 1119744 | tf_op jit(solution)/shard_map/concatenate | solution.py:211
  48.6 3.5 %collective-permute-start.4 = (bf16[9,96,16]{1,2,0:T(8,128)(2,1)S(1)}, bf16[9,96,16]{1,2,0:T(8,128)(2,1)S(1)}, u32[]{:S(2)}, u32[]{:S(2)}) collective-permute-start(bf16[9,96,16]{1,2,0:T(8,128)(2,1)S(1)} %constant_dynamic-update-slice_fusion.27), channel_id=1, source_target_pairs={{0,1},{1,0},{2,3},{3,2},{4,5},{5,4},{6,7},{7,6},{8,9},{9,8},{10,11... | collective-permute-start | bytes 82952 | tf_op jit(solution)/shard_map/ppermute | solution.py:59
  52.1 1.9 %collective-permute-start.5 = (bf16[9,96,16]{1,2,0:T(8,128)(2,1)S(1)}, bf16[9,96,16]{1,2,0:T(8,128)(2,1)S(1)}, u32[]{:S(2)}, u32[]{:S(2)}) collective-permute-start(bf16[9,96,16]{1,2,0:T(8,128)(2,1)S(1)} %constant_dynamic-update-slice_fusion.27), channel_id=1, source_target_pairs={{0,511},{1,2},{2,1},{3,4},{4,3},{5,6},{6,5},{7,8},{8,7},{9,10},{10... | collective-permute-start | bytes 82952 | tf_op jit(solution)/shard_map/ppermute | solution.py:60
  55.2 2.2 %collective-permute-done.5 = bf16[9,96,16]{1,2,0:T(8,128)(2,1)S(1)} collective-permute-done((bf16[9,96,16]{1,2,0:T(8,128)(2,1)S(1)}, bf16[9,96,16]{1,2,0:T(8,128)(2,1)S(1)}, u32[]{:S(2)}, u32[]{:S(2)}) %collective-permute-start.5) | collective-permute-done | bytes 27680 | tf_op jit(solution)/shard_map/ppermute | solution.py:60
  57.5 9.3 %collective-permute-start.6 = (bf16[9,96,16]{1,2,0:T(8,128)(2,1)S(1)}, bf16[9,96,16]{1,2,0:T(8,128)(2,1)S(1)}, u32[]{:S(2)}, u32[]{:S(2)}) collective-permute-start(bf16[9,96,16]{1,2,0:T(8,128)(2,1)S(1)} %constant_dynamic-update-slice_fusion.36), channel_id=1, source_target_pairs={{0,504},{1,505},{2,506},{3,507},{4,508},{5,509},{6,510},{7,511},{8... | collective-permute-start | bytes 82952 | tf_op jit(solution)/shard_map/ppermute | solution.py:60
  66.7 1.9 %collective-permute-start.7 = (bf16[9,96,16]{1,2,0:T(8,128)(2,1)S(1)}, bf16[9,96,16]{1,2,0:T(8,128)(2,1)S(1)}, u32[]{:S(2)}, u32[]{:S(2)}) collective-permute-start(bf16[9,96,16]{1,2,0:T(8,128)(2,1)S(1)} %constant_dynamic-update-slice_fusion.36), channel_id=1, source_target_pairs={{0,8},{1,9},{2,10},{3,11},{4,12},{5,13},{6,14},{7,15},{8,0},{9,1},... | collective-permute-start | bytes 82952 | tf_op jit(solution)/shard_map/ppermute | solution.py:59
  69.1 1.4 collective-permute-done.6
  70.5 5.1 %collective-permute-done.7 = bf16[9,96,16]{1,2,0:T(8,128)(2,1)S(1)} collective-permute-done((bf16[9,96,16]{1,2,0:T(8,128)(2,1)S(1)}, bf16[9,96,16]{1,2,0:T(8,128)(2,1)S(1)}, u32[]{:S(2)}, u32[]{:S(2)}) %collective-permute-start.7) | collective-permute-done | bytes 27680 | tf_op jit(solution)/shard_map/ppermute | solution.py:59
  76.5 0.6 gather_fusion.2
  79.7 4.0 %collective-permute-start.8 = (f32[83456]{0:T(1024)S(1)}, f32[83456]{0:T(1024)S(1)}, u32[]{:S(2)}, u32[]{:S(2)}) collective-permute-start(f32[83456]{0:T(1024)S(1)} %slice_select_fusion), channel_id=1, source_target_pairs={{0,1},{1,0},{2,3},{3,2},{4,5},{5,4},{6,7},{7,6},{8,9},{9,8},{10,11... | collective-permute-start | bytes 1001480 | tf_op jit(solution)/shard_map/ppermute | solution.py:23
  83.7 1.2 collective-permute-done.8
  85.0 1.9 %collective-permute-start.9 = (f32[41728]{0:T(1024)S(1)}, f32[41728]{0:T(1024)S(1)}, u32[]{:S(2)}, u32[]{:S(2)}) collective-permute-start(f32[41728]{0:T(1024)S(1)} %slice_select_fusion.1), channel_id=1, source_target_pairs={{0,2},{1,3},{2,0},{3,1},{4,6},{5,7},{6,4},{7,5},{8,10},{9,11},{10,... | collective-permute-start | bytes 500744 | tf_op jit(solution)/shard_map/ppermute | solution.py:23
  86.9 5.4 %collective-permute-done.9 = f32[41728]{0:T(1024)S(1)} collective-permute-done((f32[41728]{0:T(1024)S(1)}, f32[41728]{0:T(1024)S(1)}, u32[]{:S(2)}, u32[]{:S(2)}) %collective-permute-start.9) | collective-permute-done | bytes 166944 | tf_op jit(solution)/shard_map/ppermute | solution.py:23
  92.4 5.5 %collective-permute-start.10 = (f32[20864]{0:T(1024)S(1)}, f32[20864]{0:T(1024)S(1)}, u32[]{:S(2)}, u32[]{:S(2)}) collective-permute-start(f32[20864]{0:T(1024)S(1)} %slice_select_fusion.2), channel_id=1, source_target_pairs={{0,4},{1,5},{2,6},{3,7},{4,0},{5,1},{6,2},{7,3},{8,12},{9,13},{10,... | collective-permute-start | bytes 250376 | tf_op jit(solution)/shard_map/ppermute | solution.py:23
  97.9 2.1 %collective-permute-done.10 = f32[20864]{0:T(1024)S(1)} collective-permute-done((f32[20864]{0:T(1024)S(1)}, f32[20864]{0:T(1024)S(1)}, u32[]{:S(2)}, u32[]{:S(2)}) %collective-permute-start.10) | collective-permute-done | bytes 83488 | tf_op jit(solution)/shard_map/ppermute | solution.py:23
  100.1 1.9 %collective-permute-start.11 = (f32[20864]{0:T(1024)S(1)}, f32[20864]{0:T(1024)S(1)}, u32[]{:S(2)}, u32[]{:S(2)}) collective-permute-start(f32[20864]{0:T(1024)S(1)} %select_add_fusion.2), channel_id=1, source_target_pairs={{0,8},{1,9},{2,10},{3,11},{4,12},{5,13},{6,14},{7,15},{8,0},{9,1},... | collective-permute-start | bytes 250376 | tf_op jit(solution)/shard_map/ppermute | solution.py:23
  102.1 8.0 %collective-permute-done.11 = f32[20864]{0:T(1024)S(1)} collective-permute-done((f32[20864]{0:T(1024)S(1)}, f32[20864]{0:T(1024)S(1)}, u32[]{:S(2)}, u32[]{:S(2)}) %collective-permute-start.11) | collective-permute-done | bytes 83488 | tf_op jit(solution)/shard_map/ppermute | solution.py:23
  110.1 1.9 %collective-permute-start.12 = (f32[20864]{0:T(1024)S(1)}, f32[20864]{0:T(1024)S(1)}, u32[]{:S(2)}, u32[]{:S(2)}) collective-permute-start(f32[20864]{0:T(1024)S(1)} %add.346), channel_id=1, source_target_pairs={{0,16},{1,17},{2,18},{3,19},{4,20},{5,21},{6,22},{7,23},{8,24},{9,... | collective-permute-start | bytes 250376 | tf_op jit(solution)/shard_map/ppermute | solution.py:23
  112.6 2.7 %collective-permute-done.12 = f32[20864]{0:T(1024)S(1)} collective-permute-done((f32[20864]{0:T(1024)S(1)}, f32[20864]{0:T(1024)S(1)}, u32[]{:S(2)}, u32[]{:S(2)}) %collective-permute-start.12) | collective-permute-done | bytes 83488 | tf_op jit(solution)/shard_map/ppermute | solution.py:23
  115.4 1.9 %collective-permute-start.13 = (f32[20864]{0:T(1024)S(1)}, f32[20864]{0:T(1024)S(1)}, u32[]{:S(2)}, u32[]{:S(2)}) collective-permute-start(f32[20864]{0:T(1024)S(1)} %add.347), channel_id=1, source_target_pairs={{0,32},{1,33},{2,34},{3,35},{4,36},{5,37},{6,38},{7,39},{8,40},{9,... | collective-permute-start | bytes 250376 | tf_op jit(solution)/shard_map/ppermute | solution.py:23
  117.3 4.8 %collective-permute-done.13 = f32[20864]{0:T(1024)S(1)} collective-permute-done((f32[20864]{0:T(1024)S(1)}, f32[20864]{0:T(1024)S(1)}, u32[]{:S(2)}, u32[]{:S(2)}) %collective-permute-start.13) | collective-permute-done | bytes 83488 | tf_op jit(solution)/shard_map/ppermute | solution.py:23
  122.1 1.9 %collective-permute-start.14 = (f32[20864]{0:T(1024)S(1)}, f32[20864]{0:T(1024)S(1)}, u32[]{:S(2)}, u32[]{:S(2)}) collective-permute-start(f32[20864]{0:T(1024)S(1)} %add.348), channel_id=1, source_target_pairs={{0,64},{1,65},{2,66},{3,67},{4,68},{5,69},{6,70},{7,71},{8,72},{9,... | collective-permute-start | bytes 250376 | tf_op jit(solution)/shard_map/ppermute | solution.py:23
  124.1 3.6 %collective-permute-done.14 = f32[20864]{0:T(1024)S(1)} collective-permute-done((f32[20864]{0:T(1024)S(1)}, f32[20864]{0:T(1024)S(1)}, u32[]{:S(2)}, u32[]{:S(2)}) %collective-permute-start.14) | collective-permute-done | bytes 83488 | tf_op jit(solution)/shard_map/ppermute | solution.py:23
  127.7 1.9 %collective-permute-start.15 = (f32[20864]{0:T(1024)S(1)}, f32[20864]{0:T(1024)S(1)}, u32[]{:S(2)}, u32[]{:S(2)}) collective-permute-start(f32[20864]{0:T(1024)S(1)} %add.349), channel_id=1, source_target_pairs={{0,128},{1,129},{2,130},{3,131},{4,132},{5,133},{6,134},{7,135},{8... | collective-permute-start | bytes 250376 | tf_op jit(solution)/shard_map/ppermute | solution.py:23
  129.6 4.6 %collective-permute-done.15 = f32[20864]{0:T(1024)S(1)} collective-permute-done((f32[20864]{0:T(1024)S(1)}, f32[20864]{0:T(1024)S(1)}, u32[]{:S(2)}, u32[]{:S(2)}) %collective-permute-start.15) | collective-permute-done | bytes 83488 | tf_op jit(solution)/shard_map/ppermute | solution.py:23
  134.2 4.7 %collective-permute-start.16 = (f32[20864]{0:T(1024)S(1)}, f32[20864]{0:T(1024)S(1)}, u32[]{:S(2)}, u32[]{:S(2)}) collective-permute-start(f32[20864]{0:T(1024)S(1)} %add.350), channel_id=1, source_target_pairs={{0,256},{1,257},{2,258},{3,259},{4,260},{5,261},{6,262},{7,263},{8... | collective-permute-start | bytes 250376 | tf_op jit(solution)/shard_map/ppermute | solution.py:23
  139.0 5.3 %collective-permute-done.16 = f32[20864]{0:T(1024)S(1)} collective-permute-done((f32[20864]{0:T(1024)S(1)}, f32[20864]{0:T(1024)S(1)}, u32[]{:S(2)}, u32[]{:S(2)}) %collective-permute-start.16) | collective-permute-done | bytes 83488 | tf_op jit(solution)/shard_map/ppermute | solution.py:23
  144.3 3.6 %collective-permute-start.17 = (f32[20864]{0:T(1024)S(1)}, f32[20864]{0:T(1024)S(1)}, u32[]{:S(2)}, u32[]{:S(2)}) collective-permute-start(f32[20864]{0:T(1024)S(1)} %add.351), channel_id=1, source_target_pairs={{0,4},{1,5},{2,6},{3,7},{4,0},{5,1},{6,2},{7,3},{8,12},{9,13},{10,... | collective-permute-start | bytes 250376 | tf_op jit(solution)/shard_map/ppermute | solution.py:23
  148.0 2.5 %collective-permute-done.17 = f32[20864]{0:T(1024)S(1)} collective-permute-done((f32[20864]{0:T(1024)S(1)}, f32[20864]{0:T(1024)S(1)}, u32[]{:S(2)}, u32[]{:S(2)}) %collective-permute-start.17) | collective-permute-done | bytes 83488 | tf_op jit(solution)/shard_map/ppermute | solution.py:23
  150.5 4.6 %collective-permute-start.18 = (f32[41728]{0:T(1024)S(1)}, f32[41728]{0:T(1024)S(1)}, u32[]{:S(2)}, u32[]{:S(2)}) collective-permute-start(f32[41728]{0:T(1024)S(1)} %maximum_select_fusion.2), channel_id=1, source_target_pairs={{0,2},{1,3},{2,0},{3,1},{4,6},{5,7},{6,4},{7,5},{8,10},{9,11},{10,... | collective-permute-start | bytes 500744 | tf_op jit(solution)/shard_map/ppermute | solution.py:23
  155.4 0.7 copy.249
  156.1 1.7 collective-permute-done.18
  157.8 13.8 %collective-permute-start.19 = (f32[83456]{0:T(1024)S(1)}, f32[83456]{0:T(1024)S(1)}, u32[]{:S(2)}, u32[]{:S(2)}) collective-permute-start(f32[83456]{0:T(1024)S(1)} %maximum_select_fusion.1), channel_id=1, source_target_pairs={{0,1},{1,0},{2,3},{3,2},{4,5},{5,4},{6,7},{7,6},{8,9},{9,8},{10,11... | collective-permute-start | bytes 1001480 | tf_op jit(solution)/shard_map/ppermute | solution.py:23
  171.6 0.9 fusion.4
  173.5 0.9 reshape.481
  174.5 0.9 reshape.482
  (254 shorter events, 13.7 us)
Async XLA Ops:
  0.6 1.0 copy-start
  2.2 2.1 %copy-start.1 = (bf16[9,96,96]{2,1,0:T(8,128)(2,1)S(1)}, bf16[9,96,96]{2,1,0:T(8,128)(2,1)}, u32[]{:S(2)}) copy-start(bf16[9,96,96]{2,1,0:T(8,128)(2,1)} %param.17) | copy-start | bytes 497668
  4.9 11.6 %copy-start.7 = (s32[1,4]{1,0:T(1,128)S(1)}, s32[1,4]{1,0:T(1,128)}, u32[]{:S(2)}) copy-start(s32[1,4]{1,0:T(1,128)} %param.20) | copy-start | bytes 52
  4.9 11.6 %copy-start.4 = (s32[1,4]{1,0:T(1,128)S(1)}, s32[1,4]{1,0:T(1,128)}, u32[]{:S(2)}) copy-start(s32[1,4]{1,0:T(1,128)} %param.19) | copy-start | bytes 52
  4.9 11.6 %copy-start.5 = (s32[1,4]{1,0:T(1,128)S(1)}, s32[1,4]{1,0:T(1,128)}, u32[]{:S(2)}) copy-start(s32[1,4]{1,0:T(1,128)} %param.21) | copy-start | bytes 52
  4.9 11.6 %copy-start.11 = (s32[4]{0:T(128)S(1)}, s32[4]{0:T(128)}, u32[]{:S(2)}) copy-start(s32[4]{0:T(128)} %constant.137.clone) | copy-start | bytes 52
  4.9 11.8 %copy-start.10 = (s32[4]{0:T(128)S(1)}, s32[4]{0:T(128)}, u32[]{:S(2)}) copy-start(s32[4]{0:T(128)} %constant.138.clone) | copy-start | bytes 52
  5.0 12.0 %copy-start.8 = (s32[1,4]{1,0:T(1,128)S(1)}, s32[1,4]{1,0:T(1,128)}, u32[]{:S(2)}) copy-start(s32[1,4]{1,0:T(1,128)} %param.22) | copy-start | bytes 52
  5.0 0.7 copy-start.6
  5.1 27.5 %copy-start.2 = (bf16[9,96,96]{2,1,0:T(8,128)(2,1)S(1)}, bf16[9,96,96]{2,1,0:T(8,128)(2,1)}, u32[]{:S(2)}) copy-start(bf16[9,96,96]{2,1,0:T(8,128)(2,1)} %param.15) | copy-start | bytes 497668
  5.8 11.4 %collective-permute-start = (bf16[9,96,16]{1,2,0:T(8,128)(2,1)S(1)}, bf16[9,96,16]{1,2,0:T(8,128)(2,1)S(1)}, u32[]{:S(2)}, u32[]{:S(2)}) collective-permute-start(bf16[9,96,16]{1,2,0:T(8,128)(2,1)S(1)} %constant_dynamic-update-slice_fusion), channel_id=1, source_target_pairs={{0,1},{1,0},{2,3},{3,2},{4,5},{5,4},{6,7},{7,6},{8,9},{9,8},{10,11... | collective-permute-start | bytes 82952 | tf_op jit(solution)/shard_map/ppermute | solution.py:59
  14.5 5.3 %collective-permute-start.1 = (bf16[9,96,16]{1,2,0:T(8,128)(2,1)S(1)}, bf16[9,96,16]{1,2,0:T(8,128)(2,1)S(1)}, u32[]{:S(2)}, u32[]{:S(2)}) collective-permute-start(bf16[9,96,16]{1,2,0:T(8,128)(2,1)S(1)} %constant_dynamic-update-slice_fusion), channel_id=1, source_target_pairs={{0,511},{1,2},{2,1},{3,4},{4,3},{5,6},{6,5},{7,8},{8,7},{9,10},{10... | collective-permute-start | bytes 82952 | tf_op jit(solution)/shard_map/ppermute | solution.py:60
  19.8 13.1 %collective-permute-start.2 = (bf16[9,96,16]{1,2,0:T(8,128)(2,1)S(1)}, bf16[9,96,16]{1,2,0:T(8,128)(2,1)S(1)}, u32[]{:S(2)}, u32[]{:S(2)}) collective-permute-start(bf16[9,96,16]{1,2,0:T(8,128)(2,1)S(1)} %constant_dynamic-update-slice_fusion.9), channel_id=1, source_target_pairs={{0,504},{1,505},{2,506},{3,507},{4,508},{5,509},{6,510},{7,511},{8... | collective-permute-start | bytes 82952 | tf_op jit(solution)/shard_map/ppermute | solution.py:60
  30.5 9.3 %collective-permute-start.3 = (bf16[9,96,16]{1,2,0:T(8,128)(2,1)S(1)}, bf16[9,96,16]{1,2,0:T(8,128)(2,1)S(1)}, u32[]{:S(2)}, u32[]{:S(2)}) collective-permute-start(bf16[9,96,16]{1,2,0:T(8,128)(2,1)S(1)} %constant_dynamic-update-slice_fusion.9), channel_id=1, source_target_pairs={{0,8},{1,9},{2,10},{3,11},{4,12},{5,13},{6,14},{7,15},{8,0},{9,1},... | collective-permute-start | bytes 82952 | tf_op jit(solution)/shard_map/ppermute | solution.py:59
  42.4 0.8 copy-start.3
  43.7 0.7 copy-start.9
  48.6 6.6 %collective-permute-start.4 = (bf16[9,96,16]{1,2,0:T(8,128)(2,1)S(1)}, bf16[9,96,16]{1,2,0:T(8,128)(2,1)S(1)}, u32[]{:S(2)}, u32[]{:S(2)}) collective-permute-start(bf16[9,96,16]{1,2,0:T(8,128)(2,1)S(1)} %constant_dynamic-update-slice_fusion.27), channel_id=1, source_target_pairs={{0,1},{1,0},{2,3},{3,2},{4,5},{5,4},{6,7},{7,6},{8,9},{9,8},{10,11... | collective-permute-start | bytes 82952 | tf_op jit(solution)/shard_map/ppermute | solution.py:59
  52.1 5.3 %collective-permute-start.5 = (bf16[9,96,16]{1,2,0:T(8,128)(2,1)S(1)}, bf16[9,96,16]{1,2,0:T(8,128)(2,1)S(1)}, u32[]{:S(2)}, u32[]{:S(2)}) collective-permute-start(bf16[9,96,16]{1,2,0:T(8,128)(2,1)S(1)} %constant_dynamic-update-slice_fusion.27), channel_id=1, source_target_pairs={{0,511},{1,2},{2,1},{3,4},{4,3},{5,6},{6,5},{7,8},{8,7},{9,10},{10... | collective-permute-start | bytes 82952 | tf_op jit(solution)/shard_map/ppermute | solution.py:60
  57.5 13.1 %collective-permute-start.6 = (bf16[9,96,16]{1,2,0:T(8,128)(2,1)S(1)}, bf16[9,96,16]{1,2,0:T(8,128)(2,1)S(1)}, u32[]{:S(2)}, u32[]{:S(2)}) collective-permute-start(bf16[9,96,16]{1,2,0:T(8,128)(2,1)S(1)} %constant_dynamic-update-slice_fusion.36), channel_id=1, source_target_pairs={{0,504},{1,505},{2,506},{3,507},{4,508},{5,509},{6,510},{7,511},{8... | collective-permute-start | bytes 82952 | tf_op jit(solution)/shard_map/ppermute | solution.py:60
  66.7 8.9 %collective-permute-start.7 = (bf16[9,96,16]{1,2,0:T(8,128)(2,1)S(1)}, bf16[9,96,16]{1,2,0:T(8,128)(2,1)S(1)}, u32[]{:S(2)}, u32[]{:S(2)}) collective-permute-start(bf16[9,96,16]{1,2,0:T(8,128)(2,1)S(1)} %constant_dynamic-update-slice_fusion.36), channel_id=1, source_target_pairs={{0,8},{1,9},{2,10},{3,11},{4,12},{5,13},{6,14},{7,15},{8,0},{9,1},... | collective-permute-start | bytes 82952 | tf_op jit(solution)/shard_map/ppermute | solution.py:59
  79.7 5.2 %collective-permute-start.8 = (f32[83456]{0:T(1024)S(1)}, f32[83456]{0:T(1024)S(1)}, u32[]{:S(2)}, u32[]{:S(2)}) collective-permute-start(f32[83456]{0:T(1024)S(1)} %slice_select_fusion), channel_id=1, source_target_pairs={{0,1},{1,0},{2,3},{3,2},{4,5},{5,4},{6,7},{7,6},{8,9},{9,8},{10,11... | collective-permute-start | bytes 1001480 | tf_op jit(solution)/shard_map/ppermute | solution.py:23
  85.0 7.4 %collective-permute-start.9 = (f32[41728]{0:T(1024)S(1)}, f32[41728]{0:T(1024)S(1)}, u32[]{:S(2)}, u32[]{:S(2)}) collective-permute-start(f32[41728]{0:T(1024)S(1)} %slice_select_fusion.1), channel_id=1, source_target_pairs={{0,2},{1,3},{2,0},{3,1},{4,6},{5,7},{6,4},{7,5},{8,10},{9,11},{10,... | collective-permute-start | bytes 500744 | tf_op jit(solution)/shard_map/ppermute | solution.py:23
  92.4 7.7 %collective-permute-start.10 = (f32[20864]{0:T(1024)S(1)}, f32[20864]{0:T(1024)S(1)}, u32[]{:S(2)}, u32[]{:S(2)}) collective-permute-start(f32[20864]{0:T(1024)S(1)} %slice_select_fusion.2), channel_id=1, source_target_pairs={{0,4},{1,5},{2,6},{3,7},{4,0},{5,1},{6,2},{7,3},{8,12},{9,13},{10,... | collective-permute-start | bytes 250376 | tf_op jit(solution)/shard_map/ppermute | solution.py:23
  100.1 10.1 %collective-permute-start.11 = (f32[20864]{0:T(1024)S(1)}, f32[20864]{0:T(1024)S(1)}, u32[]{:S(2)}, u32[]{:S(2)}) collective-permute-start(f32[20864]{0:T(1024)S(1)} %select_add_fusion.2), channel_id=1, source_target_pairs={{0,8},{1,9},{2,10},{3,11},{4,12},{5,13},{6,14},{7,15},{8,0},{9,1},... | collective-permute-start | bytes 250376 | tf_op jit(solution)/shard_map/ppermute | solution.py:23
  110.1 5.2 %collective-permute-start.12 = (f32[20864]{0:T(1024)S(1)}, f32[20864]{0:T(1024)S(1)}, u32[]{:S(2)}, u32[]{:S(2)}) collective-permute-start(f32[20864]{0:T(1024)S(1)} %add.346), channel_id=1, source_target_pairs={{0,16},{1,17},{2,18},{3,19},{4,20},{5,21},{6,22},{7,23},{8,24},{9,... | collective-permute-start | bytes 250376 | tf_op jit(solution)/shard_map/ppermute | solution.py:23
  115.4 6.7 %collective-permute-start.13 = (f32[20864]{0:T(1024)S(1)}, f32[20864]{0:T(1024)S(1)}, u32[]{:S(2)}, u32[]{:S(2)}) collective-permute-start(f32[20864]{0:T(1024)S(1)} %add.347), channel_id=1, source_target_pairs={{0,32},{1,33},{2,34},{3,35},{4,36},{5,37},{6,38},{7,39},{8,40},{9,... | collective-permute-start | bytes 250376 | tf_op jit(solution)/shard_map/ppermute | solution.py:23
  122.1 5.5 %collective-permute-start.14 = (f32[20864]{0:T(1024)S(1)}, f32[20864]{0:T(1024)S(1)}, u32[]{:S(2)}, u32[]{:S(2)}) collective-permute-start(f32[20864]{0:T(1024)S(1)} %add.348), channel_id=1, source_target_pairs={{0,64},{1,65},{2,66},{3,67},{4,68},{5,69},{6,70},{7,71},{8,72},{9,... | collective-permute-start | bytes 250376 | tf_op jit(solution)/shard_map/ppermute | solution.py:23
  127.7 6.6 %collective-permute-start.15 = (f32[20864]{0:T(1024)S(1)}, f32[20864]{0:T(1024)S(1)}, u32[]{:S(2)}, u32[]{:S(2)}) collective-permute-start(f32[20864]{0:T(1024)S(1)} %add.349), channel_id=1, source_target_pairs={{0,128},{1,129},{2,130},{3,131},{4,132},{5,133},{6,134},{7,135},{8... | collective-permute-start | bytes 250376 | tf_op jit(solution)/shard_map/ppermute | solution.py:23
  134.2 10.1 %collective-permute-start.16 = (f32[20864]{0:T(1024)S(1)}, f32[20864]{0:T(1024)S(1)}, u32[]{:S(2)}, u32[]{:S(2)}) collective-permute-start(f32[20864]{0:T(1024)S(1)} %add.350), channel_id=1, source_target_pairs={{0,256},{1,257},{2,258},{3,259},{4,260},{5,261},{6,262},{7,263},{8... | collective-permute-start | bytes 250376 | tf_op jit(solution)/shard_map/ppermute | solution.py:23
  144.3 6.1 %collective-permute-start.17 = (f32[20864]{0:T(1024)S(1)}, f32[20864]{0:T(1024)S(1)}, u32[]{:S(2)}, u32[]{:S(2)}) collective-permute-start(f32[20864]{0:T(1024)S(1)} %add.351), channel_id=1, source_target_pairs={{0,4},{1,5},{2,6},{3,7},{4,0},{5,1},{6,2},{7,3},{8,12},{9,13},{10,... | collective-permute-start | bytes 250376 | tf_op jit(solution)/shard_map/ppermute | solution.py:23
  150.5 7.3 %collective-permute-start.18 = (f32[41728]{0:T(1024)S(1)}, f32[41728]{0:T(1024)S(1)}, u32[]{:S(2)}, u32[]{:S(2)}) collective-permute-start(f32[41728]{0:T(1024)S(1)} %maximum_select_fusion.2), channel_id=1, source_target_pairs={{0,2},{1,3},{2,0},{3,1},{4,6},{5,7},{6,4},{7,5},{8,10},{9,11},{10,... | collective-permute-start | bytes 500744 | tf_op jit(solution)/shard_map/ppermute | solution.py:23
  157.8 15.0 %collective-permute-start.19 = (f32[83456]{0:T(1024)S(1)}, f32[83456]{0:T(1024)S(1)}, u32[]{:S(2)}, u32[]{:S(2)}) collective-permute-start(f32[83456]{0:T(1024)S(1)} %maximum_select_fusion.1), channel_id=1, source_target_pairs={{0,1},{1,0},{2,3},{3,2},{4,5},{5,4},{6,7},{7,6},{8,9},{9,8},{10,11... | collective-permute-start | bytes 1001480 | tf_op jit(solution)/shard_map/ppermute | solution.py:23
